TPU v7x, 256 devices: a whole 4x4x8 slice. The times are simulated.
256 devices in a mesh: dp: 16 (over y, z_hi, core), tensor: 16 (over z_lo, x).
Axes of the slice: x: 4, y: 4, z: 8 (z_hi: 2, z_lo: 4; z = z_hi * 4 + z_lo), core: 2. Of those that a mesh axis runs over, the one named last changes fastest.
Arguments:
- token_ids: int32 [4096], P('dp'), may hold values from 0 to 128255
- attn_heads: bfloat16 [4096, 8192], P('dp', 'tensor'), may hold values from -6 to 6
- out_proj: bfloat16 [8192, 8192], P('tensor'), may hold values from -0.0625 to 0.0625
- residual: bfloat16 [4096, 8192], P(('dp', 'tensor')), may hold values from -6 to 6
- norm_gain: float32 [8192], replicated, may hold values from 0.5 to 1.5
- twist_in: bfloat16 [8192, 8192], P('dp', 'tensor'), may hold values from -0.0625 to 0.0625
- twist_out: float32 [8192], P('tensor'), may hold values from -0.26516503 to 0.26516503
- token_bias: float32 [128256], replicated, may hold values from -4 to 262
- toxicity: int32 [16], P('dp'), may hold values from 1 to 4
- prompt_len: int32 [16], P('dp'), may hold values from 1 to 128
Outputs:
- twist_vals: float32 [4096], P('dp')
- grad_in: float32 [8192, 8192], P('dp', 'tensor')
- grad_out: float32 [8192], P('tensor')
- grad_bias: float32 [128256], P('dp')
All inputs are finite; a program needn't handle non-finite values.
Results may differ from a plain program's by a relative error of at most 0.033.
Values may be sent and summed in bfloat16 or wider, within the bound.
No kernel may reach another device: no remote copies, remote signals or barrier semaphores. Data moves between devices by JAX's collectives and lax.ppermute only.
A program may use at most 128 MiB of HBM per device.

v0:
```python
import jax
import jax.numpy as jnp
from jax import lax
from jax.sharding import PartitionSpec as P


def merged_2(value, axis, join):
    pieces = jax.tree.map(lambda part: lax.all_gather(part, axis), value)
    head = jax.tree.map(lambda part: part[0], pieces)
    tail = jax.tree.map(lambda part: part[1:], pieces)
    total, _ = lax.scan(lambda total, share: (join(total, share), None), head, tail)
    return total


def normalize(hidden, norm_gain):
    values = hidden.astype(jnp.float32)
    scaled = lax.rsqrt(jnp.mean(values * values, axis=-1, keepdims=True) + 1e-05)
    return (values * scaled * norm_gain[None, :]).astype(jnp.bfloat16)


def combine(earlier, later):
    high_one, sum_one, lab_one = earlier
    high_two, sum_two, lab_two = later
    highest = jnp.maximum(high_one, high_two)
    merged = sum_one * jnp.exp(high_one - highest) + sum_two * jnp.exp(high_two - highest)
    return (highest, merged, lab_one + lab_two)


def local(
    token_ids,
    attn_heads,
    out_proj,
    residual,
    norm_gain,
    twist_in,
    twist_out,
    token_bias,
    toxicity,
    prompt_len,
):
    seq_len = attn_heads.shape[0]
    vocab_size = token_bias.shape[0]
    partial_sum = jnp.dot(attn_heads, out_proj, preferred_element_type=jnp.float32)
    summed = lax.psum(partial_sum.astype(jnp.bfloat16), "tensor").astype(jnp.float32)
    resid_all = lax.all_gather(residual, "tensor", axis=0, tiled=True)
    hidden = (resid_all.astype(jnp.float32) + summed).astype(jnp.bfloat16)
    normed = normalize(hidden, norm_gain)
    columns = normed
    pre_act = jnp.dot(
        columns,
        lax.all_gather(twist_in, "dp", axis=0, tiled=True),
        preferred_element_type=jnp.float32,
    )
    active = jax.nn.silu(pre_act)
    partial_psi = jnp.dot(active, twist_out, precision=lax.Precision.HIGHEST)
    twist_vals = lax.psum(partial_psi, "tensor") + token_bias[token_ids]
    live = jnp.arange(seq_len) >= prompt_len[0]
    live_float = live.astype(jnp.float32)
    levels = toxicity[0].astype(jnp.float32) * live_float
    local_high = jnp.where(live, twist_vals, -1e30)
    highest, totals, lab_sum = merged_2((local_high, live_float, levels), "dp", combine)
    expo = jnp.where(live, jnp.exp(jnp.where(live, twist_vals - highest, -80.0)), 0.0)
    weights = (expo / jnp.maximum(totals, 1.0) - levels / jnp.maximum(lab_sum, 1.0)) / seq_len
    grad_out = lax.psum(jnp.dot(weights, active, precision=lax.Precision.HIGHEST), "dp")
    local_bias = jnp.zeros((vocab_size,), jnp.float32).at[token_ids].add(weights)
    grad_bias = lax.psum_scatter(
        local_bias.astype(jnp.bfloat16), "dp", scatter_dimension=0, tiled=True
    ).astype(jnp.float32)
    sigma = jax.nn.sigmoid(pre_act)
    d_pre = (
        weights[:, None] * twist_out[None, :] * sigma * (1.0 + pre_act * (1.0 - sigma))
    ).astype(jnp.bfloat16)
    contract = (((0,), (0,)), ((), ()))
    columns = normed
    grad_in = lax.psum_scatter(
        lax.dot_general(columns, d_pre, contract, preferred_element_type=jnp.float32).astype(
            jnp.bfloat16
        ),
        "dp",
        scatter_dimension=0,
        tiled=True,
    ).astype(jnp.float32)
    return (twist_vals, grad_in, grad_out, grad_bias)


def solution(mesh):
    placed = (
        P("dp"),
        P("dp", "tensor"),
        P("tensor", None),
        P(("dp", "tensor"), None),
        P(),
        P("dp", "tensor"),
        P("tensor"),
        P(),
        P("dp"),
        P("dp"),
    )
    return jax.shard_map(
        local,
        mesh=mesh,
        in_specs=placed,
        out_specs=(P("dp"), P("dp", "tensor"), P("tensor"), P("dp")),
        check_vma=False,
    )
```

profile of v0, /device:TPU:2, one launch (start us, length us, event | category | flops | bytes accessed | tf_op | source)
XLA Modules:
  0.0 797.6 jit_solution(13153336247750633944)
XLA Ops:
  7.2 0.0 copy-start
  7.2 0.0 copy-start.2
  7.2 0.0 all-reduce.4.cloned.1.call-start
  7.2 7.8 convolution_convert_fusion.1
  15.1 0.0 copy-start.3
  15.1 0.0 all-reduce.4.cloned.1.call-update
  15.1 0.0 all-gather.7.cloned.1.call-start
  15.1 0.7 all-gather.7.cloned.1.call-update
  15.8 0.0 all-gather.9.cloned.1.call-start
  15.9 0.7 all-gather.9.cloned.1.call-update
  16.6 0.0 all-reduce.6.cloned.1.call-start
  17.9 33.4 %all-gather.3 = f32[16,1,256]{2,1,0:T(1,128)S(1)} all-gather(f32[1,1,256]{2,1,0:T(1,128)S(1)} %fusion.13), channel_id=1, replica_groups=mesh['dp'=16,'tensor'=16] {'dp'}, dimensions={0}, use_global_device_ids=true | all-gather | bytes 17408 | tf_op jit(solution)/shard_map/all_gather | solution.py:8
  51.4 24.1 %all-gather.2 = f32[16,1,256]{2,1,0:T(1,128)S(1)} all-gather(f32[1,1,256]{2,1,0:T(1,128)S(1)} %fusion.14), channel_id=1, replica_groups=mesh['dp'=16,'tensor'=16] {'dp'}, dimensions={0}, use_global_device_ids=true | all-gather | bytes 17408 | tf_op jit(solution)/shard_map/all_gather | solution.py:8
  75.5 0.0 copy-done.2
  75.5 0.0 copy-done
  75.5 1.7 gather_fusion
  77.3 118.5 %all-reduce.4.cloned.1.call-done = bf16[256,8192]{1,0:T(8,128)(2,1)} async-done(((bf16[256,8192]{1,0:T(8,128)(2,1)}), bf16[256,8192]{1,0:T(8,128)(2,1)}) %all-reduce.4.cloned.1.call-update) | async-done | bytes 4194320 | tf_op jit(solution)/shard_map/psum | solution.py:44
  195.8 87.7 %all-gather.7.cloned.1.call-done = bf16[256,8192]{1,0:T(8,128)(2,1)} async-done(((bf16[16,8192]{1,0:T(8,128)(2,1)}), bf16[256,8192]{1,0:T(8,128)(2,1)}) %all-gather.7.cloned.1.call-update) | async-done | bytes 4194320 | tf_op jit(solution)/shard_map/all_gather | solution.py:45
  283.5 4.9 fusion
  288.4 0.0 copy-start.4
  288.5 104.6 %all-gather.9.cloned.1.call-done = bf16[8192,512]{1,0:T(8,128)(2,1)} async-done(((bf16[512,512]{1,0:T(8,128)(2,1)}), bf16[8192,512]{1,0:T(8,128)(2,1)}) %all-gather.9.cloned.1.call-update) | async-done | bytes 8388624 | tf_op jit(solution)/shard_map/all_gather | solution.py:51
  393.1 0.0 copy-done.3
  393.1 8.2 %fusion.20 = f32[256,512]{1,0:T(8,128)S(1)} fusion(bf16[8192,512]{1,0:T(8,128)(2,1)} %all-gather.9.cloned.1.call-done, f32[8192]{0:T(1024)S(1)} %copy-done.3, f32[256]{0:T(256)S(1)} %add_rsqrt_fusion, bf16[256,8192]{1,0:T(8,128)(2,1)} %all-reduce.4.cloned.1.call-done, bf16[256,8192]{1,0:T(8,128)(2,1)} %all-gather.7.cloned.1.call-done), kind=kOutput, calls=%fused_computation.41 | convolution fusion | flops 2164260864 | bytes 17335296 | tf_op jit(solution)/shard_map/dot_general | solution.py:49
  401.3 0.0 copy-done.4
  401.4 0.6 fusion.11
  402.0 38.4 %psum.22 = f32[256]{0:T(256)S(1)} all-reduce(f32[256]{0:T(256)S(1)} %bitcast.53), channel_id=1, replica_groups=mesh['dp'=16,'tensor'=16] {'tensor'}, use_global_device_ids=true, to_apply=%region_2.3 | all-reduce | flops 256 | bytes 2048 | tf_op jit(solution)/shard_map/psum | solution.py:56
  440.3 0.0 copy-start.1
  440.3 23.8 %all-gather.1 = f32[16,1,256]{2,1,0:T(1,128)S(1)} all-gather(f32[1,1,256]{2,1,0:T(1,128)S(1)} %bitcast.51), channel_id=2, replica_groups=mesh['dp'=16,'tensor'=16] {'dp'}, dimensions={0}, use_global_device_ids=true | all-gather | bytes 17408 | tf_op jit(solution)/shard_map/all_gather | solution.py:8
  464.1 1.3 while.14
  465.4 2.1 scatter_custom_fusion
  467.5 0.7 convert_element_type.61
  468.2 0.0 all-reduce.6.cloned.1.call-update
  468.3 0.2 reduce-scatter.2.cloned.1.call-start
  468.5 10.1 %convolution_convert_fusion = bf16[8192,512]{1,0:T(8,128)(2,1)} fusion(f32[256,512]{1,0:T(8,128)S(1)} %fusion.20, f32[512]{0:T(512)S(1)} %copy-done.4, f32[256]{0:T(256)S(1)} %subtract_multiply_fusion, f32[8192]{0:T(1024)S(1)} %copy-done.3, f32[256]{0:T(256)S(1)} %add_rsqrt_fusion, bf16[256,8192]{1,0:T(8,128)(2,1)} %all-reduce.4.cloned.1.call-done, ...), kind=kOutput, calls=%fused_computation.6 | convolution fusion | flops 2169765888 | bytes 17338368 | tf_op jit(solution)/shard_map/dot_general | solution.py:76
  478.6 0.0 copy-done.1
  478.6 0.0 copy-start.5
  478.6 0.0 reduce-scatter.2.cloned.1.call-update
  478.6 0.6 copy-done.5
  479.2 0.6 dynamic-slice
  480.5 0.5 fusion.9
  480.9 49.3 %psum.23 = f32[512]{0:T(512)} all-reduce(f32[512]{0:T(512)S(1)} %bitcast.52), channel_id=1, replica_groups=mesh['dp'=16,'tensor'=16] {'dp'}, use_global_device_ids=true, to_apply=%region_6.7 | all-reduce | flops 512 | bytes 4096 | tf_op jit(solution)/shard_map/psum | solution.py:64
  530.2 113.1 %all-reduce.6.cloned.1.call-done = bf16[128256]{0:T(1024)(128)(2,1)} async-done(((bf16[128256]{0:T(1024)(128)(2,1)}), bf16[128256]{0:T(1024)(128)(2,1)}) %all-reduce.6.cloned.1.call-update) | async-done | bytes 256528
  643.3 1.4 dynamic-slice_convert_fusion
  644.7 144.2 %reduce-scatter.2.cloned.1.call-done = bf16[512,512]{1,0:T(8,128)(2,1)} async-done(((bf16[8192,512]{1,0:T(8,128)(2,1)}), bf16[512,512]{1,0:T(8,128)(2,1)}) %reduce-scatter.2.cloned.1.call-update) | async-done | bytes 524304 | tf_op jit(solution)/shard_map/reduce_scatter | solution.py:75
  788.9 2.1 convert_element_type.60
  (76 shorter events, 0.9 us)
Async XLA Ops:
  7.2 68.4 %copy-start = (f32[128256]{0:T(1024)S(1)}, f32[128256]{0:T(1024)}, u32[]{:S(2)}) copy-start(f32[128256]{0:T(1024)} %param.19) | copy-start | bytes 1539076
  7.2 68.3 %copy-start.2 = (s32[256]{0:T(256)S(1)}, s32[256]{0:T(256)}, u32[]{:S(2)}) copy-start(s32[256]{0:T(256)} %param.12) | copy-start | bytes 3076
  7.2 188.6 %all-reduce.4.cloned.1.call-start = ((), (), s32[]{:S(2)}) async-start(), calls=%async_computation.2 | async-start | bytes 8388608 | tf_op jit(solution)/shard_map/psum | solution.py:44
  15.1 378.0 %copy-start.3 = (f32[8192]{0:T(1024)S(1)}, f32[8192]{0:T(1024)}, u32[]{:S(2)}) copy-start(f32[8192]{0:T(1024)} %param.16) | copy-start | bytes 98308
  15.1 268.4 %all-gather.7.cloned.1.call-start = ((), (), s32[]{:S(2)}) async-start(), calls=%async_computation.1 | async-start | bytes 4456448 | tf_op jit(solution)/shard_map/all_gather | solution.py:45
  15.8 377.3 %all-gather.9.cloned.1.call-start = ((), (), s32[]{:S(2)}) async-start(), calls=%async_computation.3 | async-start | bytes 8912896 | tf_op jit(solution)/shard_map/all_gather | solution.py:51
  16.6 626.7 %all-reduce.6.cloned.1.call-start = ((), (), s32[]{:S(2)}) async-start(), calls=%async_computation.5 | async-start | bytes 516096
  288.4 112.9 %copy-start.4 = (f32[512]{0:T(512)S(1)}, f32[512]{0:T(512)}, u32[]{:S(2)}) copy-start(f32[512]{0:T(512)} %param.18) | copy-start | bytes 6148
  440.3 38.2 %copy-start.1 = (f32[256]{0:T(256)}, f32[256]{0:T(256)S(1)}, u32[]{:S(2)}) copy-start(f32[256]{0:T(256)S(1)} %get-tuple-element.63) | copy-start | bytes 3076
  468.3 320.7 %reduce-scatter.2.cloned.1.call-start = ((), (), s32[]{:S(2)}) async-start(), calls=%async_computation.4 | async-start | bytes 8912896 | tf_op jit(solution)/shard_map/reduce_scatter | solution.py:75
  478.6 0.7 copy-start.5
Sparse Core Ops, SparseCore 0:
  15.2 180.5 all-reduce.3
  197.6 85.8 all-gather.6
  286.2 106.8 all-gather.8
  468.4 174.8 all-reduce.5
  647.8 141.1 reduce-scatter.1
where the time goes:
time: 798 us
  waiting for transfers between devices  570 us (71%)
  blocking collectives  169 us (21%)
  matrix products  27.2 us (3%)
  between operations  15.9 us (2%)
  other arithmetic  11.8 us (1%)
    reduce_scatter x1, waiting for transfers between devices, local(): lax.psum_scatter(lax.dot_general(columns, d_pre, contract, preferred_elem...  144 us
    psum x1, waiting for transfers between devices, local(): lax.psum(partial_sum.astype(jnp.bfloat16), 'tensor').astype(jnp.float32)  119 us
    unnamed x6, waiting for transfers between devices  115 us
    all_gather x1, waiting for transfers between devices, local(): lax.all_gather(twist_in, 'dp', axis=0, tiled=True)  105 us
    all_gather x1, waiting for transfers between devices, local(): resid_all = lax.all_gather(residual, 'tensor', axis=0, tiled=True)  87.7 us
    all_gather x3, blocking collectives, merged_2(): pieces = jax.tree.map(lambda part: lax.all_gather(part, axis), value)  81.4 us
    psum x1, blocking collectives, local(): lax.psum(jnp.dot(weights, active, precision=lax.Precision.HIGHEST), 'dp')  49.3 us
    psum x1, blocking collectives, local(): twist_vals = lax.psum(partial_psi, 'tensor') + token_bias[token_ids]  38.4 us
  transfers between devices with their start and end apart: 5, of which 5 were waited for; matrix products, arithmetic and copies ran while one was open for 2% of the time, Pallas kernels for 0%

commit v1 on v0

v1 whole, which is shorter than its diff:
```python
import jax
import jax.numpy as jnp
from jax import lax
from jax.sharding import PartitionSpec as P


def normalize(hidden, norm_gain):
    values = hidden.astype(jnp.float32)
    scaled = lax.rsqrt(jnp.mean(values * values, axis=-1, keepdims=True) + 1e-05)
    return (values * scaled * norm_gain[None, :]).astype(jnp.bfloat16)


def local(
    token_ids,
    attn_heads,
    out_proj,
    residual,
    norm_gain,
    twist_in,
    twist_out,
    token_bias,
    toxicity,
    prompt_len,
):
    seq_len = attn_heads.shape[0]
    vocab_size = token_bias.shape[0]
    n_dp = lax.axis_size("dp")
    r = lax.axis_index("dp")

    ints = jnp.concatenate([token_ids, prompt_len, toxicity])
    ints_all = lax.all_gather(ints, "dp", axis=0)
    ids_all = ints_all[:, :seq_len]
    plen_all = ints_all[:, seq_len]
    tox_all = ints_all[:, seq_len + 1]

    twist_full = lax.all_gather(twist_in, "dp", axis=0, tiled=True)

    partial_sum = jnp.dot(attn_heads, out_proj, preferred_element_type=jnp.float32)
    summed = lax.psum_scatter(
        partial_sum.astype(jnp.bfloat16), "tensor", scatter_dimension=0, tiled=True
    ).astype(jnp.float32)
    hidden = (residual.astype(jnp.float32) + summed).astype(jnp.bfloat16)
    normed_rows = normalize(hidden, norm_gain)
    normed = lax.all_gather(normed_rows, "tensor", axis=0, tiled=True)

    pre_act = jnp.dot(normed, twist_full, preferred_element_type=jnp.float32)
    active = jax.nn.silu(pre_act)
    partial_psi = jnp.dot(active, twist_out, precision=lax.Precision.HIGHEST)
    slot = (jnp.arange(n_dp) == r).astype(jnp.float32)
    psi_all = lax.psum(slot[:, None] * partial_psi[None, :], ("dp", "tensor"))
    grid = psi_all + token_bias[ids_all]

    live = jnp.arange(seq_len)[None, :] >= plen_all[:, None]
    levels = tox_all.astype(jnp.float32)[:, None] * live.astype(jnp.float32)
    highest = jnp.max(jnp.where(live, grid, -1e30), axis=0)
    expo = jnp.where(live, jnp.exp(jnp.where(live, grid - highest[None, :], -80.0)), 0.0)
    totals = jnp.sum(expo, axis=0)
    lab_sum = jnp.sum(levels, axis=0)
    weights_all = (
        expo / jnp.maximum(totals, 1.0)[None, :] - levels / jnp.maximum(lab_sum, 1.0)[None, :]
    ) / seq_len

    twist_vals = lax.dynamic_index_in_dim(grid, r, axis=0, keepdims=False)
    weights = lax.dynamic_index_in_dim(weights_all, r, axis=0, keepdims=False)

    grad_out = lax.psum(jnp.dot(weights, active, precision=lax.Precision.HIGHEST), "dp")

    slice_len = vocab_size // n_dp
    idx = ids_all.reshape(-1) - r * slice_len
    idx = jnp.where((idx >= 0) & (idx < slice_len), idx, slice_len)
    grad_bias = jnp.zeros((slice_len,), jnp.float32).at[idx].add(
        weights_all.reshape(-1), mode="drop"
    )

    sigma = jax.nn.sigmoid(pre_act)
    d_pre = (
        weights[:, None] * twist_out[None, :] * sigma * (1.0 + pre_act * (1.0 - sigma))
    ).astype(jnp.bfloat16)
    contract = (((0,), (0,)), ((), ()))
    grad_in = lax.psum_scatter(
        lax.dot_general(normed, d_pre, contract, preferred_element_type=jnp.float32).astype(
            jnp.bfloat16
        ),
        "dp",
        scatter_dimension=0,
        tiled=True,
    ).astype(jnp.float32)
    return (twist_vals, grad_in, grad_out, grad_bias)


def solution(mesh):
    placed = (
        P("dp"),
        P("dp", "tensor"),
        P("tensor", None),
        P(("dp", "tensor"), None),
        P(),
        P("dp", "tensor"),
        P("tensor"),
        P(),
        P("dp"),
        P("dp"),
    )
    return jax.shard_map(
        local,
        mesh=mesh,
        in_specs=placed,
        out_specs=(P("dp"), P("dp", "tensor"), P("tensor"), P("dp")),
        check_vma=False,
    )
```

time: 798 us -> 513 us (0.64)
  waiting for transfers between devices: 570 us -> 199 us
  blocking collectives: 169 us -> 213 us
  other arithmetic: 11.8 us -> 34 us
  local copies, waits for them, and re-layouts: 3.33 us -> 24.5 us
    all_gather x2, waiting for transfers between devices: 192 us -> 0.04 us  [the longest x1 0.03 us: local(): twist_full = lax.all_gather(twist_in, 'dp', axis=0, tiled=True)]
    psum x1 -> x0, waiting for transfers between devices: 119 us -> none  [local(): lax.psum(partial_sum.astype(jnp.bfloat16), 'tensor').astype(jnp.float32)]
    unnamed x6 -> x4, waiting for transfers between devices: 115 us -> 0.57 us
    unnamed x0 -> x1, blocking collectives: none -> 84.1 us
    all_gather x3 -> x0, blocking collectives: 81.4 us -> none  [merged_2(): pieces = jax.tree.map(lambda part: lax.all_gather(part, axis), value)]
    reduce_scatter x1 -> x2, waiting for transfers between devices: 144 us -> 198 us  [the longest x1 143 us: local(): lax.psum_scatter(partial_sum.astype(jnp.bfloat16), 'tensor', scatter_dime...]
    psum x1, blocking collectives: 38.4 us -> 76.4 us  [local(): psi_all = lax.psum(slot[:, None] * partial_psi[None, :], ('dp', 'tensor'))]
    scatter-add x1, other arithmetic: 2.07 us -> 28.1 us  [local(): jnp.zeros((slice_len,), jnp.float32).at[idx]]
  transfers between devices with their start and end apart: 5 -> 4, of which waited for: 5 -> 2; matrix products, arithmetic and copies ran while one was open for 2% -> 11% of each run, Pallas kernels for 0% -> 0%
where the time goes in v1:
time: 513 us
  blocking collectives  213 us (42%)
  waiting for transfers between devices  199 us (39%)
  other arithmetic  34 us (7%)
  local copies, waits for them, and re-layouts  24.5 us (5%)
  matrix products  23.9 us (5%)
  between operations  17.8 us (3%)
    reduce_scatter x1, waiting for transfers between devices, local(): lax.psum_scatter(partial_sum.astype(jnp.bfloat16), 'tensor', scatter_dime...  143 us
    unnamed x1, blocking collectives  84.1 us
    psum x1, blocking collectives, local(): psi_all = lax.psum(slot[:, None] * partial_psi[None, :], ('dp', 'tensor'))  76.4 us
    reduce_scatter x1, waiting for transfers between devices, local(): lax.psum_scatter(lax.dot_general(normed, d_pre, contract, preferred_eleme...  55.3 us
    psum x1, blocking collectives, local(): lax.psum(jnp.dot(weights, active, precision=lax.Precision.HIGHEST), 'dp')  52.9 us
    scatter-add x1, other arithmetic, local(): jnp.zeros((slice_len,), jnp.float32).at[idx]  28.1 us
    gather x2, local copies, waits for them, and re-layouts, local(): grid = psi_all + token_bias[ids_all]  23 us
  transfers between devices with their start and end apart: 4, of which 2 were waited for; matrix products, arithmetic and copies ran while one was open for 11% of the time, Pallas kernels for 0%

profile of v1, /device:TPU:2, one launch (start us, length us, event | category | flops | bytes accessed | tf_op | source)
XLA Modules:
  0.0 512.8 jit_solution(1004239497600625176)
XLA Ops:
  8.0 0.0 copy-start
  8.0 0.0 copy-start.5
  8.0 0.0 copy-start.1
  8.0 0.0 copy-start.2
  8.0 0.0 copy-start.3
  8.1 0.0 reduce-scatter.3.cloned.1.call-start
  8.1 7.9 %convolution_convert_fusion.1 = bf16[256,8192]{1,0:T(8,128)(2,1)} fusion(bf16[256,512]{1,0:T(8,128)(2,1)} %param.11, bf16[512,8192]{1,0:T(8,128)(2,1)} %param.12), kind=kOutput, calls=%fused_computation.3 | convolution fusion | flops 2149580800 | bytes 12845056 | tf_op jit(solution)/shard_map/dot_general | solution.py:38
  16.0 0.0 reduce-scatter.3.cloned.1.call-update
  16.0 0.0 all-gather.6.cloned.1.call-start
  16.0 0.5 all-gather.6.cloned.1.call-update
  16.6 0.0 all-gather.4.cloned.1.call-start
  16.6 143.1 %reduce-scatter.3.cloned.1.call-done = bf16[16,8192]{1,0:T(8,128)(2,1)} async-done(((bf16[256,8192]{1,0:T(8,128)(2,1)}), bf16[16,8192]{1,0:T(8,128)(2,1)}) %reduce-scatter.3.cloned.1.call-update) | async-done | bytes 262160 | tf_op jit(solution)/shard_map/reduce_scatter | solution.py:39
  159.8 0.0 copy-done.1
  159.8 1.2 fusion
  160.9 0.0 copy-done.2
  160.9 1.8 fusion.2
  162.7 0.0 all-gather.4.cloned.1.call-update
  162.7 0.0 reduce-scatter.5.cloned.1.call-start
  164.1 0.0 copy-done.5
  164.1 0.6 dynamic-slice
  165.4 0.0 copy-done.3
  165.4 0.2 add_dynamic-update-slice_fusion
  165.6 84.1 %all-reduce = s32[4128]{0:T(1024)S(1)} all-reduce(s32[4128]{0:T(1024)S(1)} %add_dynamic-update-slice_fusion), channel_id=2, replica_groups=mesh['dp'=16,'tensor'=16] {'dp'}, use_global_device_ids=true, to_apply=%add | all-reduce | flops 4128 | bytes 33024
  249.7 0.1 reshape.87
  249.9 0.0 copy-done
  249.9 23.0 %gather_fusion = f32[4096]{0:T(1024)S(1)} fusion(f32[128256]{0:T(1024)S(1)} %copy-done, s32[4096]{0:T(1024)S(1)} %broadcast_clamp_fusion), kind=kCustom, calls=%fused_computation | custom fusion | bytes 49152 | tf_op jit(solution)/shard_map/gather | solution.py:51
  272.9 0.1 slice_reduce_fusion
  273.0 0.2 fusion.17
  273.2 0.0 copy-start.4
  273.2 0.0 all-gather.6.cloned.1.call-done
  273.3 0.0 all-gather.4.cloned.1.call-done
  273.3 7.0 %fusion.22 = f32[256,512]{1,0:T(8,128)S(1)} fusion(bf16[256,8192]{1,0:T(8,128)(2,1)} %all-gather.4.cloned.1.call-done, bf16[8192,512]{1,0:T(8,128)(2,1)} %all-gather.6.cloned.1.call-done), kind=kOutput, calls=%fused_computation.49 | convolution fusion | flops 2147483648 | bytes 13107200 | tf_op jit(solution)/shard_map/dot_general | solution.py:46
  280.3 0.0 copy-done.4
  280.3 0.6 fusion.9
  280.9 0.1 broadcast_multiply_fusion
  281.0 76.4 %psum.14 = f32[16,256]{1,0:T(8,128)S(1)} all-reduce(f32[16,256]{1,0:T(8,128)S(1)} %broadcast_multiply_fusion), channel_id=1, replica_groups=mesh['dp'=16,'tensor'=16] {'dp','tensor'}, use_global_device_ids=true, to_apply=%region_2.3 | all-reduce | flops 4096 | bytes 32768 | tf_op jit(solution)/shard_map/psum | solution.py:50
  357.4 0.1 select_reduce_fusion.1
  357.5 0.1 fusion.16
  357.6 0.1 fusion.12
  357.7 8.0 %convolution_convert_fusion = bf16[8192,512]{1,0:T(8,128)(2,1)} fusion(bf16[256,8192]{1,0:T(8,128)(2,1)} %all-gather.4.cloned.1.call-done, f32[256,512]{1,0:T(8,128)S(1)} %fusion.22, f32[512]{0:T(512)S(1)} %copy-done.4, f32[256]{0:T(256)S(1)} %bitcast.33), kind=kOutput, calls=%fused_computation.2 | convolution fusion | flops 2152988672 | bytes 13110272 | tf_op jit(solution)/shard_map/dot_general | solution.py:81
  365.6 0.0 reduce-scatter.5.cloned.1.call-update
  365.7 0.1 fusion.29
  365.8 28.1 %scatter_custom_fusion = f32[8016]{0:T(1024)} fusion(s32[4096]{0:T(1024)S(1)} %bitcast.29, f32[4096]{0:T(1024)S(1)} %bitcast.30, f32[]{:T(128)} %constant.16.clone.1), kind=kCustom, calls=%fused_computation.27 | custom fusion | flops 4096 | bytes 32068 | tf_op jit(solution)/shard_map/scatter-add | solution.py:71
  393.9 0.5 fusion.7
  394.4 52.9 %psum.15 = f32[512]{0:T(512)} all-reduce(f32[512]{0:T(512)S(1)} %bitcast.31), channel_id=1, replica_groups=mesh['dp'=16,'tensor'=16] {'dp'}, use_global_device_ids=true, to_apply=%region_7.8 | all-reduce | flops 512 | bytes 4096 | tf_op jit(solution)/shard_map/psum | solution.py:66
  447.3 0.6 constant_dynamic-slice_fusion.1
  447.9 55.3 %reduce-scatter.5.cloned.1.call-done = bf16[512,512]{1,0:T(8,128)(2,1)} async-done(((bf16[8192,512]{1,0:T(8,128)(2,1)}), bf16[512,512]{1,0:T(8,128)(2,1)}) %reduce-scatter.5.cloned.1.call-update) | async-done | bytes 524304 | tf_op jit(solution)/shard_map/reduce_scatter | solution.py:80
  503.1 2.1 convert_element_type.49
  (12 shorter events, 0.1 us)
Async XLA Ops:
  8.0 241.9 %copy-start = (f32[128256]{0:T(1024)S(1)}, f32[128256]{0:T(1024)}, u32[]{:S(2)}) copy-start(f32[128256]{0:T(1024)} %param.17) | copy-start | bytes 1539076
  8.0 156.1 %copy-start.5 = (u32[256]{0:T(256)S(1)}, u32[256]{0:T(256)}, u32[]{:S(2)}) copy-start(u32[256]{0:T(256)} %constant.48) | copy-start | bytes 3076
  8.0 151.7 %copy-start.1 = (bf16[16,8192]{1,0:T(8,128)(2,1)S(1)}, bf16[16,8192]{1,0:T(8,128)(2,1)}, u32[]{:S(2)}) copy-start(bf16[16,8192]{1,0:T(8,128)(2,1)} %param.13) | copy-start | bytes 786436
  8.0 152.9 %copy-start.2 = (f32[8192]{0:T(1024)S(1)}, f32[8192]{0:T(1024)}, u32[]{:S(2)}) copy-start(f32[8192]{0:T(1024)} %param.14) | copy-start | bytes 98308
  8.0 157.3 %copy-start.3 = (s32[256]{0:T(256)S(1)}, s32[256]{0:T(256)}, u32[]{:S(2)}) copy-start(s32[256]{0:T(256)} %param.10) | copy-start | bytes 3076
  8.1 151.7 %reduce-scatter.3.cloned.1.call-start = ((), (), s32[]{:S(2)}) async-start(), calls=%async_computation.2 | async-start | bytes 4456448 | tf_op jit(solution)/shard_map/reduce_scatter | solution.py:39
  16.0 257.3 %all-gather.6.cloned.1.call-start = ((), (), s32[]{:S(2)}) async-start(), calls=%async_computation.4 | async-start | bytes 8912896 | tf_op jit(solution)/shard_map/all_gather | solution.py:36
  16.6 256.7 %all-gather.4.cloned.1.call-start = ((), (), s32[]{:S(2)}) async-start(), calls=%async_computation.3 | async-start | bytes 4456448 | tf_op jit(solution)/shard_map/all_gather | solution.py:44
  162.7 340.4 %reduce-scatter.5.cloned.1.call-start = ((), (), s32[]{:S(2)}) async-start(), calls=%async_computation.5 | async-start | bytes 8912896 | tf_op jit(solution)/shard_map/reduce_scatter | solution.py:80
  273.2 7.1 %copy-start.4 = (f32[512]{0:T(512)S(1)}, f32[512]{0:T(512)}, u32[]{:S(2)}) copy-start(f32[512]{0:T(512)} %param.16) | copy-start | bytes 6148
Sparse Core Ops, SparseCore 0:
  16.1 143.5 reduce-scatter.2
Sparse Core Ops, SparseCore 1:
  19.2 114.6 all-gather.5
  162.8 89.8 all-gather.3
  365.8 137.3 reduce-scatter.4

commit v2 on v1

--- a/solution.py
+++ b/solution.py
@@ -2,6 +2,8 @@
 import jax.numpy as jnp
 from jax import lax
 from jax.sharding import PartitionSpec as P
+
+SPLITS = 1
 
 
 def normalize(hidden, norm_gain):
@@ -23,35 +25,50 @@
     prompt_len,
 ):
     seq_len = attn_heads.shape[0]
+    width = out_proj.shape[1]
     vocab_size = token_bias.shape[0]
     n_dp = lax.axis_size("dp")
     r = lax.axis_index("dp")
-
-    ints = jnp.concatenate([token_ids, prompt_len, toxicity])
-    ints_all = lax.all_gather(ints, "dp", axis=0)
-    ids_all = ints_all[:, :seq_len]
-    plen_all = ints_all[:, seq_len]
-    tox_all = ints_all[:, seq_len + 1]
+    j = lax.axis_index("tensor")
+    rows = residual.shape[0]
 
     twist_full = lax.all_gather(twist_in, "dp", axis=0, tiled=True)
 
+    resid_pad = lax.dynamic_update_slice(
+        jnp.zeros((seq_len, width), residual.dtype), residual, (j * rows, 0)
+    )
     partial_sum = jnp.dot(attn_heads, out_proj, preferred_element_type=jnp.float32)
-    summed = lax.psum_scatter(
-        partial_sum.astype(jnp.bfloat16), "tensor", scatter_dimension=0, tiled=True
-    ).astype(jnp.float32)
-    hidden = (residual.astype(jnp.float32) + summed).astype(jnp.bfloat16)
-    normed_rows = normalize(hidden, norm_gain)
-    normed = lax.all_gather(normed_rows, "tensor", axis=0, tiled=True)
+    partial_sum = (partial_sum + resid_pad.astype(jnp.float32)).astype(jnp.bfloat16)
+    cut = width // SPLITS
+    hidden = jnp.concatenate(
+        [lax.psum(partial_sum[:, s * cut:(s + 1) * cut], "tensor") for s in range(SPLITS)],
+        axis=1,
+    )
+    normed = normalize(hidden, norm_gain)
 
     pre_act = jnp.dot(normed, twist_full, preferred_element_type=jnp.float32)
     active = jax.nn.silu(pre_act)
     partial_psi = jnp.dot(active, twist_out, precision=lax.Precision.HIGHEST)
+
+    lead = (j == 0).astype(jnp.float32)
+    own_bias = token_bias[token_ids]
+    row = jnp.concatenate(
+        [
+            partial_psi + lead * own_bias,
+            lead * token_ids.astype(jnp.float32),
+            lead * prompt_len.astype(jnp.float32),
+            lead * toxicity.astype(jnp.float32),
+        ]
+    )
     slot = (jnp.arange(n_dp) == r).astype(jnp.float32)
-    psi_all = lax.psum(slot[:, None] * partial_psi[None, :], ("dp", "tensor"))
-    grid = psi_all + token_bias[ids_all]
+    slab = lax.psum(slot[:, None] * row[None, :], ("dp", "tensor"))
+    grid = slab[:, :seq_len]
+    ids_all = slab[:, seq_len:2 * seq_len].astype(jnp.int32)
+    plen_all = slab[:, 2 * seq_len]
+    tox_all = slab[:, 2 * seq_len + 1]
 
-    live = jnp.arange(seq_len)[None, :] >= plen_all[:, None]
-    levels = tox_all.astype(jnp.float32)[:, None] * live.astype(jnp.float32)
+    live = jnp.arange(seq_len, dtype=jnp.float32)[None, :] >= plen_all[:, None]
+    levels = tox_all[:, None] * live.astype(jnp.float32)
     highest = jnp.max(jnp.where(live, grid, -1e30), axis=0)
     expo = jnp.where(live, jnp.exp(jnp.where(live, grid - highest[None, :], -80.0)), 0.0)
     totals = jnp.sum(expo, axis=0)
@@ -77,13 +94,18 @@
         weights[:, None] * twist_out[None, :] * sigma * (1.0 + pre_act * (1.0 - sigma))
     ).astype(jnp.bfloat16)
     contract = (((0,), (0,)), ((), ()))
-    grad_in = lax.psum_scatter(
-        lax.dot_general(normed, d_pre, contract, preferred_element_type=jnp.float32).astype(
-            jnp.bfloat16
-        ),
-        "dp",
-        scatter_dimension=0,
-        tiled=True,
+    grad_part = lax.dot_general(
+        normed, d_pre, contract, preferred_element_type=jnp.float32
+    ).astype(jnp.bfloat16)
+    hcut = grad_part.shape[1] // SPLITS
+    grad_in = jnp.concatenate(
+        [
+            lax.psum_scatter(
+                grad_part[:, s * hcut:(s + 1) * hcut], "dp", scatter_dimension=0, tiled=True
+            )
+            for s in range(SPLITS)
+        ],
+        axis=1,
     ).astype(jnp.float32)
     return (twist_vals, grad_in, grad_out, grad_bias)
 

time: 513 us -> 493 us (0.961)
  waiting for transfers between devices: 199 us -> 284 us
  blocking collectives: 213 us -> 130 us
  local copies, waits for them, and re-layouts: 24.5 us -> 3.97 us
    psum x0 -> x1, waiting for transfers between devices: none -> 229 us  [local(): lax.psum(partial_sum[:, s * cut:(s + 1) * cut], 'tensor')]
    reduce_scatter x2 -> x1, waiting for transfers between devices: 198 us -> 54.8 us  [local(): lax.psum_scatter(grad_part[:, s * hcut:(s + 1) * hcut], 'dp', scatter_dim...]
    unnamed x1 -> x0, blocking collectives: 84.1 us -> none
    gather x2 -> x1, local copies, waits for them, and re-layouts: 23 us -> 1.72 us  [local(): own_bias = token_bias[token_ids]]
  transfers between devices with their start and end apart: 4 -> 3, of which waited for: 2 -> 2; matrix products, arithmetic and copies ran while one was open for 11% -> 7% of each run, Pallas kernels for 0% -> 0%
where the time goes in v2:
time: 493 us
  waiting for transfers between devices  284 us (58%)
  blocking collectives  130 us (26%)
  other arithmetic  33.7 us (7%)
  matrix products  24.1 us (5%)
  between operations  17 us (3%)
    psum x1, waiting for transfers between devices, local(): lax.psum(partial_sum[:, s * cut:(s + 1) * cut], 'tensor')  229 us
    psum x1, blocking collectives, local(): slab = lax.psum(slot[:, None] * row[None, :], ('dp', 'tensor'))  75.9 us
    reduce_scatter x1, waiting for transfers between devices, local(): lax.psum_scatter(grad_part[:, s * hcut:(s + 1) * hcut], 'dp', scatter_dim...  54.8 us
    psum x1, blocking collectives, local(): lax.psum(jnp.dot(weights, active, precision=lax.Precision.HIGHEST), 'dp')  53.7 us
    scatter-add x1, other arithmetic, local(): jnp.zeros((slice_len,), jnp.float32).at[idx]  27.9 us
  transfers between devices with their start and end apart: 3, of which 2 were waited for; matrix products, arithmetic and copies ran while one was open for 7% of the time, Pallas kernels for 0%

profile of v2, /device:TPU:2, one launch (start us, length us, event | category | flops | bytes accessed | tf_op | source)
XLA Modules:
  0.0 492.5 jit_solution(2865151279003750199)
XLA Ops:
  8.0 0.0 copy-start
  8.0 0.0 all-reduce.2.cloned.1.call-start
  8.1 0.5 broadcast_in_dim.32
  8.5 1.0 constant_dynamic-update-slice_fusion
  9.5 0.0 copy-start.1
  9.5 7.9 %fusion = bf16[256,8192]{1,0:T(8,128)(2,1)} fusion(bf16[256,512]{1,0:T(8,128)(2,1)} %param.11, bf16[512,8192]{1,0:T(8,128)(2,1)} %param.12, bf16[256,8192]{1,0:T(8,128)(2,1)S(1)} %constant_dynamic-update-slice_fusion), kind=kOutput, calls=%fused_computation.6 | convolution fusion | flops 2153775104 | bytes 17039360 | tf_op jit(solution)/shard_map/dot_general | solution.py:40
  17.4 0.0 copy-start.2
  17.4 0.0 all-reduce.2.cloned.1.call-update
  17.5 0.0 all-gather.2.cloned.1.call-start
  17.5 0.5 all-gather.2.cloned.1.call-update
  18.0 0.0 reduce-scatter.2.cloned.1.call-start
  19.4 0.0 copy-done.1
  19.4 0.0 copy-done
  19.4 1.7 gather_fusion
  21.2 228.7 %all-reduce.2.cloned.1.call-done = bf16[256,8192]{1,0:T(8,128)(2,1)} async-done(((bf16[256,8192]{1,0:T(8,128)(2,1)}), bf16[256,8192]{1,0:T(8,128)(2,1)}) %all-reduce.2.cloned.1.call-update) | async-done | bytes 4194320 | tf_op jit(solution)/shard_map/psum | solution.py:44
  249.9 3.1 fusion.1
  253.0 0.0 copy-start.3
  253.0 0.0 all-gather.2.cloned.1.call-done
  253.1 0.0 copy-done.2
  253.1 7.0 %fusion.5 = f32[256,512]{1,0:T(8,128)S(1)} fusion(bf16[8192,512]{1,0:T(8,128)(2,1)} %all-gather.2.cloned.1.call-done, bf16[256,8192]{1,0:T(8,128)(2,1)} %all-reduce.2.cloned.1.call-done, f32[8192]{0:T(1024)S(1)} %copy-done.2, f32[256]{0:T(256)S(1)} %add_rsqrt_fusion), kind=kOutput, calls=%fused_computation.10 | convolution fusion | flops 2155872256 | bytes 13140992 | tf_op jit(solution)/shard_map/dot_general | solution.py:49
  260.1 0.0 copy-done.3
  260.1 0.6 fusion.13
  260.7 0.1 pad_maximum_fusion
  260.8 0.1 broadcast_multiply_fusion
  260.9 75.9 %psum.22 = f32[16,514]{1,0:T(8,128)S(1)} all-reduce(f32[16,514]{1,0:T(8,128)S(1)} %broadcast_multiply_fusion), channel_id=1, replica_groups=mesh['dp'=16,'tensor'=16] {'dp','tensor'}, use_global_device_ids=true, to_apply=%region_2.3 | all-reduce | flops 8224 | bytes 65792 | tf_op jit(solution)/shard_map/psum | solution.py:64
  336.8 0.2 slice_reduce_fusion.1
  337.0 0.1 select_reduce_fusion.1
  337.1 0.1 fusion.21
  337.2 0.1 fusion.16
  337.3 8.1 %convolution_convert_fusion = bf16[8192,512]{1,0:T(8,128)(2,1)} fusion(bf16[256,8192]{1,0:T(8,128)(2,1)} %all-reduce.2.cloned.1.call-done, f32[8192]{0:T(1024)S(1)} %copy-done.2, f32[256]{0:T(256)S(1)} %add_rsqrt_fusion, f32[256,512]{1,0:T(8,128)S(1)} %fusion.5, f32[512]{0:T(512)S(1)} %copy-done.3, f32[256]{0:T(256)S(1)} %bitcast.26), kind=kOutput, calls=%fused_computation.2 | convolution fusion | flops 2161377280 | bytes 13144064 | tf_op jit(solution)/shard_map/dot_general | solution.py:97
  345.4 0.0 reduce-scatter.2.cloned.1.call-update
  345.5 27.9 %scatter_custom_fusion = f32[8016]{0:T(1024)} fusion(s32[4096]{0:T(1024)S(1)} %bitcast.24, f32[4096]{0:T(1024)S(1)} %bitcast.23, f32[]{:T(128)} %constant.11.clone.1), kind=kCustom, calls=%fused_computation.29 | custom fusion | flops 4096 | bytes 32068 | tf_op jit(solution)/shard_map/scatter-add | solution.py:88
  373.4 0.5 fusion.11
  373.8 53.7 %psum.23 = f32[512]{0:T(512)} all-reduce(f32[512]{0:T(512)S(1)} %bitcast.25), channel_id=1, replica_groups=mesh['dp'=16,'tensor'=16] {'dp'}, use_global_device_ids=true, to_apply=%region_7.8 | all-reduce | flops 512 | bytes 4096 | tf_op jit(solution)/shard_map/psum | solution.py:83
  427.5 0.6 constant_dynamic-slice_fusion.1
  428.1 54.8 %reduce-scatter.2.cloned.1.call-done = bf16[512,512]{1,0:T(8,128)(2,1)} async-done(((bf16[8192,512]{1,0:T(8,128)(2,1)}), bf16[512,512]{1,0:T(8,128)(2,1)}) %reduce-scatter.2.cloned.1.call-update) | async-done | bytes 524304 | tf_op jit(solution)/shard_map/reduce_scatter | solution.py:103
  482.9 2.1 convert_element_type.55
  (12 shorter events, 0.1 us)
Async XLA Ops:
  8.0 11.4 %copy-start = (f32[128256]{0:T(1024)S(1)}, f32[128256]{0:T(1024)}, u32[]{:S(2)}) copy-start(f32[128256]{0:T(1024)} %param.17) | copy-start | bytes 1539076
  8.0 241.9 %all-reduce.2.cloned.1.call-start = ((), (), s32[]{:S(2)}) async-start(), calls=%async_computation.1 | async-start | bytes 8388608 | tf_op jit(solution)/shard_map/psum | solution.py:44
  9.5 9.9 %copy-start.1 = (s32[256]{0:T(256)S(1)}, s32[256]{0:T(256)}, u32[]{:S(2)}) copy-start(s32[256]{0:T(256)} %param.10) | copy-start | bytes 3076
  17.4 235.6 %copy-start.2 = (f32[8192]{0:T(1024)S(1)}, f32[8192]{0:T(1024)}, u32[]{:S(2)}) copy-start(f32[8192]{0:T(1024)} %param.14) | copy-start | bytes 98308
  17.5 235.6 %all-gather.2.cloned.1.call-start = ((), (), s32[]{:S(2)}) async-start(), calls=%async_computation.2 | async-start | bytes 8912896 | tf_op jit(solution)/shard_map/all_gather | solution.py:35
  18.0 464.9 %reduce-scatter.2.cloned.1.call-start = ((), (), s32[]{:S(2)}) async-start(), calls=%async_computation.3 | async-start | bytes 8912896 | tf_op jit(solution)/shard_map/reduce_scatter | solution.py:103
  253.0 7.1 %copy-start.3 = (f32[512]{0:T(512)S(1)}, f32[512]{0:T(512)}, u32[]{:S(2)}) copy-start(f32[512]{0:T(512)} %param.16) | copy-start | bytes 6148
Sparse Core Ops, SparseCore 0:
  17.6 232.2 all-reduce.1
Sparse Core Ops, SparseCore 1:
  20.6 114.6 all-gather.1
  345.5 137.4 reduce-scatter.1

commit v3 on v2

--- a/solution.py
+++ b/solution.py
@@ -1,7 +1,7 @@
 import jax
 import jax.numpy as jnp
 from jax import lax
-from jax.sharding import PartitionSpec as P
+from jax.sharding import Mesh, PartitionSpec as P
 
 SPLITS = 1
 
@@ -29,7 +29,7 @@
     vocab_size = token_bias.shape[0]
     n_dp = lax.axis_size("dp")
     r = lax.axis_index("dp")
-    j = lax.axis_index("tensor")
+    j = lax.axis_index(("tz", "tx"))
     rows = residual.shape[0]
 
     twist_full = lax.all_gather(twist_in, "dp", axis=0, tiled=True)
@@ -39,11 +39,9 @@
     )
     partial_sum = jnp.dot(attn_heads, out_proj, preferred_element_type=jnp.float32)
     partial_sum = (partial_sum + resid_pad.astype(jnp.float32)).astype(jnp.bfloat16)
-    cut = width // SPLITS
-    hidden = jnp.concatenate(
-        [lax.psum(partial_sum[:, s * cut:(s + 1) * cut], "tensor") for s in range(SPLITS)],
-        axis=1,
-    )
+    part = lax.psum_scatter(partial_sum, "tx", scatter_dimension=1, tiled=True)
+    part = lax.psum(part, "tz")
+    hidden = lax.all_gather(part, "tx", axis=1, tiled=True)
     normed = normalize(hidden, norm_gain)
 
     pre_act = jnp.dot(normed, twist_full, preferred_element_type=jnp.float32)
@@ -61,7 +59,7 @@
         ]
     )
     slot = (jnp.arange(n_dp) == r).astype(jnp.float32)
-    slab = lax.psum(slot[:, None] * row[None, :], ("dp", "tensor"))
+    slab = lax.psum(slot[:, None] * row[None, :], ("dp", "tz", "tx"))
     grid = slab[:, :seq_len]
     ids_all = slab[:, seq_len:2 * seq_len].astype(jnp.int32)
     plen_all = slab[:, 2 * seq_len]
@@ -111,22 +109,26 @@
 
 
 def solution(mesh):
+    n_dp, n_tensor = mesh.devices.shape
+    n_x = 4
+    split = Mesh(mesh.devices.reshape(n_dp, n_tensor // n_x, n_x), ("dp", "tz", "tx"))
+    tensor = ("tz", "tx")
     placed = (
         P("dp"),
-        P("dp", "tensor"),
-        P("tensor", None),
-        P(("dp", "tensor"), None),
+        P("dp", tensor),
+        P(tensor, None),
+        P(("dp",) + tensor, None),
         P(),
-        P("dp", "tensor"),
-        P("tensor"),
+        P("dp", tensor),
+        P(tensor),
         P(),
         P("dp"),
         P("dp"),
     )
     return jax.shard_map(
         local,
-        mesh=mesh,
+        mesh=split,
         in_specs=placed,
-        out_specs=(P("dp"), P("dp", "tensor"), P("tensor"), P("dp")),
+        out_specs=(P("dp"), P("dp", tensor), P(tensor), P("dp")),
         check_vma=False,
     )

time: 493 us -> 535 us (1.085)
  waiting for transfers between devices: 284 us -> 334 us
    psum x1, waiting for transfers between devices: 229 us -> 67.8 us  [local(): part = lax.psum(part, 'tz')]
    all_gather x1, waiting for transfers between devices: 0.03 us -> 109 us  [local(): twist_full = lax.all_gather(twist_in, 'dp', axis=0, tiled=True)]
    reduce_scatter x0 -> x1, waiting for transfers between devices: none -> 51.2 us  [local(): part = lax.psum_scatter(partial_sum, 'tx', scatter_dimension=1, tiled=True)]
    all_gather x0 -> x1, waiting for transfers between devices: none -> 47 us  [local(): hidden = lax.all_gather(part, 'tx', axis=1, tiled=True)]
  transfers between devices with their start and end apart: 3 -> 5, of which waited for: 2 -> 5; matrix products, arithmetic and copies ran while one was open for 7% -> 6% of each run, Pallas kernels for 0% -> 0%
where the time goes in v3:
time: 535 us
  waiting for transfers between devices  334 us (62%)
  blocking collectives  125 us (23%)
  other arithmetic  33.2 us (6%)
  matrix products  24 us (4%)
  between operations  15.3 us (3%)
    all_gather x1, waiting for transfers between devices, local(): twist_full = lax.all_gather(twist_in, 'dp', axis=0, tiled=True)  109 us
    psum x1, blocking collectives, local(): slab = lax.psum(slot[:, None] * row[None, :], ('dp', 'tz', 'tx'))  74.1 us
    psum x1, waiting for transfers between devices, local(): part = lax.psum(part, 'tz')  67.8 us
    reduce_scatter x1, waiting for transfers between devices, local(): lax.psum_scatter(grad_part[:, s * hcut:(s + 1) * hcut], 'dp', scatter_dim...  58.4 us
    reduce_scatter x1, waiting for transfers between devices, local(): part = lax.psum_scatter(partial_sum, 'tx', scatter_dimension=1, tiled=True)  51.2 us
    psum x1, blocking collectives, local(): lax.psum(jnp.dot(weights, active, precision=lax.Precision.HIGHEST), 'dp')  50.9 us
    all_gather x1, waiting for transfers between devices, local(): hidden = lax.all_gather(part, 'tx', axis=1, tiled=True)  47 us
    scatter-add x1, other arithmetic, local(): jnp.zeros((slice_len,), jnp.float32).at[idx]  27.4 us
  transfers between devices with their start and end apart: 5, of which 5 were waited for; matrix products, arithmetic and copies ran while one was open for 6% of the time, Pallas kernels for 0%

profile of v3, /device:TPU:2, one launch (start us, length us, event | category | flops | bytes accessed | tf_op | source)
XLA Modules:
  0.0 535.4 jit_solution(12805364486706586550)
XLA Ops:
  7.2 0.0 copy-start
  7.2 0.0 reduce-scatter.3.cloned.1.call-start
  7.2 0.5 broadcast_in_dim.32
  7.7 1.0 constant_dynamic-update-slice_fusion
  8.7 0.0 copy-start.1
  8.7 7.9 %fusion = bf16[256,8192]{1,0:T(8,128)(2,1)} fusion(bf16[256,512]{1,0:T(8,128)(2,1)} %param.11, bf16[512,8192]{1,0:T(8,128)(2,1)} %param.12, bf16[256,8192]{1,0:T(8,128)(2,1)S(1)} %constant_dynamic-update-slice_fusion), kind=kOutput, calls=%fused_computation.6 | convolution fusion | flops 2153775104 | bytes 17039360 | tf_op jit(solution)/shard_map/dot_general | solution.py:40
  16.6 0.0 copy-start.2
  16.6 0.0 reduce-scatter.3.cloned.1.call-update
  16.6 0.0 all-reduce.2.cloned.1.call-start
  16.6 51.2 %reduce-scatter.3.cloned.1.call-done = bf16[256,2048]{1,0:T(8,128)(2,1)} async-done(((bf16[256,8192]{1,0:T(8,128)(2,1)}), bf16[256,2048]{1,0:T(8,128)(2,1)}) %reduce-scatter.3.cloned.1.call-update) | async-done | bytes 1048592 | tf_op jit(solution)/shard_map/reduce_scatter | solution.py:42
  67.8 0.0 all-reduce.2.cloned.1.call-update
  67.9 0.0 all-gather.3.cloned.1.call-start
  67.9 67.8 %all-reduce.2.cloned.1.call-done = bf16[256,2048]{1,0:T(8,128)(2,1)} async-done(((bf16[256,2048]{1,0:T(8,128)(2,1)}), bf16[256,2048]{1,0:T(8,128)(2,1)}) %all-reduce.2.cloned.1.call-update) | async-done | bytes 1048592 | tf_op jit(solution)/shard_map/psum | solution.py:43
  135.7 0.0 all-gather.3.cloned.1.call-update
  135.7 0.0 all-gather.5.cloned.1.call-start
  135.7 0.5 all-gather.5.cloned.1.call-update
  136.3 0.0 reduce-scatter.5.cloned.1.call-start
  137.6 0.0 copy-done.1
  137.7 0.0 copy-done
  137.7 1.7 gather_fusion
  139.4 47.0 %all-gather.3.cloned.1.call-done = bf16[256,8192]{1,0:T(8,128)(2,1)} async-done(((bf16[256,2048]{1,0:T(8,128)(2,1)}), bf16[256,8192]{1,0:T(8,128)(2,1)}) %all-gather.3.cloned.1.call-update) | async-done | bytes 4194320 | tf_op jit(solution)/shard_map/all_gather | solution.py:44
  186.4 3.1 fusion.1
  189.6 0.0 copy-start.3
  189.6 108.8 %all-gather.5.cloned.1.call-done = bf16[8192,512]{1,0:T(8,128)(2,1)} async-done(((bf16[512,512]{1,0:T(8,128)(2,1)}), bf16[8192,512]{1,0:T(8,128)(2,1)}) %all-gather.5.cloned.1.call-update) | async-done | bytes 8388624 | tf_op jit(solution)/shard_map/all_gather | solution.py:35
  298.4 0.0 copy-done.2
  298.4 7.0 %fusion.5 = f32[256,512]{1,0:T(8,128)S(1)} fusion(bf16[8192,512]{1,0:T(8,128)(2,1)} %all-gather.5.cloned.1.call-done, bf16[256,8192]{1,0:T(8,128)(2,1)} %all-gather.3.cloned.1.call-done, f32[8192]{0:T(1024)S(1)} %copy-done.2, f32[256]{0:T(256)S(1)} %add_rsqrt_fusion), kind=kOutput, calls=%fused_computation.10 | convolution fusion | flops 2155872256 | bytes 13140992 | tf_op jit(solution)/shard_map/dot_general | solution.py:47
  305.4 0.0 copy-done.3
  305.4 0.6 fusion.13
  306.0 0.1 pad_maximum_fusion
  306.1 0.1 broadcast_multiply_fusion
  306.2 74.1 %psum.22 = f32[16,514]{1,0:T(8,128)S(1)} all-reduce(f32[16,514]{1,0:T(8,128)S(1)} %broadcast_multiply_fusion), channel_id=1, replica_groups=mesh['dp'=16,'tz'=4,'tx'=4] {'dp','tz','tx'}, use_global_device_ids=true, to_apply=%region_3.4 | all-reduce | flops 8224 | bytes 65792 | tf_op jit(solution)/shard_map/psum | solution.py:62
  380.2 0.2 slice_reduce_fusion.1
  380.4 0.1 select_reduce_fusion.1
  380.5 0.1 fusion.21
  380.6 0.1 fusion.16
  380.7 8.1 %convolution_convert_fusion = bf16[8192,512]{1,0:T(8,128)(2,1)} fusion(bf16[256,8192]{1,0:T(8,128)(2,1)} %all-gather.3.cloned.1.call-done, f32[8192]{0:T(1024)S(1)} %copy-done.2, f32[256]{0:T(256)S(1)} %add_rsqrt_fusion, f32[256,512]{1,0:T(8,128)S(1)} %fusion.5, f32[512]{0:T(512)S(1)} %copy-done.3, f32[256]{0:T(256)S(1)} %bitcast.26), kind=kOutput, calls=%fused_computation.2 | convolution fusion | flops 2161377280 | bytes 13144064 | tf_op jit(solution)/shard_map/dot_general | solution.py:95
  388.8 0.0 reduce-scatter.5.cloned.1.call-update
  388.9 27.4 %scatter_custom_fusion = f32[8016]{0:T(1024)} fusion(s32[4096]{0:T(1024)S(1)} %bitcast.24, f32[4096]{0:T(1024)S(1)} %bitcast.23, f32[]{:T(128)} %constant.15.clone.1), kind=kCustom, calls=%fused_computation.29 | custom fusion | flops 4096 | bytes 32068 | tf_op jit(solution)/shard_map/scatter-add | solution.py:86
  416.3 0.5 fusion.11
  416.8 50.9 %psum.23 = f32[512]{0:T(512)} all-reduce(f32[512]{0:T(512)S(1)} %bitcast.25), channel_id=1, replica_groups=mesh['dp'=16,'tz'=4,'tx'=4] {'dp'}, use_global_device_ids=true, to_apply=%region_8.9 | all-reduce | flops 512 | bytes 4096 | tf_op jit(solution)/shard_map/psum | solution.py:81
  467.7 0.6 constant_dynamic-slice_fusion.1
  468.3 58.4 %reduce-scatter.5.cloned.1.call-done = bf16[512,512]{1,0:T(8,128)(2,1)} async-done(((bf16[8192,512]{1,0:T(8,128)(2,1)}), bf16[512,512]{1,0:T(8,128)(2,1)}) %reduce-scatter.5.cloned.1.call-update) | async-done | bytes 524304 | tf_op jit(solution)/shard_map/reduce_scatter | solution.py:101
  526.7 2.1 convert_element_type.55
  (12 shorter events, 0.1 us)
Async XLA Ops:
  7.2 130.5 %copy-start = (f32[128256]{0:T(1024)S(1)}, f32[128256]{0:T(1024)}, u32[]{:S(2)}) copy-start(f32[128256]{0:T(1024)} %param.17) | copy-start | bytes 1539076
  7.2 60.7 %reduce-scatter.3.cloned.1.call-start = ((), (), s32[]{:S(2)}) async-start(), calls=%async_computation.2 | async-start | bytes 5242880 | tf_op jit(solution)/shard_map/reduce_scatter | solution.py:42
  8.7 129.0 %copy-start.1 = (s32[256]{0:T(256)S(1)}, s32[256]{0:T(256)}, u32[]{:S(2)}) copy-start(s32[256]{0:T(256)} %param.10) | copy-start | bytes 3076
  16.6 281.8 %copy-start.2 = (f32[8192]{0:T(1024)S(1)}, f32[8192]{0:T(1024)}, u32[]{:S(2)}) copy-start(f32[8192]{0:T(1024)} %param.14) | copy-start | bytes 98308
  16.6 119.1 %all-reduce.2.cloned.1.call-start = ((), (), s32[]{:S(2)}) async-start(), calls=%async_computation.3 | async-start | bytes 2097152 | tf_op jit(solution)/shard_map/psum | solution.py:43
  67.9 118.6 %all-gather.3.cloned.1.call-start = ((), (), s32[]{:S(2)}) async-start(), calls=%async_computation.4 | async-start | bytes 5242880 | tf_op jit(solution)/shard_map/all_gather | solution.py:44
  135.7 162.6 %all-gather.5.cloned.1.call-start = ((), (), s32[]{:S(2)}) async-start(), calls=%async_computation.5 | async-start | bytes 8912896 | tf_op jit(solution)/shard_map/all_gather | solution.py:35
  136.3 390.5 %reduce-scatter.5.cloned.1.call-start = ((), (), s32[]{:S(2)}) async-start(), calls=%async_computation.6 | async-start | bytes 8912896 | tf_op jit(solution)/shard_map/reduce_scatter | solution.py:101
  189.6 115.8 %copy-start.3 = (f32[512]{0:T(512)S(1)}, f32[512]{0:T(512)}, u32[]{:S(2)}) copy-start(f32[512]{0:T(512)} %param.16) | copy-start | bytes 6148
Sparse Core Ops, SparseCore 0:
  16.7 51.0 reduce-scatter.2
  70.5 65.1 all-reduce.1
  137.5 48.9 all-gather.2
  189.0 109.3 all-gather.4
  389.0 137.7 reduce-scatter.4

commit v4 on v3

--- a/solution.py
+++ b/solution.py
@@ -32,7 +32,16 @@
     j = lax.axis_index(("tz", "tx"))
     rows = residual.shape[0]
 
-    twist_full = lax.all_gather(twist_in, "dp", axis=0, tiled=True)
+    stack = twist_in[None]
+    bits = (2, 3, 1, 0)
+    for b in bits:
+        got = lax.ppermute(stack, "dp", [(i, i ^ (1 << b)) for i in range(n_dp)])
+        stack = jnp.concatenate([stack, got])
+    pos = jnp.arange(n_dp)
+    want = jnp.zeros((n_dp,), jnp.int32)
+    for p_bit in range(len(bits)):
+        want = want | ((((pos ^ r) >> bits[p_bit]) & 1) << p_bit)
+    twist_full = jnp.take(stack, want, axis=0).reshape(-1, twist_in.shape[1])
 
     resid_pad = lax.dynamic_update_slice(
         jnp.zeros((seq_len, width), residual.dtype), residual, (j * rows, 0)

time: 535 us -> 498 us (0.931)
  waiting for transfers between devices: 334 us -> 248 us
  local copies, waits for them, and re-layouts: 3.97 us -> 23 us
  other arithmetic: 33.2 us -> 46.6 us
  starting transfers between devices: 0.19 us -> 12.3 us
    ppermute x0 -> x4, waiting for transfers between devices: none -> 136 us  [local(): got = lax.ppermute(stack, 'dp', [(i, i ^ 1 << b) for i in range(n_dp)])]
    all_gather x1 -> x0, waiting for transfers between devices: 109 us -> none  [local(): twist_full = lax.all_gather(twist_in, 'dp', axis=0, tiled=True)]
    reduce_scatter x1, waiting for transfers between devices: 51.2 us -> 2.97 us  [local(): part = lax.psum_scatter(partial_sum, 'tx', scatter_dimension=1, tiled=True)]
    psum x1, waiting for transfers between devices: 67.8 us -> 29.4 us  [local(): part = lax.psum(part, 'tz')]
    all_gather x1, waiting for transfers between devices: 47 us -> 21 us  [local(): hidden = lax.all_gather(part, 'tx', axis=1, tiled=True)]
    ppermute x0 -> x4, starting transfers between devices: none -> 12.1 us  [local(): got = lax.ppermute(stack, 'dp', [(i, i ^ 1 << b) for i in range(n_dp)])]
    gather x0 -> x1, local copies, waits for them, and re-layouts: none -> 8.64 us  [local(): twist_full = jnp.take(stack, want, axis=0).reshape(-1, twist_in.shape[1])]
    select_n x0 -> x2, other arithmetic: none -> 7.51 us  [local(): twist_full = jnp.take(stack, want, axis=0).reshape(-1, twist_in.shape[1])]
  transfers between devices with their start and end apart: 5 -> 8, of which waited for: 5 -> 7; matrix products, arithmetic and copies ran while one was open for 6% -> 13% of each run, Pallas kernels for 0% -> 0%
where the time goes in v4:
time: 498 us
  waiting for transfers between devices  248 us (50%)
  blocking collectives  129 us (26%)
  other arithmetic  46.6 us (9%)
  matrix products  24.2 us (5%)
  local copies, waits for them, and re-layouts  23 us (5%)
  between operations  15.3 us (3%)
  starting transfers between devices  12.3 us (2%)
    ppermute x4, waiting for transfers between devices, local(): got = lax.ppermute(stack, 'dp', [(i, i ^ 1 << b) for i in range(n_dp)])  136 us
    psum x1, blocking collectives, local(): slab = lax.psum(slot[:, None] * row[None, :], ('dp', 'tz', 'tx'))  76.5 us
    reduce_scatter x1, waiting for transfers between devices, local(): lax.psum_scatter(grad_part[:, s * hcut:(s + 1) * hcut], 'dp', scatter_dim...  58.1 us
    psum x1, blocking collectives, local(): lax.psum(jnp.dot(weights, active, precision=lax.Precision.HIGHEST), 'dp')  52.1 us
    psum x1, waiting for transfers between devices, local(): part = lax.psum(part, 'tz')  29.4 us
    scatter-add x1, other arithmetic, local(): jnp.zeros((slice_len,), jnp.float32).at[idx]  28.3 us
    all_gather x1, waiting for transfers between devices, local(): hidden = lax.all_gather(part, 'tx', axis=1, tiled=True)  21 us
    ppermute x4, starting transfers between devices, local(): got = lax.ppermute(stack, 'dp', [(i, i ^ 1 << b) for i in range(n_dp)])  12.1 us
  transfers between devices with their start and end apart: 8, of which 7 were waited for; matrix products, arithmetic and copies ran while one was open for 13% of the time, Pallas kernels for 0%

profile of v4, /device:TPU:2, one launch (start us, length us, event | category | flops | bytes accessed | tf_op | source)
XLA Modules:
  0.0 497.6 jit_solution(10963663892827144191)
XLA Ops:
  7.2 0.0 copy-start
  7.2 0.0 reduce-scatter.3.cloned.1.call-start
  7.2 0.5 broadcast_in_dim.49
  7.7 1.0 constant_dynamic-update-slice_fusion.5
  8.7 0.0 copy-start.2
  8.7 7.9 %fusion = bf16[256,8192]{1,0:T(8,128)(2,1)} fusion(bf16[256,512]{1,0:T(8,128)(2,1)} %param.11, bf16[512,8192]{1,0:T(8,128)(2,1)} %param.12, bf16[256,8192]{1,0:T(8,128)(2,1)S(1)} %constant_dynamic-update-slice_fusion.5), kind=kOutput, calls=%fused_computation.7 | convolution fusion | flops 2153775104 | bytes 17039360 | tf_op jit(solution)/shard_map/dot_general | solution.py:49
  16.6 0.0 reduce-scatter.3.cloned.1.call-update
  16.6 0.0 all-reduce.2.cloned.1.call-start
  16.7 0.0 copy-done.2
  16.7 0.0 copy-start.3
  16.7 1.7 collective-permute-start
  18.4 12.1 %collective-permute-done = bf16[1,512,512]{2,1,0:T(8,128)(2,1)S(1)} collective-permute-done((bf16[1,512,512]{2,1,0:T(8,128)(2,1)S(1)}, bf16[1,512,512]{2,1,0:T(8,128)(2,1)S(1)}, u32[]{:S(2)}, u32[]{:S(2)}) %collective-permute-start) | collective-permute-done | bytes 524320 | tf_op jit(solution)/shard_map/ppermute | solution.py:38
  30.5 0.1 pad_maximum_fusion.2
  30.6 3.3 collective-permute-start.1
  33.9 22.4 %collective-permute-done.1 = bf16[2,512,512]{2,1,0:T(8,128)(2,1)S(1)} collective-permute-done((bf16[2,512,512]{2,1,0:T(8,128)(2,1)S(1)}, bf16[2,512,512]{2,1,0:T(8,128)(2,1)S(1)}, u32[]{:S(2)}, u32[]{:S(2)}) %collective-permute-start.1) | collective-permute-done | bytes 1048608 | tf_op jit(solution)/shard_map/ppermute | solution.py:38
  56.2 1.5 pad_maximum_fusion.1
  57.7 7.2 %collective-permute-start.2 = (bf16[4,512,512]{2,1,0:T(8,128)(2,1)}, bf16[4,512,512]{2,1,0:T(8,128)(2,1)}, u32[]{:S(2)}, u32[]{:S(2)}) collective-permute-start(bf16[4,512,512]{2,1,0:T(8,128)(2,1)} %pad_maximum_fusion.1), channel_id=1, source_target_pairs={{0,32},{16,48},{32,0},{48,16},{64,96},{80,112},{96,64},{112,80},{1... | collective-permute-start | bytes 6291464 | tf_op jit(solution)/shard_map/ppermute | solution.py:38
  64.9 3.0 reduce-scatter.3.cloned.1.call-done
  67.9 0.0 all-reduce.2.cloned.1.call-update
  67.9 0.0 all-gather.2.cloned.1.call-start
  68.0 101.7 %collective-permute-done.2 = bf16[4,512,512]{2,1,0:T(8,128)(2,1)} collective-permute-done((bf16[4,512,512]{2,1,0:T(8,128)(2,1)}, bf16[4,512,512]{2,1,0:T(8,128)(2,1)}, u32[]{:S(2)}, u32[]{:S(2)}) %collective-permute-start.2) | collective-permute-done | bytes 2097184 | tf_op jit(solution)/shard_map/ppermute | solution.py:38
  169.6 3.4 pad_maximum_fusion
  173.1 0.0 collective-permute-start.3
  173.1 29.4 %all-reduce.2.cloned.1.call-done = bf16[256,2048]{1,0:T(8,128)(2,1)} async-done(((bf16[256,2048]{1,0:T(8,128)(2,1)}), bf16[256,2048]{1,0:T(8,128)(2,1)}) %all-reduce.2.cloned.1.call-update) | async-done | bytes 1048592 | tf_op jit(solution)/shard_map/psum | solution.py:52
  202.4 0.0 all-gather.2.cloned.1.call-update
  202.5 0.0 reduce-scatter.5.cloned.1.call-start
  203.8 0.1 broadcast_bitcast_fusion
  203.9 0.0 copy-done.3
  204.0 0.0 copy-done
  204.0 1.7 gather_fusion.1
  205.7 0.9 constant_dynamic-update-slice_fusion.4
  206.6 0.9 constant_dynamic-update-slice_fusion.3
  207.5 1.0 constant_dynamic-update-slice_fusion.2
  208.6 3.0 constant_dynamic-update-slice_fusion.1
  211.6 0.0 collective-permute-done.3
  211.6 4.4 constant_dynamic-update-slice_fusion
  216.0 8.6 %gather_fusion = bf16[16,512,512]{2,1,0:T(8,128)(2,1)} fusion(bf16[16,512,512]{2,1,0:T(8,128)(2,1)} %constant_dynamic-update-slice_fusion, s32[1024]{0:T(1024)S(1)} %pad_clamp_fusion.1), kind=kCustom, calls=%fused_computation | custom fusion | bytes 16777280 | tf_op jit(solution)/shard_map/jit(_take)/gather | solution.py:44
  224.6 0.0 copy-start.4
  224.6 7.5 %bitcast_select_fusion = bf16[8192,512]{1,0:T(8,128)(2,1)} fusion(bf16[16,512,512]{2,1,0:T(8,128)(2,1)} %gather_fusion, pred[8192]{0:T(1024)(128)(4,1)S(1)} %bitcast.36), kind=kLoop, calls=%fused_computation.11 | loop fusion | flops 4194304 | bytes 16785408 | tf_op jit(solution)/shard_map/jit(_take)/select_n | solution.py:44
  232.1 21.0 %all-gather.2.cloned.1.call-done = bf16[256,8192]{1,0:T(8,128)(2,1)} async-done(((bf16[256,2048]{1,0:T(8,128)(2,1)}), bf16[256,8192]{1,0:T(8,128)(2,1)}) %all-gather.2.cloned.1.call-update) | async-done | bytes 4194320 | tf_op jit(solution)/shard_map/all_gather | solution.py:53
  253.2 3.1 fusion.1
  256.3 0.0 copy-done.4
  256.3 0.0 copy-start.5
  256.3 7.0 %fusion.5 = f32[256,512]{1,0:T(8,128)S(1)} fusion(bf16[8192,512]{1,0:T(8,128)(2,1)} %bitcast_select_fusion, bf16[256,8192]{1,0:T(8,128)(2,1)} %all-gather.2.cloned.1.call-done, f32[8192]{0:T(1024)S(1)} %copy-done.4, f32[256]{0:T(256)S(1)} %add_rsqrt_fusion), kind=kOutput, calls=%fused_computation.14 | convolution fusion | flops 2155872256 | bytes 13140992 | tf_op jit(solution)/shard_map/dot_general | solution.py:56
  263.4 0.0 copy-done.5
  263.4 0.6 fusion.13
  264.0 0.1 pad_maximum_fusion.3
  264.1 0.1 broadcast_multiply_fusion
  264.2 76.5 %psum.22 = f32[16,514]{1,0:T(8,128)S(1)} all-reduce(f32[16,514]{1,0:T(8,128)S(1)} %broadcast_multiply_fusion), channel_id=1, replica_groups=mesh['dp'=16,'tz'=4,'tx'=4] {'dp','tz','tx'}, use_global_device_ids=true, to_apply=%region_3.4 | all-reduce | flops 8224 | bytes 65792 | tf_op jit(solution)/shard_map/psum | solution.py:71
  340.7 0.2 slice_reduce_fusion.1
  340.9 0.1 select_reduce_fusion.1
  340.9 0.1 fusion.21
  341.1 0.1 fusion.16
  341.2 0.0 copy-start.1
  341.2 8.1 %convolution_convert_fusion = bf16[8192,512]{1,0:T(8,128)(2,1)} fusion(bf16[256,8192]{1,0:T(8,128)(2,1)} %all-gather.2.cloned.1.call-done, f32[8192]{0:T(1024)S(1)} %copy-done.4, f32[256]{0:T(256)S(1)} %add_rsqrt_fusion, f32[256,512]{1,0:T(8,128)S(1)} %fusion.5, f32[512]{0:T(512)S(1)} %copy-done.5, f32[256]{0:T(256)S(1)} %bitcast.40), kind=kOutput, calls=%fused_computation.3 | convolution fusion | flops 2161377280 | bytes 13144064 | tf_op jit(solution)/shard_map/dot_general | solution.py:104
  349.3 0.0 reduce-scatter.5.cloned.1.call-update
  349.4 28.3 %scatter_custom_fusion = f32[8016]{0:T(1024)} fusion(s32[4096]{0:T(1024)S(1)} %bitcast.38, f32[4096]{0:T(1024)S(1)} %bitcast.37, f32[]{:T(128)} %constant.19.clone.1), kind=kCustom, calls=%fused_computation.34 | custom fusion | flops 4096 | bytes 32068 | tf_op jit(solution)/shard_map/scatter-add | solution.py:95
  377.7 0.5 fusion.11
  378.2 52.1 %psum.23 = f32[512]{0:T(512)} all-reduce(f32[512]{0:T(512)S(1)} %bitcast.39), channel_id=1, replica_groups=mesh['dp'=16,'tz'=4,'tx'=4] {'dp'}, use_global_device_ids=true, to_apply=%region_8.9 | all-reduce | flops 512 | bytes 4096 | tf_op jit(solution)/shard_map/psum | solution.py:90
  430.3 0.6 constant_dynamic-slice_fusion.1
  430.9 58.1 %reduce-scatter.5.cloned.1.call-done = bf16[512,512]{1,0:T(8,128)(2,1)} async-done(((bf16[8192,512]{1,0:T(8,128)(2,1)}), bf16[512,512]{1,0:T(8,128)(2,1)}) %reduce-scatter.5.cloned.1.call-update) | async-done | bytes 524304 | tf_op jit(solution)/shard_map/reduce_scatter | solution.py:110
  489.0 2.1 convert_element_type.55
  491.1 0.0 copy-done.1
  (16 shorter events, 0.2 us)
Async XLA Ops:
  7.2 196.8 %copy-start = (f32[128256]{0:T(1024)S(1)}, f32[128256]{0:T(1024)}, u32[]{:S(2)}) copy-start(f32[128256]{0:T(1024)} %param.17) | copy-start | bytes 1539076
  7.2 60.7 %reduce-scatter.3.cloned.1.call-start = ((), (), s32[]{:S(2)}) async-start(), calls=%async_computation.2 | async-start | bytes 5242880 | tf_op jit(solution)/shard_map/reduce_scatter | solution.py:51
  8.7 8.0 %copy-start.2 = (bf16[512,512]{1,0:T(8,128)(2,1)S(1)}, bf16[512,512]{1,0:T(8,128)(2,1)}, u32[]{:S(2)}) copy-start(bf16[512,512]{1,0:T(8,128)(2,1)} %param.15) | copy-start | bytes 1572868
  16.6 185.8 %all-reduce.2.cloned.1.call-start = ((), (), s32[]{:S(2)}) async-start(), calls=%async_computation.3 | async-start | bytes 2097152 | tf_op jit(solution)/shard_map/psum | solution.py:52
  16.7 187.2 %copy-start.3 = (s32[256]{0:T(256)S(1)}, s32[256]{0:T(256)}, u32[]{:S(2)}) copy-start(s32[256]{0:T(256)} %param.10) | copy-start | bytes 3076
  16.7 13.8 %collective-permute-start = (bf16[1,512,512]{2,1,0:T(8,128)(2,1)S(1)}, bf16[1,512,512]{2,1,0:T(8,128)(2,1)S(1)}, u32[]{:S(2)}, u32[]{:S(2)}) collective-permute-start(bf16[1,512,512]{2,1,0:T(8,128)(2,1)S(1)} %bitcast.30), channel_id=1, source_target_pairs={{0,64},{16,80},{32,96},{48,112},{64,0},{80,16},{96,32},{112,48},{1... | collective-permute-start | bytes 1572872 | tf_op jit(solution)/shard_map/ppermute | solution.py:38
  30.6 25.6 %collective-permute-start.1 = (bf16[2,512,512]{2,1,0:T(8,128)(2,1)S(1)}, bf16[2,512,512]{2,1,0:T(8,128)(2,1)S(1)}, u32[]{:S(2)}, u32[]{:S(2)}) collective-permute-start(bf16[2,512,512]{2,1,0:T(8,128)(2,1)S(1)} %pad_maximum_fusion.2), channel_id=1, source_target_pairs={{0,128},{16,144},{32,160},{48,176},{64,192},{80,208},{96,224},{112... | collective-permute-start | bytes 3145736 | tf_op jit(solution)/shard_map/ppermute | solution.py:38
  57.7 111.9 %collective-permute-start.2 = (bf16[4,512,512]{2,1,0:T(8,128)(2,1)}, bf16[4,512,512]{2,1,0:T(8,128)(2,1)}, u32[]{:S(2)}, u32[]{:S(2)}) collective-permute-start(bf16[4,512,512]{2,1,0:T(8,128)(2,1)} %pad_maximum_fusion.1), channel_id=1, source_target_pairs={{0,32},{16,48},{32,0},{48,16},{64,96},{80,112},{96,64},{112,80},{1... | collective-permute-start | bytes 6291464 | tf_op jit(solution)/shard_map/ppermute | solution.py:38
  67.9 185.3 %all-gather.2.cloned.1.call-start = ((), (), s32[]{:S(2)}) async-start(), calls=%async_computation.4 | async-start | bytes 5242880 | tf_op jit(solution)/shard_map/all_gather | solution.py:53
  173.1 38.5 %collective-permute-start.3 = (bf16[8,512,512]{2,1,0:T(8,128)(2,1)}, bf16[8,512,512]{2,1,0:T(8,128)(2,1)}, u32[]{:S(2)}, u32[]{:S(2)}) collective-permute-start(bf16[8,512,512]{2,1,0:T(8,128)(2,1)} %pad_maximum_fusion), channel_id=1, source_target_pairs={{0,16},{16,0},{32,48},{48,32},{64,80},{80,64},{96,112},{112,96},{1... | collective-permute-start | bytes 12582920 | tf_op jit(solution)/shard_map/ppermute | solution.py:38
  202.5 286.5 %reduce-scatter.5.cloned.1.call-start = ((), (), s32[]{:S(2)}) async-start(), calls=%async_computation.5 | async-start | bytes 8912896 | tf_op jit(solution)/shard_map/reduce_scatter | solution.py:110
  224.6 31.7 %copy-start.4 = (f32[8192]{0:T(1024)S(1)}, f32[8192]{0:T(1024)}, u32[]{:S(2)}) copy-start(f32[8192]{0:T(1024)} %param.14) | copy-start | bytes 98308
  256.3 7.1 %copy-start.5 = (f32[512]{0:T(512)S(1)}, f32[512]{0:T(512)}, u32[]{:S(2)}) copy-start(f32[512]{0:T(512)} %param.16) | copy-start | bytes 6148
  341.2 149.9 %copy-start.1 = (f32[128256]{0:T(1024)S(1)}, f32[128256]{0:T(1024)}, u32[]{:S(2)}) copy-start(f32[128256]{0:T(1024)} %param.17) | copy-start | bytes 1539076
Sparse Core Ops, SparseCore 0:
  16.8 51.0 reduce-scatter.2
  70.6 131.8 all-reduce.1
  204.2 48.9 all-gather.1
  349.5 139.4 reduce-scatter.4

commit v5 on v4

--- a/solution.py
+++ b/solution.py
@@ -33,7 +33,7 @@
     rows = residual.shape[0]
 
     stack = twist_in[None]
-    bits = (2, 3, 1, 0)
+    bits = (1, 2, 3, 0)
     for b in bits:
         got = lax.ppermute(stack, "dp", [(i, i ^ (1 << b)) for i in range(n_dp)])
         stack = jnp.concatenate([stack, got])

time: 498 us -> 435 us (0.87)
  waiting for transfers between devices: 248 us -> 185 us
    ppermute x4, waiting for transfers between devices: 136 us -> 80.6 us  [local(): got = lax.ppermute(stack, 'dp', [(i, i ^ 1 << b) for i in range(n_dp)])]
    psum x1, waiting for transfers between devices: 29.4 us -> 24.1 us  [local(): part = lax.psum(part, 'tz')]
  transfers between devices with their start and end apart: 8 -> 8, of which waited for: 7 -> 7; matrix products, arithmetic and copies ran while one was open for 13% -> 14% of each run, Pallas kernels for 0% -> 0%
where the time goes in v5:
time: 435 us
  waiting for transfers between devices  185 us (43%)
  blocking collectives  129 us (30%)
  other arithmetic  46.4 us (11%)
  matrix products  24.2 us (6%)
  local copies, waits for them, and re-layouts  23 us (5%)
  between operations  15.3 us (4%)
  starting transfers between devices  12.3 us (3%)
    ppermute x4, waiting for transfers between devices, local(): got = lax.ppermute(stack, 'dp', [(i, i ^ 1 << b) for i in range(n_dp)])  80.6 us
    psum x1, blocking collectives, local(): slab = lax.psum(slot[:, None] * row[None, :], ('dp', 'tz', 'tx'))  76.5 us
    reduce_scatter x1, waiting for transfers between devices, local(): lax.psum_scatter(grad_part[:, s * hcut:(s + 1) * hcut], 'dp', scatter_dim...  58.7 us
    psum x1, blocking collectives, local(): lax.psum(jnp.dot(weights, active, precision=lax.Precision.HIGHEST), 'dp')  52.2 us
    scatter-add x1, other arithmetic, local(): jnp.zeros((slice_len,), jnp.float32).at[idx]  28.1 us
    psum x1, waiting for transfers between devices, local(): part = lax.psum(part, 'tz')  24.1 us
    all_gather x1, waiting for transfers between devices, local(): hidden = lax.all_gather(part, 'tx', axis=1, tiled=True)  21 us
    ppermute x4, starting transfers between devices, local(): got = lax.ppermute(stack, 'dp', [(i, i ^ 1 << b) for i in range(n_dp)])  12.1 us
  transfers between devices with their start and end apart: 8, of which 7 were waited for; matrix products, arithmetic and copies ran while one was open for 14% of the time, Pallas kernels for 0%

profile of v5, /device:TPU:2, one launch (start us, length us, event | category | flops | bytes accessed | tf_op | source)
XLA Modules:
  0.0 435.0 jit_solution(13029512865388354771)
XLA Ops:
  7.2 0.0 copy-start
  7.2 0.0 reduce-scatter.3.cloned.1.call-start
  7.2 0.5 broadcast_in_dim.49
  7.7 1.0 constant_dynamic-update-slice_fusion.5
  8.7 0.0 copy-start.2
  8.7 7.9 %fusion = bf16[256,8192]{1,0:T(8,128)(2,1)} fusion(bf16[256,512]{1,0:T(8,128)(2,1)} %param.11, bf16[512,8192]{1,0:T(8,128)(2,1)} %param.12, bf16[256,8192]{1,0:T(8,128)(2,1)S(1)} %constant_dynamic-update-slice_fusion.5), kind=kOutput, calls=%fused_computation.7 | convolution fusion | flops 2153775104 | bytes 17039360 | tf_op jit(solution)/shard_map/dot_general | solution.py:49
  16.6 0.0 reduce-scatter.3.cloned.1.call-update
  16.6 0.0 all-reduce.2.cloned.1.call-start
  16.7 0.0 copy-done.2
  16.7 0.0 copy-start.3
  16.7 7.3 %collective-permute-start = (bf16[1,512,512]{2,1,0:T(8,128)(2,1)S(1)}, bf16[1,512,512]{2,1,0:T(8,128)(2,1)S(1)}, u32[]{:S(2)}, u32[]{:S(2)}) collective-permute-start(bf16[1,512,512]{2,1,0:T(8,128)(2,1)S(1)} %bitcast.30), channel_id=1, source_target_pairs={{0,32},{16,48},{32,0},{48,16},{64,96},{80,112},{96,64},{112,80},{1... | collective-permute-start | bytes 1572872 | tf_op jit(solution)/shard_map/ppermute | solution.py:38
  24.0 14.2 %collective-permute-done = bf16[1,512,512]{2,1,0:T(8,128)(2,1)S(1)} collective-permute-done((bf16[1,512,512]{2,1,0:T(8,128)(2,1)S(1)}, bf16[1,512,512]{2,1,0:T(8,128)(2,1)S(1)}, u32[]{:S(2)}, u32[]{:S(2)}) %collective-permute-start) | collective-permute-done | bytes 524320 | tf_op jit(solution)/shard_map/ppermute | solution.py:38
  38.2 0.1 pad_maximum_fusion.2
  38.3 1.7 collective-permute-start.1
  39.9 22.6 %collective-permute-done.1 = bf16[2,512,512]{2,1,0:T(8,128)(2,1)S(1)} collective-permute-done((bf16[2,512,512]{2,1,0:T(8,128)(2,1)S(1)}, bf16[2,512,512]{2,1,0:T(8,128)(2,1)S(1)}, u32[]{:S(2)}, u32[]{:S(2)}) %collective-permute-start.1) | collective-permute-done | bytes 1048608 | tf_op jit(solution)/shard_map/ppermute | solution.py:38
  62.5 1.5 pad_maximum_fusion.1
  64.1 3.2 collective-permute-start.2
  67.3 0.6 reduce-scatter.3.cloned.1.call-done
  67.9 0.0 all-reduce.2.cloned.1.call-update
  67.9 0.0 all-gather.2.cloned.1.call-start
  68.0 43.8 %collective-permute-done.2 = bf16[4,512,512]{2,1,0:T(8,128)(2,1)} collective-permute-done((bf16[4,512,512]{2,1,0:T(8,128)(2,1)}, bf16[4,512,512]{2,1,0:T(8,128)(2,1)}, u32[]{:S(2)}, u32[]{:S(2)}) %collective-permute-start.2) | collective-permute-done | bytes 2097184 | tf_op jit(solution)/shard_map/ppermute | solution.py:38
  111.8 3.4 pad_maximum_fusion
  115.2 0.0 collective-permute-start.3
  115.2 24.1 %all-reduce.2.cloned.1.call-done = bf16[256,2048]{1,0:T(8,128)(2,1)} async-done(((bf16[256,2048]{1,0:T(8,128)(2,1)}), bf16[256,2048]{1,0:T(8,128)(2,1)}) %all-reduce.2.cloned.1.call-update) | async-done | bytes 1048592 | tf_op jit(solution)/shard_map/psum | solution.py:52
  139.3 0.0 all-gather.2.cloned.1.call-update
  139.3 0.0 reduce-scatter.5.cloned.1.call-start
  140.7 0.1 broadcast_bitcast_fusion
  140.8 0.0 copy-done.3
  140.8 0.0 copy-done
  140.9 1.7 gather_fusion.1
  142.6 0.9 constant_dynamic-update-slice_fusion.4
  143.5 0.9 constant_dynamic-update-slice_fusion.3
  144.4 1.0 constant_dynamic-update-slice_fusion.2
  145.5 3.0 constant_dynamic-update-slice_fusion.1
  148.5 0.0 collective-permute-done.3
  148.5 4.4 %constant_dynamic-update-slice_fusion = bf16[16,512,512]{2,1,0:T(8,128)(2,1)} fusion(bf16[16,512,512]{2,1,0:T(8,128)(2,1)} %constant_dynamic-update-slice_fusion.1, bf16[8,512,512]{2,1,0:T(8,128)(2,1)} %collective-permute-done.3), kind=kLoop, calls=%fused_computation.41 | loop fusion | bytes 8388608 | tf_op jit(solution)/shard_map/concatenate | solution.py:39
  152.9 8.6 %gather_fusion = bf16[16,512,512]{2,1,0:T(8,128)(2,1)} fusion(bf16[16,512,512]{2,1,0:T(8,128)(2,1)} %constant_dynamic-update-slice_fusion, s32[1024]{0:T(1024)S(1)} %pad_clamp_fusion.1), kind=kCustom, calls=%fused_computation | custom fusion | bytes 16777280 | tf_op jit(solution)/shard_map/jit(_take)/gather | solution.py:44
  161.5 0.0 copy-start.4
  161.5 7.5 %bitcast_select_fusion = bf16[8192,512]{1,0:T(8,128)(2,1)} fusion(bf16[16,512,512]{2,1,0:T(8,128)(2,1)} %gather_fusion, pred[8192]{0:T(1024)(128)(4,1)S(1)} %bitcast.36), kind=kLoop, calls=%fused_computation.11 | loop fusion | flops 4194304 | bytes 16785408 | tf_op jit(solution)/shard_map/jit(_take)/select_n | solution.py:44
  169.0 21.0 %all-gather.2.cloned.1.call-done = bf16[256,8192]{1,0:T(8,128)(2,1)} async-done(((bf16[256,2048]{1,0:T(8,128)(2,1)}), bf16[256,8192]{1,0:T(8,128)(2,1)}) %all-gather.2.cloned.1.call-update) | async-done | bytes 4194320 | tf_op jit(solution)/shard_map/all_gather | solution.py:53
  190.1 3.1 fusion.1
  193.2 0.0 copy-done.4
  193.2 0.0 copy-start.5
  193.2 7.0 %fusion.5 = f32[256,512]{1,0:T(8,128)S(1)} fusion(bf16[8192,512]{1,0:T(8,128)(2,1)} %bitcast_select_fusion, bf16[256,8192]{1,0:T(8,128)(2,1)} %all-gather.2.cloned.1.call-done, f32[8192]{0:T(1024)S(1)} %copy-done.4, f32[256]{0:T(256)S(1)} %add_rsqrt_fusion), kind=kOutput, calls=%fused_computation.14 | convolution fusion | flops 2155872256 | bytes 13140992 | tf_op jit(solution)/shard_map/dot_general | solution.py:56
  200.2 0.0 copy-done.5
  200.3 0.6 fusion.13
  200.9 0.1 pad_maximum_fusion.3
  201.0 0.1 broadcast_multiply_fusion
  201.0 76.5 %psum.22 = f32[16,514]{1,0:T(8,128)S(1)} all-reduce(f32[16,514]{1,0:T(8,128)S(1)} %broadcast_multiply_fusion), channel_id=1, replica_groups=mesh['dp'=16,'tz'=4,'tx'=4] {'dp','tz','tx'}, use_global_device_ids=true, to_apply=%region_3.4 | all-reduce | flops 8224 | bytes 65792 | tf_op jit(solution)/shard_map/psum | solution.py:71
  277.6 0.2 slice_reduce_fusion.1
  277.7 0.1 select_reduce_fusion.1
  277.8 0.1 fusion.21
  277.9 0.1 fusion.16
  278.1 0.0 copy-start.1
  278.1 8.1 %convolution_convert_fusion = bf16[8192,512]{1,0:T(8,128)(2,1)} fusion(bf16[256,8192]{1,0:T(8,128)(2,1)} %all-gather.2.cloned.1.call-done, f32[8192]{0:T(1024)S(1)} %copy-done.4, f32[256]{0:T(256)S(1)} %add_rsqrt_fusion, f32[256,512]{1,0:T(8,128)S(1)} %fusion.5, f32[512]{0:T(512)S(1)} %copy-done.5, f32[256]{0:T(256)S(1)} %bitcast.40), kind=kOutput, calls=%fused_computation.3 | convolution fusion | flops 2161377280 | bytes 13144064 | tf_op jit(solution)/shard_map/dot_general | solution.py:104
  286.2 0.0 reduce-scatter.5.cloned.1.call-update
  286.3 28.1 %scatter_custom_fusion = f32[8016]{0:T(1024)} fusion(s32[4096]{0:T(1024)S(1)} %bitcast.38, f32[4096]{0:T(1024)S(1)} %bitcast.37, f32[]{:T(128)} %constant.19.clone.1), kind=kCustom, calls=%fused_computation.34 | custom fusion | flops 4096 | bytes 32068 | tf_op jit(solution)/shard_map/scatter-add | solution.py:95
  314.4 0.5 fusion.11
  314.9 52.2 %psum.23 = f32[512]{0:T(512)} all-reduce(f32[512]{0:T(512)S(1)} %bitcast.39), channel_id=1, replica_groups=mesh['dp'=16,'tz'=4,'tx'=4] {'dp'}, use_global_device_ids=true, to_apply=%region_8.9 | all-reduce | flops 512 | bytes 4096 | tf_op jit(solution)/shard_map/psum | solution.py:90
  367.0 0.6 constant_dynamic-slice_fusion.1
  367.6 58.7 %reduce-scatter.5.cloned.1.call-done = bf16[512,512]{1,0:T(8,128)(2,1)} async-done(((bf16[8192,512]{1,0:T(8,128)(2,1)}), bf16[512,512]{1,0:T(8,128)(2,1)}) %reduce-scatter.5.cloned.1.call-update) | async-done | bytes 524304 | tf_op jit(solution)/shard_map/reduce_scatter | solution.py:110
  426.3 2.1 convert_element_type.55
  428.4 0.0 copy-done.1
  (16 shorter events, 0.2 us)
Async XLA Ops:
  7.2 133.7 %copy-start = (f32[128256]{0:T(1024)S(1)}, f32[128256]{0:T(1024)}, u32[]{:S(2)}) copy-start(f32[128256]{0:T(1024)} %param.17) | copy-start | bytes 1539076
  7.2 60.7 %reduce-scatter.3.cloned.1.call-start = ((), (), s32[]{:S(2)}) async-start(), calls=%async_computation.2 | async-start | bytes 5242880 | tf_op jit(solution)/shard_map/reduce_scatter | solution.py:51
  8.7 8.0 %copy-start.2 = (bf16[512,512]{1,0:T(8,128)(2,1)S(1)}, bf16[512,512]{1,0:T(8,128)(2,1)}, u32[]{:S(2)}) copy-start(bf16[512,512]{1,0:T(8,128)(2,1)} %param.15) | copy-start | bytes 1572868
  16.6 122.7 %all-reduce.2.cloned.1.call-start = ((), (), s32[]{:S(2)}) async-start(), calls=%async_computation.3 | async-start | bytes 2097152 | tf_op jit(solution)/shard_map/psum | solution.py:52
  16.7 124.1 %copy-start.3 = (s32[256]{0:T(256)S(1)}, s32[256]{0:T(256)}, u32[]{:S(2)}) copy-start(s32[256]{0:T(256)} %param.10) | copy-start | bytes 3076
  16.7 21.5 %collective-permute-start = (bf16[1,512,512]{2,1,0:T(8,128)(2,1)S(1)}, bf16[1,512,512]{2,1,0:T(8,128)(2,1)S(1)}, u32[]{:S(2)}, u32[]{:S(2)}) collective-permute-start(bf16[1,512,512]{2,1,0:T(8,128)(2,1)S(1)} %bitcast.30), channel_id=1, source_target_pairs={{0,32},{16,48},{32,0},{48,16},{64,96},{80,112},{96,64},{112,80},{1... | collective-permute-start | bytes 1572872 | tf_op jit(solution)/shard_map/ppermute | solution.py:38
  38.3 24.3 %collective-permute-start.1 = (bf16[2,512,512]{2,1,0:T(8,128)(2,1)S(1)}, bf16[2,512,512]{2,1,0:T(8,128)(2,1)S(1)}, u32[]{:S(2)}, u32[]{:S(2)}) collective-permute-start(bf16[2,512,512]{2,1,0:T(8,128)(2,1)S(1)} %pad_maximum_fusion.2), channel_id=1, source_target_pairs={{0,64},{16,80},{32,96},{48,112},{64,0},{80,16},{96,32},{112,48},{1... | collective-permute-start | bytes 3145736 | tf_op jit(solution)/shard_map/ppermute | solution.py:38
  64.1 47.7 %collective-permute-start.2 = (bf16[4,512,512]{2,1,0:T(8,128)(2,1)}, bf16[4,512,512]{2,1,0:T(8,128)(2,1)}, u32[]{:S(2)}, u32[]{:S(2)}) collective-permute-start(bf16[4,512,512]{2,1,0:T(8,128)(2,1)} %pad_maximum_fusion.1), channel_id=1, source_target_pairs={{0,128},{16,144},{32,160},{48,176},{64,192},{80,208},{96,224},{112... | collective-permute-start | bytes 6291464 | tf_op jit(solution)/shard_map/ppermute | solution.py:38
  67.9 122.2 %all-gather.2.cloned.1.call-start = ((), (), s32[]{:S(2)}) async-start(), calls=%async_computation.4 | async-start | bytes 5242880 | tf_op jit(solution)/shard_map/all_gather | solution.py:53
  115.2 33.3 %collective-permute-start.3 = (bf16[8,512,512]{2,1,0:T(8,128)(2,1)}, bf16[8,512,512]{2,1,0:T(8,128)(2,1)}, u32[]{:S(2)}, u32[]{:S(2)}) collective-permute-start(bf16[8,512,512]{2,1,0:T(8,128)(2,1)} %pad_maximum_fusion), channel_id=1, source_target_pairs={{0,16},{16,0},{32,48},{48,32},{64,80},{80,64},{96,112},{112,96},{1... | collective-permute-start | bytes 12582920 | tf_op jit(solution)/shard_map/ppermute | solution.py:38
  139.3 286.9 %reduce-scatter.5.cloned.1.call-start = ((), (), s32[]{:S(2)}) async-start(), calls=%async_computation.5 | async-start | bytes 8912896 | tf_op jit(solution)/shard_map/reduce_scatter | solution.py:110
  161.5 31.7 %copy-start.4 = (f32[8192]{0:T(1024)S(1)}, f32[8192]{0:T(1024)}, u32[]{:S(2)}) copy-start(f32[8192]{0:T(1024)} %param.14) | copy-start | bytes 98308
  193.2 7.1 %copy-start.5 = (f32[512]{0:T(512)S(1)}, f32[512]{0:T(512)}, u32[]{:S(2)}) copy-start(f32[512]{0:T(512)} %param.16) | copy-start | bytes 6148
  278.1 150.4 %copy-start.1 = (f32[128256]{0:T(1024)S(1)}, f32[128256]{0:T(1024)}, u32[]{:S(2)}) copy-start(f32[128256]{0:T(1024)} %param.17) | copy-start | bytes 1539076
Sparse Core Ops, SparseCore 0:
  16.8 51.0 reduce-scatter.2
  70.6 68.7 all-reduce.1
  141.1 48.9 all-gather.1
  286.4 139.8 reduce-scatter.4

commit v6 on v5

--- a/solution.py
+++ b/solution.py
@@ -104,16 +104,22 @@
     grad_part = lax.dot_general(
         normed, d_pre, contract, preferred_element_type=jnp.float32
     ).astype(jnp.bfloat16)
-    hcut = grad_part.shape[1] // SPLITS
-    grad_in = jnp.concatenate(
-        [
-            lax.psum_scatter(
-                grad_part[:, s * hcut:(s + 1) * hcut], "dp", scatter_dimension=0, tiled=True
-            )
-            for s in range(SPLITS)
-        ],
-        axis=1,
-    ).astype(jnp.float32)
+    cols = grad_part.shape[1] // 2
+    native = lax.psum_scatter(grad_part[:, :cols], "dp", scatter_dimension=0, tiled=True)
+    n_bits = n_dp.bit_length() - 1
+    acc = grad_part[:, cols:].astype(jnp.float32).reshape((2,) * n_bits + (-1, cols))
+    left = list(range(n_bits - 1, -1, -1))
+    for b in (0, 2, 3, 1):
+        axis = left.index(b)
+        left.remove(b)
+        mine = (r >> b) & 1
+        keep = lax.dynamic_index_in_dim(acc, mine, axis=axis, keepdims=False)
+        send = lax.dynamic_index_in_dim(acc, 1 - mine, axis=axis, keepdims=False)
+        got = lax.ppermute(
+            send.astype(jnp.bfloat16), "dp", [(i, i ^ (1 << b)) for i in range(n_dp)]
+        )
+        acc = keep + got.astype(jnp.float32)
+    grad_in = jnp.concatenate([native.astype(jnp.float32), acc], axis=1)
     return (twist_vals, grad_in, grad_out, grad_bias)
 
 

time: 435 us -> 436 us (level)
  waiting for transfers between devices: 185 us -> 160 us
  other arithmetic: 46.4 us -> 58 us
  local copies, waits for them, and re-layouts: 23 us -> 33.7 us
    reduce_scatter x1, waiting for transfers between devices: 58.7 us -> 0.02 us  [local(): lax.psum_scatter(grad_part[:, :cols], 'dp', scatter_dimension=0, tiled=True)]
    ppermute x0 -> x4, waiting for transfers between devices: none -> 33.1 us  [local(): lax.ppermute(send.astype(jnp.bfloat16), 'dp', [(i, i ^ 1 << b) for i in r...]
    add x0 -> x4, other arithmetic: none -> 8.01 us  [local(): acc = keep + got.astype(jnp.float32)]
    unnamed x20 -> x34, local copies, waits for them, and re-layouts: 6.01 us -> 13.7 us
  transfers between devices with their start and end apart: 8 -> 12, of which waited for: 7 -> 7; matrix products, arithmetic and copies ran while one was open for 14% -> 17% of each run, Pallas kernels for 0% -> 0%
where the time goes in v6:
time: 436 us; the launch traced here: 433 us
  waiting for transfers between devices  160 us (37%)
  blocking collectives  132 us (30%)
  other arithmetic  58 us (13%)
  local copies, waits for them, and re-layouts  33.7 us (8%)
  matrix products  20.6 us (5%)
  between operations  15.5 us (4%)
  starting transfers between devices  13.9 us (3%)
    ppermute x4, waiting for transfers between devices, local(): got = lax.ppermute(stack, 'dp', [(i, i ^ 1 << b) for i in range(n_dp)])  81.2 us
    psum x1, blocking collectives, local(): slab = lax.psum(slot[:, None] * row[None, :], ('dp', 'tz', 'tx'))  76.5 us
    psum x1, blocking collectives, local(): lax.psum(jnp.dot(weights, active, precision=lax.Precision.HIGHEST), 'dp')  55.8 us
    ppermute x4, waiting for transfers between devices, local(): lax.ppermute(send.astype(jnp.bfloat16), 'dp', [(i, i ^ 1 << b) for i in r...  33.1 us
    scatter-add x1, other arithmetic, local(): jnp.zeros((slice_len,), jnp.float32).at[idx]  28.4 us
    psum x1, waiting for transfers between devices, local(): part = lax.psum(part, 'tz')  24.1 us
    all_gather x1, waiting for transfers between devices, local(): hidden = lax.all_gather(part, 'tx', axis=1, tiled=True)  21.1 us
    unnamed x34, local copies, waits for them, and re-layouts  13.7 us
  transfers between devices with their start and end apart: 12, of which 7 were waited for; matrix products, arithmetic and copies ran while one was open for 17% of the time, Pallas kernels for 0%

profile of v6, /device:TPU:2, one launch (start us, length us, event | category | flops | bytes accessed | tf_op | source)
XLA Modules:
  0.0 433.4 jit_solution(34055352258375199)
XLA Ops:
  7.2 0.0 reduce-scatter.3.cloned.1.call-start
  7.3 0.5 broadcast_in_dim.49
  7.7 0.5 copy-done.7
  8.2 0.1 copy-done.9
  8.3 7.8 %fusion = bf16[256,8192]{1,0:T(8,128)(2,1)} fusion(bf16[256,512]{1,0:T(8,128)(2,1)S(1)} %copy-done.9, bf16[512,8192]{1,0:T(8,128)(2,1)} %param.12, bf16[256,8192]{1,0:T(8,128)(2,1)S(1)} %constant_dynamic-update-slice_fusion.5), kind=kOutput, calls=%fused_computation.7 | convolution fusion | flops 2153775104 | bytes 17039360 | tf_op jit(solution)/shard_map/dot_general | solution.py:49
  16.1 0.0 all-reduce.2.cloned.1.call-start
  16.1 1.0 copy-done.4
  17.1 7.2 %collective-permute-start = (bf16[1,512,512]{2,1,0:T(8,128)(2,1)S(1)}, bf16[1,512,512]{2,1,0:T(8,128)(2,1)S(1)}, u32[]{:S(2)}, u32[]{:S(2)}) collective-permute-start(bf16[1,512,512]{2,1,0:T(8,128)(2,1)S(1)} %bitcast.49), channel_id=1, source_target_pairs={{0,32},{16,48},{32,0},{48,16},{64,96},{80,112},{96,64},{112,80},{1... | collective-permute-start | bytes 1572872 | tf_op jit(solution)/shard_map/ppermute | solution.py:38
  24.3 14.2 %collective-permute-done = bf16[1,512,512]{2,1,0:T(8,128)(2,1)S(1)} collective-permute-done((bf16[1,512,512]{2,1,0:T(8,128)(2,1)S(1)}, bf16[1,512,512]{2,1,0:T(8,128)(2,1)S(1)}, u32[]{:S(2)}, u32[]{:S(2)}) %collective-permute-start) | collective-permute-done | bytes 524320 | tf_op jit(solution)/shard_map/ppermute | solution.py:38
  38.5 0.1 pad_maximum_fusion.2
  38.6 1.7 collective-permute-start.1
  40.2 22.6 %collective-permute-done.1 = bf16[2,512,512]{2,1,0:T(8,128)(2,1)S(1)} collective-permute-done((bf16[2,512,512]{2,1,0:T(8,128)(2,1)S(1)}, bf16[2,512,512]{2,1,0:T(8,128)(2,1)S(1)}, u32[]{:S(2)}, u32[]{:S(2)}) %collective-permute-start.1) | collective-permute-done | bytes 1048608 | tf_op jit(solution)/shard_map/ppermute | solution.py:38
  62.8 1.5 pad_maximum_fusion.1
  64.3 3.2 collective-permute-start.2
  67.6 44.4 %collective-permute-done.2 = bf16[4,512,512]{2,1,0:T(8,128)(2,1)} collective-permute-done((bf16[4,512,512]{2,1,0:T(8,128)(2,1)}, bf16[4,512,512]{2,1,0:T(8,128)(2,1)}, u32[]{:S(2)}, u32[]{:S(2)}) %collective-permute-start.2) | collective-permute-done | bytes 2097184 | tf_op jit(solution)/shard_map/ppermute | solution.py:38
  112.0 3.4 pad_maximum_fusion
  115.5 24.1 %all-reduce.2.cloned.1.call-done = bf16[256,2048]{1,0:T(8,128)(2,1)} async-done(((bf16[256,2048]{1,0:T(8,128)(2,1)}), bf16[256,2048]{1,0:T(8,128)(2,1)}) %all-reduce.2.cloned.1.call-update) | async-done | bytes 1048592 | tf_op jit(solution)/shard_map/psum | solution.py:52
  139.6 0.0 reduce-scatter.5.cloned.1.call-start
  141.0 0.1 broadcast_bitcast_fusion
  141.1 1.7 gather_fusion.1
  142.9 0.9 constant_dynamic-update-slice_fusion.4
  143.8 0.9 constant_dynamic-update-slice_fusion.3
  144.6 1.0 constant_dynamic-update-slice_fusion.2
  145.7 3.0 constant_dynamic-update-slice_fusion.1
  148.7 4.4 %constant_dynamic-update-slice_fusion = bf16[16,512,512]{2,1,0:T(8,128)(2,1)} fusion(bf16[16,512,512]{2,1,0:T(8,128)(2,1)} %constant_dynamic-update-slice_fusion.1, bf16[8,512,512]{2,1,0:T(8,128)(2,1)} %collective-permute-done.3), kind=kLoop, calls=%fused_computation.54 | loop fusion | bytes 8388608 | tf_op jit(solution)/shard_map/concatenate | solution.py:39
  153.1 8.6 %gather_fusion = bf16[16,512,512]{2,1,0:T(8,128)(2,1)} fusion(bf16[16,512,512]{2,1,0:T(8,128)(2,1)} %constant_dynamic-update-slice_fusion, s32[1024]{0:T(1024)S(1)} %pad_clamp_fusion.1), kind=kCustom, calls=%fused_computation | custom fusion | bytes 16777280 | tf_op jit(solution)/shard_map/jit(_take)/gather | solution.py:44
  161.8 7.5 %bitcast_select_fusion = bf16[8192,512]{1,0:T(8,128)(2,1)} fusion(bf16[16,512,512]{2,1,0:T(8,128)(2,1)} %gather_fusion, pred[8192]{0:T(1024)(128)(4,1)S(1)} %bitcast.55), kind=kLoop, calls=%fused_computation.11 | loop fusion | flops 4194304 | bytes 16785408 | tf_op jit(solution)/shard_map/jit(_take)/select_n | solution.py:44
  169.2 21.1 %all-gather.2.cloned.1.call-done = bf16[256,8192]{1,0:T(8,128)(2,1)} async-done(((bf16[256,2048]{1,0:T(8,128)(2,1)}), bf16[256,8192]{1,0:T(8,128)(2,1)}) %all-gather.2.cloned.1.call-update) | async-done | bytes 4194320 | tf_op jit(solution)/shard_map/all_gather | solution.py:53
  190.3 3.3 fusion.1
  193.6 0.2 copy-done.5
  193.8 5.8 %fusion.6 = f32[256,512]{1,0:T(8,128)S(1)} fusion(bf16[8192,512]{1,0:T(8,128)(2,1)} %bitcast_select_fusion, bf16[256,8192]{1,0:T(8,128)(2,1)S(1)} %copy-done.5, f32[8192]{0:T(1024)S(1)} %copy-done.10, f32[256]{0:T(256)S(1)} %add_rsqrt_fusion), kind=kOutput, calls=%fused_computation.19 | convolution fusion | flops 2155872256 | bytes 13140992 | tf_op jit(solution)/shard_map/dot_general | solution.py:56
  199.7 0.6 fusion.17
  200.3 0.1 pad_maximum_fusion.4
  200.4 0.1 broadcast_multiply_fusion
  200.4 76.5 %psum.22 = f32[16,514]{1,0:T(8,128)S(1)} all-reduce(f32[16,514]{1,0:T(8,128)S(1)} %broadcast_multiply_fusion), channel_id=1, replica_groups=mesh['dp'=16,'tz'=4,'tx'=4] {'dp','tz','tx'}, use_global_device_ids=true, to_apply=%region_3.4 | all-reduce | flops 8224 | bytes 65792 | tf_op jit(solution)/shard_map/psum | solution.py:71
  276.9 0.2 slice_reduce_fusion.1
  277.1 0.1 select_reduce_fusion.1
  277.2 0.1 fusion.25
  277.3 0.1 fusion.20
  277.4 4.9 %convolution_convert_fusion = bf16[8192,512]{1,0:T(8,128)(2,1)S(1)} fusion(bf16[256,8192]{1,0:T(8,128)(2,1)} %all-gather.2.cloned.1.call-done, f32[8192]{0:T(1024)S(1)} %copy-done.10, f32[256]{0:T(256)S(1)} %add_rsqrt_fusion, f32[256,512]{1,0:T(8,128)S(1)} %fusion.6, f32[512]{0:T(512)S(1)} %copy-done.11, f32[256]{0:T(256)S(1)} %bitcast.59), kind=kOutput, calls=%fused_computation.3 | convolution fusion | flops 2161377280 | bytes 13144064 | tf_op jit(solution)/shard_map/dot_general | solution.py:104
  282.3 3.5 fusion.31
  285.8 3.1 convert.1
  288.9 3.2 copy-done.2
  292.2 0.2 fusion.4
  292.4 0.1 collective-permute-start.4
  292.5 5.0 %collective-permute-done.4 = bf16[2,2,2,512,256]{4,3,2,0,1:T(8,128)(2,1)} collective-permute-done((bf16[2,2,2,512,256]{4,3,2,0,1:T(8,128)(2,1)S(1)}, bf16[2,2,2,512,256]{4,3,2,0,1:T(8,128)(2,1)}, u32[]{:S(2)}, u32[]{:S(2)}) %collective-permute-start.4) | collective-permute-done | bytes 2097184 | tf_op jit(solution)/shard_map/ppermute | solution.py:118
  297.5 3.5 bitcast_add_fusion
  301.1 1.9 copy-done.3
  303.0 0.1 fusion.8
  303.1 0.1 collective-permute-start.5
  303.3 28.1 %collective-permute-done.5 = bf16[2,2,512,256]{3,2,1,0:T(8,128)(2,1)} collective-permute-done((bf16[2,2,512,256]{3,2,1,0:T(8,128)(2,1)S(1)}, bf16[2,2,512,256]{3,2,1,0:T(8,128)(2,1)}, u32[]{:S(2)}, u32[]{:S(2)}) %collective-permute-start.5) | collective-permute-done | bytes 1048608 | tf_op jit(solution)/shard_map/ppermute | solution.py:118
  331.3 2.2 bitcast_add_fusion.1
  333.5 0.1 fusion.9
  333.6 1.4 collective-permute-start.6
  335.0 28.4 %scatter_custom_fusion = f32[8016]{0:T(1024)} fusion(s32[4096]{0:T(1024)S(1)} %bitcast.57, f32[4096]{0:T(1024)S(1)} %bitcast.56, f32[]{:T(128)} %constant.95.clone.1), kind=kCustom, calls=%fused_computation.47 | custom fusion | flops 4096 | bytes 32068 | tf_op jit(solution)/shard_map/scatter-add | solution.py:95
  363.4 1.2 bitcast_add_fusion.2
  364.6 1.0 copy-done.6
  365.6 0.1 collective-permute-start.7
  365.7 1.5 fusion.15
  367.2 55.8 %psum.23 = f32[512]{0:T(512)} all-reduce(f32[512]{0:T(512)S(1)} %bitcast.58), channel_id=1, replica_groups=mesh['dp'=16,'tz'=4,'tx'=4] {'dp'}, use_global_device_ids=true, to_apply=%region_8.9 | all-reduce | flops 512 | bytes 4096 | tf_op jit(solution)/shard_map/psum | solution.py:90
  423.0 0.6 constant_dynamic-slice_fusion.3
  423.6 1.1 bitcast_add_fusion.3
  424.7 1.0 convert_element_type.92
  425.7 1.1 pad_maximum_fusion.3
  (48 shorter events, 0.4 us)
Async XLA Ops:
  7.2 133.9 %copy-start = (f32[128256]{0:T(1024)S(1)}, f32[128256]{0:T(1024)}, u32[]{:S(2)}) copy-start(f32[128256]{0:T(1024)} %param.17) | copy-start | bytes 1539076
  7.2 1.0 copy-start.7
  7.2 1.1 copy-start.9
  7.2 60.3 %reduce-scatter.3.cloned.1.call-start = ((), (), s32[]{:S(2)}) async-start(), calls=%async_computation.2 | async-start | bytes 5242880 | tf_op jit(solution)/shard_map/reduce_scatter | solution.py:51
  16.0 1.0 copy-start.4
  16.1 123.5 %all-reduce.2.cloned.1.call-start = ((), (), s32[]{:S(2)}) async-start(), calls=%async_computation.3 | async-start | bytes 2097152 | tf_op jit(solution)/shard_map/psum | solution.py:52
  17.1 21.4 %collective-permute-start = (bf16[1,512,512]{2,1,0:T(8,128)(2,1)S(1)}, bf16[1,512,512]{2,1,0:T(8,128)(2,1)S(1)}, u32[]{:S(2)}, u32[]{:S(2)}) collective-permute-start(bf16[1,512,512]{2,1,0:T(8,128)(2,1)S(1)} %bitcast.49), channel_id=1, source_target_pairs={{0,32},{16,48},{32,0},{48,16},{64,96},{80,112},{96,64},{112,80},{1... | collective-permute-start | bytes 1572872 | tf_op jit(solution)/shard_map/ppermute | solution.py:38
  38.6 24.3 %collective-permute-start.1 = (bf16[2,512,512]{2,1,0:T(8,128)(2,1)S(1)}, bf16[2,512,512]{2,1,0:T(8,128)(2,1)S(1)}, u32[]{:S(2)}, u32[]{:S(2)}) collective-permute-start(bf16[2,512,512]{2,1,0:T(8,128)(2,1)S(1)} %pad_maximum_fusion.2), channel_id=1, source_target_pairs={{0,64},{16,80},{32,96},{48,112},{64,0},{80,16},{96,32},{112,48},{1... | collective-permute-start | bytes 3145736 | tf_op jit(solution)/shard_map/ppermute | solution.py:38
  64.3 47.7 %collective-permute-start.2 = (bf16[4,512,512]{2,1,0:T(8,128)(2,1)}, bf16[4,512,512]{2,1,0:T(8,128)(2,1)}, u32[]{:S(2)}, u32[]{:S(2)}) collective-permute-start(bf16[4,512,512]{2,1,0:T(8,128)(2,1)} %pad_maximum_fusion.1), channel_id=1, source_target_pairs={{0,128},{16,144},{32,160},{48,176},{64,192},{80,208},{96,224},{112... | collective-permute-start | bytes 6291464 | tf_op jit(solution)/shard_map/ppermute | solution.py:38
  67.5 73.5 %copy-start.8 = (s32[256]{0:T(256)S(1)}, s32[256]{0:T(256)}, u32[]{:S(2)}) copy-start(s32[256]{0:T(256)} %param.10) | copy-start | bytes 3076
  67.6 122.8 %all-gather.2.cloned.1.call-start = ((), (), s32[]{:S(2)}) async-start(), calls=%async_computation.4 | async-start | bytes 5242880 | tf_op jit(solution)/shard_map/all_gather | solution.py:53
  115.5 33.2 %collective-permute-start.3 = (bf16[8,512,512]{2,1,0:T(8,128)(2,1)}, bf16[8,512,512]{2,1,0:T(8,128)(2,1)}, u32[]{:S(2)}, u32[]{:S(2)}) collective-permute-start(bf16[8,512,512]{2,1,0:T(8,128)(2,1)} %pad_maximum_fusion), channel_id=1, source_target_pairs={{0,16},{16,0},{32,48},{48,32},{64,80},{80,64},{96,112},{112,96},{1... | collective-permute-start | bytes 12582920 | tf_op jit(solution)/shard_map/ppermute | solution.py:38
  139.6 285.1 %reduce-scatter.5.cloned.1.call-start = ((), (), s32[]{:S(2)}) async-start(), calls=%async_computation.5 | async-start | bytes 4456448 | tf_op jit(solution)/shard_map/reduce_scatter | solution.py:108
  161.8 31.8 %copy-start.10 = (f32[8192]{0:T(1024)S(1)}, f32[8192]{0:T(1024)}, u32[]{:S(2)}) copy-start(f32[8192]{0:T(1024)} %param.14) | copy-start | bytes 98308
  190.3 3.4 copy-start.5
  193.8 5.9 %copy-start.11 = (f32[512]{0:T(512)S(1)}, f32[512]{0:T(512)}, u32[]{:S(2)}) copy-start(f32[512]{0:T(512)} %param.16) | copy-start | bytes 6148
  199.6 82.7 %copy-start.12 = (f32[256,512]{1,0:T(8,128)}, f32[256,512]{1,0:T(8,128)S(1)}, u32[]{:S(2)}) copy-start(f32[256,512]{1,0:T(8,128)S(1)} %fusion.6) | copy-start | bytes 1572868
  288.9 3.2 copy-start.2
  292.4 5.1 %collective-permute-start.4 = (bf16[2,2,2,512,256]{4,3,2,0,1:T(8,128)(2,1)S(1)}, bf16[2,2,2,512,256]{4,3,2,0,1:T(8,128)(2,1)}, u32[]{:S(2)}, u32[]{:S(2)}) collective-permute-start(bf16[2,2,2,512,256]{4,3,2,0,1:T(8,128)(2,1)S(1)} %fusion.4), channel_id=1, source_target_pairs={{0,16},{16,0},{32,48},{48,32},{64,80},{80,64},{96,112},{112,96},{1... | collective-permute-start | bytes 6291464 | tf_op jit(solution)/shard_map/ppermute | solution.py:118
  301.1 1.9 copy-start.3
  303.1 28.2 %collective-permute-start.5 = (bf16[2,2,512,256]{3,2,1,0:T(8,128)(2,1)S(1)}, bf16[2,2,512,256]{3,2,1,0:T(8,128)(2,1)}, u32[]{:S(2)}, u32[]{:S(2)}) collective-permute-start(bf16[2,2,512,256]{3,2,1,0:T(8,128)(2,1)S(1)} %fusion.8), channel_id=1, source_target_pairs={{0,64},{16,80},{32,96},{48,112},{64,0},{80,16},{96,32},{112,48},{1... | collective-permute-start | bytes 3145736 | tf_op jit(solution)/shard_map/ppermute | solution.py:118
  333.6 29.9 %collective-permute-start.6 = (bf16[2,512,256]{2,1,0:T(8,128)(2,1)S(1)}, bf16[2,512,256]{2,1,0:T(8,128)(2,1)}, u32[]{:S(2)}, u32[]{:S(2)}) collective-permute-start(bf16[2,512,256]{2,1,0:T(8,128)(2,1)S(1)} %fusion.9), channel_id=1, source_target_pairs={{0,128},{16,144},{32,160},{48,176},{64,192},{80,208},{96,224},{112... | collective-permute-start | bytes 1572872 | tf_op jit(solution)/shard_map/ppermute | solution.py:118
  335.0 91.8 %copy-start.1 = (f32[128256]{0:T(1024)S(1)}, f32[128256]{0:T(1024)}, u32[]{:S(2)}) copy-start(f32[128256]{0:T(1024)} %param.17) | copy-start | bytes 1539076
  364.6 1.0 copy-start.6
  365.6 58.0 %collective-permute-start.7 = (bf16[512,256]{1,0:T(8,128)(2,1)S(1)}, bf16[512,256]{1,0:T(8,128)(2,1)S(1)}, u32[]{:S(2)}, u32[]{:S(2)}) collective-permute-start(bf16[512,256]{1,0:T(8,128)(2,1)S(1)} %fusion.11), channel_id=1, source_target_pairs={{0,32},{16,48},{32,0},{48,16},{64,96},{80,112},{96,64},{112,80},{1... | collective-permute-start | bytes 786440 | tf_op jit(solution)/shard_map/ppermute | solution.py:118
Sparse Core Ops, SparseCore 0:
  16.2 51.0 reduce-scatter.2
  70.0 69.5 all-reduce.1
  141.4 48.9 all-gather.1
  286.0 106.2 reduce-scatter.4

commit v7 on v6

--- a/solution.py
+++ b/solution.py
@@ -87,7 +87,11 @@
     twist_vals = lax.dynamic_index_in_dim(grid, r, axis=0, keepdims=False)
     weights = lax.dynamic_index_in_dim(weights_all, r, axis=0, keepdims=False)
 
-    grad_out = lax.psum(jnp.dot(weights, active, precision=lax.Precision.HIGHEST), "dp")
+    grad_out = jnp.dot(weights, active, precision=lax.Precision.HIGHEST)
+    for b in (0, 2, 3, 1):
+        grad_out = grad_out + lax.ppermute(
+            grad_out, "dp", [(i, i ^ (1 << b)) for i in range(n_dp)]
+        )
 
     slice_len = vocab_size // n_dp
     idx = ids_all.reshape(-1) - r * slice_len

time: 436 us -> 406 us (0.931)
  blocking collectives: 132 us -> 76.5 us
  waiting for transfers between devices: 160 us -> 177 us
  starting transfers between devices: 13.9 us -> 24.5 us
    psum x1 -> x0, blocking collectives: 55.8 us -> none  [local(): lax.psum(jnp.dot(weights, active, precision=lax.Precision.HIGHEST), 'dp')]
    reduce_scatter x1, waiting for transfers between devices: 0.02 us -> 11.2 us  [local(): lax.psum_scatter(grad_part[:, :cols], 'dp', scatter_dimension=0, tiled=True)]
    ppermute x0 -> x4, waiting for transfers between devices: none -> 10.1 us  [local(): lax.ppermute(grad_out, 'dp', [(i, i ^ 1 << b) for i in range(n_dp)])]
    ppermute x4, starting transfers between devices: 1.68 us -> 8.16 us  [local(): lax.ppermute(send.astype(jnp.bfloat16), 'dp', [(i, i ^ 1 << b) for i in r...]
    unnamed x34 -> x32, local copies, waits for them, and re-layouts: 13.7 us -> 10.5 us
  transfers between devices with their start and end apart: 12 -> 16, of which waited for: 7 -> 10; matrix products, arithmetic and copies ran while one was open for 17% -> 18% of each run, Pallas kernels for 0% -> 0%
where the time goes in v7:
time: 406 us; the launch traced here: 405 us
  waiting for transfers between devices  177 us (44%)
  blocking collectives  76.5 us (19%)
  other arithmetic  59.3 us (15%)
  local copies, waits for them, and re-layouts  31.4 us (8%)
  starting transfers between devices  24.5 us (6%)
  matrix products  20.6 us (5%)
  between operations  15.4 us (4%)
    ppermute x4, waiting for transfers between devices, local(): got = lax.ppermute(stack, 'dp', [(i, i ^ 1 << b) for i in range(n_dp)])  81.2 us
    psum x1, blocking collectives, local(): slab = lax.psum(slot[:, None] * row[None, :], ('dp', 'tz', 'tx'))  76.5 us
    ppermute x4, waiting for transfers between devices, local(): lax.ppermute(send.astype(jnp.bfloat16), 'dp', [(i, i ^ 1 << b) for i in r...  29.5 us
    scatter-add x1, other arithmetic, local(): jnp.zeros((slice_len,), jnp.float32).at[idx]  28.2 us
    psum x1, waiting for transfers between devices, local(): part = lax.psum(part, 'tz')  24.1 us
    all_gather x1, waiting for transfers between devices, local(): hidden = lax.all_gather(part, 'tx', axis=1, tiled=True)  21.1 us
    ppermute x4, starting transfers between devices, local(): got = lax.ppermute(stack, 'dp', [(i, i ^ 1 << b) for i in range(n_dp)])  12 us
    reduce_scatter x1, waiting for transfers between devices, local(): lax.psum_scatter(grad_part[:, :cols], 'dp', scatter_dimension=0, tiled=True)  11.2 us
  transfers between devices with their start and end apart: 16, of which 10 were waited for; matrix products, arithmetic and copies ran while one was open for 18% of the time, Pallas kernels for 0%

profile of v7, /device:TPU:2, one launch (start us, length us, event | category | flops | bytes accessed | tf_op | source)
XLA Modules:
  0.0 405.1 jit_solution(12243759462785066182)
XLA Ops:
  7.3 0.5 broadcast_in_dim.49
  7.7 0.5 copy-done.6
  8.3 7.8 %fusion = bf16[256,8192]{1,0:T(8,128)(2,1)} fusion(bf16[256,512]{1,0:T(8,128)(2,1)S(1)} %copy-done.8, bf16[512,8192]{1,0:T(8,128)(2,1)} %param.12, bf16[256,8192]{1,0:T(8,128)(2,1)S(1)} %constant_dynamic-update-slice_fusion.5), kind=kOutput, calls=%fused_computation.7 | convolution fusion | flops 2153775104 | bytes 17039360 | tf_op jit(solution)/shard_map/dot_general | solution.py:49
  16.1 1.0 copy-done.3
  17.1 7.2 %collective-permute-start = (bf16[1,512,512]{2,1,0:T(8,128)(2,1)S(1)}, bf16[1,512,512]{2,1,0:T(8,128)(2,1)S(1)}, u32[]{:S(2)}, u32[]{:S(2)}) collective-permute-start(bf16[1,512,512]{2,1,0:T(8,128)(2,1)S(1)} %bitcast.49), channel_id=1, source_target_pairs={{0,32},{16,48},{32,0},{48,16},{64,96},{80,112},{96,64},{112,80},{1... | collective-permute-start | bytes 1572872 | tf_op jit(solution)/shard_map/ppermute | solution.py:38
  24.3 14.2 %collective-permute-done = bf16[1,512,512]{2,1,0:T(8,128)(2,1)S(1)} collective-permute-done((bf16[1,512,512]{2,1,0:T(8,128)(2,1)S(1)}, bf16[1,512,512]{2,1,0:T(8,128)(2,1)S(1)}, u32[]{:S(2)}, u32[]{:S(2)}) %collective-permute-start) | collective-permute-done | bytes 524320 | tf_op jit(solution)/shard_map/ppermute | solution.py:38
  38.5 0.1 pad_maximum_fusion.2
  38.6 1.7 collective-permute-start.1
  40.2 22.6 %collective-permute-done.1 = bf16[2,512,512]{2,1,0:T(8,128)(2,1)S(1)} collective-permute-done((bf16[2,512,512]{2,1,0:T(8,128)(2,1)S(1)}, bf16[2,512,512]{2,1,0:T(8,128)(2,1)S(1)}, u32[]{:S(2)}, u32[]{:S(2)}) %collective-permute-start.1) | collective-permute-done | bytes 1048608 | tf_op jit(solution)/shard_map/ppermute | solution.py:38
  62.8 1.5 pad_maximum_fusion.1
  64.3 3.2 collective-permute-start.2
  67.6 44.4 %collective-permute-done.2 = bf16[4,512,512]{2,1,0:T(8,128)(2,1)} collective-permute-done((bf16[4,512,512]{2,1,0:T(8,128)(2,1)}, bf16[4,512,512]{2,1,0:T(8,128)(2,1)}, u32[]{:S(2)}, u32[]{:S(2)}) %collective-permute-start.2) | collective-permute-done | bytes 2097184 | tf_op jit(solution)/shard_map/ppermute | solution.py:38
  112.1 3.4 pad_maximum_fusion
  115.5 24.1 %all-reduce.2.cloned.1.call-done = bf16[256,2048]{1,0:T(8,128)(2,1)} async-done(((bf16[256,2048]{1,0:T(8,128)(2,1)}), bf16[256,2048]{1,0:T(8,128)(2,1)}) %all-reduce.2.cloned.1.call-update) | async-done | bytes 1048592 | tf_op jit(solution)/shard_map/psum | solution.py:52
  141.0 0.1 broadcast_bitcast_fusion
  141.1 1.7 gather_fusion.1
  142.9 0.9 constant_dynamic-update-slice_fusion.4
  143.8 0.9 constant_dynamic-update-slice_fusion.3
  144.6 1.0 constant_dynamic-update-slice_fusion.2
  145.7 3.0 constant_dynamic-update-slice_fusion.1
  148.7 4.4 %constant_dynamic-update-slice_fusion = bf16[16,512,512]{2,1,0:T(8,128)(2,1)} fusion(bf16[16,512,512]{2,1,0:T(8,128)(2,1)} %constant_dynamic-update-slice_fusion.1, bf16[8,512,512]{2,1,0:T(8,128)(2,1)} %collective-permute-done.3), kind=kLoop, calls=%fused_computation.54 | loop fusion | bytes 8388608 | tf_op jit(solution)/shard_map/concatenate | solution.py:39
  153.1 8.7 %gather_fusion = bf16[16,512,512]{2,1,0:T(8,128)(2,1)} fusion(bf16[16,512,512]{2,1,0:T(8,128)(2,1)} %constant_dynamic-update-slice_fusion, s32[1024]{0:T(1024)S(1)} %pad_clamp_fusion.1), kind=kCustom, calls=%fused_computation | custom fusion | bytes 16777280 | tf_op jit(solution)/shard_map/jit(_take)/gather | solution.py:44
  161.8 7.5 %bitcast_select_fusion = bf16[8192,512]{1,0:T(8,128)(2,1)} fusion(bf16[16,512,512]{2,1,0:T(8,128)(2,1)} %gather_fusion, pred[8192]{0:T(1024)(128)(4,1)S(1)} %bitcast.55), kind=kLoop, calls=%fused_computation.11 | loop fusion | flops 4194304 | bytes 16785408 | tf_op jit(solution)/shard_map/jit(_take)/select_n | solution.py:44
  169.2 21.1 %all-gather.2.cloned.1.call-done = bf16[256,8192]{1,0:T(8,128)(2,1)} async-done(((bf16[256,2048]{1,0:T(8,128)(2,1)}), bf16[256,8192]{1,0:T(8,128)(2,1)}) %all-gather.2.cloned.1.call-update) | async-done | bytes 4194320 | tf_op jit(solution)/shard_map/all_gather | solution.py:53
  190.3 3.3 fusion.1
  193.6 0.2 copy-done.4
  193.8 5.8 %fusion.6 = f32[256,512]{1,0:T(8,128)S(1)} fusion(bf16[8192,512]{1,0:T(8,128)(2,1)} %bitcast_select_fusion, bf16[256,8192]{1,0:T(8,128)(2,1)S(1)} %copy-done.4, f32[8192]{0:T(1024)S(1)} %copy-done.9, f32[256]{0:T(256)S(1)} %add_rsqrt_fusion), kind=kOutput, calls=%fused_computation.19 | convolution fusion | flops 2155872256 | bytes 13140992 | tf_op jit(solution)/shard_map/dot_general | solution.py:56
  199.7 0.6 fusion.17
  200.3 0.1 pad_maximum_fusion.4
  200.4 0.1 broadcast_multiply_fusion
  200.4 76.5 %psum.15 = f32[16,514]{1,0:T(8,128)S(1)} all-reduce(f32[16,514]{1,0:T(8,128)S(1)} %broadcast_multiply_fusion), channel_id=1, replica_groups=mesh['dp'=16,'tz'=4,'tx'=4] {'dp','tz','tx'}, use_global_device_ids=true, to_apply=%region_3.4 | all-reduce | flops 8224 | bytes 65792 | tf_op jit(solution)/shard_map/psum | solution.py:71
  277.0 0.2 slice_reduce_fusion.1
  277.1 0.1 select_reduce_fusion.1
  277.2 0.1 fusion.25
  277.3 0.1 fusion.20
  277.5 4.9 %convolution_convert_fusion = bf16[8192,512]{1,0:T(8,128)(2,1)S(1)} fusion(bf16[256,8192]{1,0:T(8,128)(2,1)} %all-gather.2.cloned.1.call-done, f32[8192]{0:T(1024)S(1)} %copy-done.9, f32[256]{0:T(256)S(1)} %add_rsqrt_fusion, f32[256,512]{1,0:T(8,128)S(1)} %fusion.6, f32[512]{0:T(512)S(1)} %copy-done.10, f32[256]{0:T(256)S(1)} %bitcast.60), kind=kOutput, calls=%fused_computation.3 | convolution fusion | flops 2161377280 | bytes 13144064 | tf_op jit(solution)/shard_map/dot_general | solution.py:108
  282.3 2.3 fusion.31
  284.6 4.1 %convert.1 = f32[2,2,2,2,512,256]{5,4,3,2,1,0:T(8,128)} convert(bf16[2,2,2,2,512,256]{5,4,3,2,1,0:T(8,128)(2,1)S(1)} %bitcast.48) | non-fusion elementwise | flops 2097152 | bytes 12582912 | tf_op jit(solution)/shard_map/reshape | solution.py:114
  288.8 2.4 fusion.4
  291.2 0.1 collective-permute-start.4
  291.3 4.3 %collective-permute-done.4 = bf16[2,2,2,512,256]{4,3,2,0,1:T(8,128)(2,1)} collective-permute-done((bf16[2,2,2,512,256]{4,3,2,0,1:T(8,128)(2,1)S(1)}, bf16[2,2,2,512,256]{4,3,2,0,1:T(8,128)(2,1)}, u32[]{:S(2)}, u32[]{:S(2)}) %collective-permute-start.4) | collective-permute-done | bytes 2097184 | tf_op jit(solution)/shard_map/ppermute | solution.py:122
  295.6 3.5 bitcast_add_fusion
  299.0 1.9 copy-done.2
  301.0 0.1 fusion.8
  301.1 0.1 collective-permute-start.5
  301.2 25.2 %collective-permute-done.5 = bf16[2,2,512,256]{3,2,1,0:T(8,128)(2,1)} collective-permute-done((bf16[2,2,512,256]{3,2,1,0:T(8,128)(2,1)S(1)}, bf16[2,2,512,256]{3,2,1,0:T(8,128)(2,1)}, u32[]{:S(2)}, u32[]{:S(2)}) %collective-permute-start.5) | collective-permute-done | bytes 1048608 | tf_op jit(solution)/shard_map/ppermute | solution.py:122
  326.4 2.2 bitcast_add_fusion.1
  328.7 2.1 collective-permute-start.6
  330.8 1.6 fusion.15
  332.4 1.2 collective-permute-done.8
  333.5 0.1 collective-permute-start.9
  333.7 8.9 %collective-permute-done.9 = f32[512]{0:T(512)S(1)} collective-permute-done((f32[512]{0:T(512)S(1)}, f32[512]{0:T(512)S(1)}, u32[]{:S(2)}, u32[]{:S(2)}) %collective-permute-start.9) | collective-permute-done | bytes 2080 | tf_op jit(solution)/shard_map/ppermute | solution.py:92
  342.6 3.7 collective-permute-start.10
  346.4 1.2 bitcast_add_fusion.2
  347.6 1.0 copy-done.5
  348.5 5.9 %collective-permute-start.7 = (bf16[512,256]{1,0:T(8,128)(2,1)S(1)}, bf16[512,256]{1,0:T(8,128)(2,1)S(1)}, u32[]{:S(2)}, u32[]{:S(2)}) collective-permute-start(bf16[512,256]{1,0:T(8,128)(2,1)S(1)} %fusion.11), channel_id=1, source_target_pairs={{0,32},{16,48},{32,0},{48,16},{64,96},{80,112},{96,64},{112,80},{1... | collective-permute-start | bytes 786440 | tf_op jit(solution)/shard_map/ppermute | solution.py:122
  354.5 0.2 collective-permute-start.11
  354.7 0.6 constant_dynamic-slice_fusion.3
  355.3 28.2 %scatter_custom_fusion = f32[8016]{0:T(1024)} fusion(s32[4096]{0:T(1024)S(1)} %bitcast.56, f32[4096]{0:T(1024)S(1)} %bitcast.57, f32[]{:T(128)} %constant.95.clone.1), kind=kCustom, calls=%fused_computation.47 | custom fusion | flops 4096 | bytes 32068 | tf_op jit(solution)/shard_map/scatter-add | solution.py:99
  383.5 0.6 add.161
  384.0 1.1 bitcast_add_fusion.3
  385.2 11.2 %reduce-scatter.5.cloned.1.call-done = bf16[512,256]{1,0:T(8,128)(2,1)} async-done(((bf16[8192,256]{1,0:T(8,128)(2,1)}), bf16[512,256]{1,0:T(8,128)(2,1)}) %reduce-scatter.5.cloned.1.call-update) | async-done | bytes 262160 | tf_op jit(solution)/shard_map/reduce_scatter | solution.py:112
  396.4 1.0 convert_element_type.92
  397.4 1.1 pad_maximum_fusion.3
  (57 shorter events, 0.6 us)
Async XLA Ops:
  7.2 133.9 %copy-start = (f32[128256]{0:T(1024)S(1)}, f32[128256]{0:T(1024)}, u32[]{:S(2)}) copy-start(f32[128256]{0:T(1024)} %param.17) | copy-start | bytes 1539076
  7.2 1.0 copy-start.6
  7.2 1.1 copy-start.8
  7.2 60.3 %reduce-scatter.3.cloned.1.call-start = ((), (), s32[]{:S(2)}) async-start(), calls=%async_computation.2 | async-start | bytes 5242880 | tf_op jit(solution)/shard_map/reduce_scatter | solution.py:51
  16.0 1.0 copy-start.3
  16.1 123.5 %all-reduce.2.cloned.1.call-start = ((), (), s32[]{:S(2)}) async-start(), calls=%async_computation.3 | async-start | bytes 2097152 | tf_op jit(solution)/shard_map/psum | solution.py:52
  17.1 21.4 %collective-permute-start = (bf16[1,512,512]{2,1,0:T(8,128)(2,1)S(1)}, bf16[1,512,512]{2,1,0:T(8,128)(2,1)S(1)}, u32[]{:S(2)}, u32[]{:S(2)}) collective-permute-start(bf16[1,512,512]{2,1,0:T(8,128)(2,1)S(1)} %bitcast.49), channel_id=1, source_target_pairs={{0,32},{16,48},{32,0},{48,16},{64,96},{80,112},{96,64},{112,80},{1... | collective-permute-start | bytes 1572872 | tf_op jit(solution)/shard_map/ppermute | solution.py:38
  38.6 24.3 %collective-permute-start.1 = (bf16[2,512,512]{2,1,0:T(8,128)(2,1)S(1)}, bf16[2,512,512]{2,1,0:T(8,128)(2,1)S(1)}, u32[]{:S(2)}, u32[]{:S(2)}) collective-permute-start(bf16[2,512,512]{2,1,0:T(8,128)(2,1)S(1)} %pad_maximum_fusion.2), channel_id=1, source_target_pairs={{0,64},{16,80},{32,96},{48,112},{64,0},{80,16},{96,32},{112,48},{1... | collective-permute-start | bytes 3145736 | tf_op jit(solution)/shard_map/ppermute | solution.py:38
  64.3 47.7 %collective-permute-start.2 = (bf16[4,512,512]{2,1,0:T(8,128)(2,1)}, bf16[4,512,512]{2,1,0:T(8,128)(2,1)}, u32[]{:S(2)}, u32[]{:S(2)}) collective-permute-start(bf16[4,512,512]{2,1,0:T(8,128)(2,1)} %pad_maximum_fusion.1), channel_id=1, source_target_pairs={{0,128},{16,144},{32,160},{48,176},{64,192},{80,208},{96,224},{112... | collective-permute-start | bytes 6291464 | tf_op jit(solution)/shard_map/ppermute | solution.py:38
  67.6 73.5 %copy-start.7 = (s32[256]{0:T(256)S(1)}, s32[256]{0:T(256)}, u32[]{:S(2)}) copy-start(s32[256]{0:T(256)} %param.10) | copy-start | bytes 3076
  67.6 122.8 %all-gather.2.cloned.1.call-start = ((), (), s32[]{:S(2)}) async-start(), calls=%async_computation.4 | async-start | bytes 5242880 | tf_op jit(solution)/shard_map/all_gather | solution.py:53
  115.5 33.2 %collective-permute-start.3 = (bf16[8,512,512]{2,1,0:T(8,128)(2,1)}, bf16[8,512,512]{2,1,0:T(8,128)(2,1)}, u32[]{:S(2)}, u32[]{:S(2)}) collective-permute-start(bf16[8,512,512]{2,1,0:T(8,128)(2,1)} %pad_maximum_fusion), channel_id=1, source_target_pairs={{0,16},{16,0},{32,48},{48,32},{64,80},{80,64},{96,112},{112,96},{1... | collective-permute-start | bytes 12582920 | tf_op jit(solution)/shard_map/ppermute | solution.py:38
  139.6 256.8 %reduce-scatter.5.cloned.1.call-start = ((), (), s32[]{:S(2)}) async-start(), calls=%async_computation.5 | async-start | bytes 4456448 | tf_op jit(solution)/shard_map/reduce_scatter | solution.py:112
  161.8 31.8 %copy-start.9 = (f32[8192]{0:T(1024)S(1)}, f32[8192]{0:T(1024)}, u32[]{:S(2)}) copy-start(f32[8192]{0:T(1024)} %param.14) | copy-start | bytes 98308
  190.3 3.4 copy-start.4
  193.8 5.9 %copy-start.10 = (f32[512]{0:T(512)S(1)}, f32[512]{0:T(512)}, u32[]{:S(2)}) copy-start(f32[512]{0:T(512)} %param.16) | copy-start | bytes 6148
  199.6 82.7 %copy-start.11 = (f32[256,512]{1,0:T(8,128)}, f32[256,512]{1,0:T(8,128)S(1)}, u32[]{:S(2)}) copy-start(f32[256,512]{1,0:T(8,128)S(1)} %fusion.6) | copy-start | bytes 1572868
  291.2 4.4 %collective-permute-start.4 = (bf16[2,2,2,512,256]{4,3,2,0,1:T(8,128)(2,1)S(1)}, bf16[2,2,2,512,256]{4,3,2,0,1:T(8,128)(2,1)}, u32[]{:S(2)}, u32[]{:S(2)}) collective-permute-start(bf16[2,2,2,512,256]{4,3,2,0,1:T(8,128)(2,1)S(1)} %fusion.4), channel_id=1, source_target_pairs={{0,16},{16,0},{32,48},{48,32},{64,80},{80,64},{96,112},{112,96},{1... | collective-permute-start | bytes 6291464 | tf_op jit(solution)/shard_map/ppermute | solution.py:122
  299.0 1.9 copy-start.2
  301.1 25.4 %collective-permute-start.5 = (bf16[2,2,512,256]{3,2,1,0:T(8,128)(2,1)S(1)}, bf16[2,2,512,256]{3,2,1,0:T(8,128)(2,1)}, u32[]{:S(2)}, u32[]{:S(2)}) collective-permute-start(bf16[2,2,512,256]{3,2,1,0:T(8,128)(2,1)S(1)} %fusion.8), channel_id=1, source_target_pairs={{0,64},{16,80},{32,96},{48,112},{64,0},{80,16},{96,32},{112,48},{1... | collective-permute-start | bytes 3145736 | tf_op jit(solution)/shard_map/ppermute | solution.py:122
  328.7 17.7 %collective-permute-start.6 = (bf16[2,512,256]{2,1,0:T(8,128)(2,1)S(1)}, bf16[2,512,256]{2,1,0:T(8,128)(2,1)}, u32[]{:S(2)}, u32[]{:S(2)}) collective-permute-start(bf16[2,512,256]{2,1,0:T(8,128)(2,1)S(1)} %fusion.9), channel_id=1, source_target_pairs={{0,128},{16,144},{32,160},{48,176},{64,192},{80,208},{96,224},{112... | collective-permute-start | bytes 1572872 | tf_op jit(solution)/shard_map/ppermute | solution.py:122
  330.8 67.7 %copy-start.1 = (f32[128256]{0:T(1024)S(1)}, f32[128256]{0:T(1024)}, u32[]{:S(2)}) copy-start(f32[128256]{0:T(1024)} %param.17) | copy-start | bytes 1539076
  332.3 1.2 collective-permute-start.8
  333.5 9.1 %collective-permute-start.9 = (f32[512]{0:T(512)S(1)}, f32[512]{0:T(512)S(1)}, u32[]{:S(2)}, u32[]{:S(2)}) collective-permute-start(f32[512]{0:T(512)S(1)} %add.158), channel_id=1, source_target_pairs={{0,64},{16,80},{32,96},{48,112},{64,0},{80,16},{96,32},{112,48},{1... | collective-permute-start | bytes 6152 | tf_op jit(solution)/shard_map/ppermute | solution.py:92
  342.6 11.8 %collective-permute-start.10 = (f32[512]{0:T(512)S(1)}, f32[512]{0:T(512)S(1)}, u32[]{:S(2)}, u32[]{:S(2)}) collective-permute-start(f32[512]{0:T(512)S(1)} %add.159), channel_id=1, source_target_pairs={{0,128},{16,144},{32,160},{48,176},{64,192},{80,208},{96,224},{112... | collective-permute-start | bytes 6152 | tf_op jit(solution)/shard_map/ppermute | solution.py:92
  347.5 1.0 copy-start.5
  348.5 35.5 %collective-permute-start.7 = (bf16[512,256]{1,0:T(8,128)(2,1)S(1)}, bf16[512,256]{1,0:T(8,128)(2,1)S(1)}, u32[]{:S(2)}, u32[]{:S(2)}) collective-permute-start(bf16[512,256]{1,0:T(8,128)(2,1)S(1)} %fusion.11), channel_id=1, source_target_pairs={{0,32},{16,48},{32,0},{48,16},{64,96},{80,112},{96,64},{112,80},{1... | collective-permute-start | bytes 786440 | tf_op jit(solution)/shard_map/ppermute | solution.py:122
  354.5 29.0 %collective-permute-start.11 = (f32[512]{0:T(512)S(1)}, f32[512]{0:T(512)S(1)}, u32[]{:S(2)}, u32[]{:S(2)}) collective-permute-start(f32[512]{0:T(512)S(1)} %add.160), channel_id=1, source_target_pairs={{0,32},{16,48},{32,0},{48,16},{64,96},{80,112},{96,64},{112,80},{1... | collective-permute-start | bytes 6152 | tf_op jit(solution)/shard_map/ppermute | solution.py:92
Sparse Core Ops, SparseCore 0:
  16.2 51.0 reduce-scatter.2
  70.0 69.5 all-reduce.1
  141.4 48.9 all-gather.1
  288.9 107.4 reduce-scatter.4

commit v8 on v7

--- a/solution.py
+++ b/solution.py
@@ -68,7 +68,14 @@
         ]
     )
     slot = (jnp.arange(n_dp) == r).astype(jnp.float32)
-    slab = lax.psum(slot[:, None] * row[None, :], ("dp", "tz", "tx"))
+    slab = slot[:, None] * row[None, :]
+    n_tensor = lax.axis_size(("tz", "tx"))
+    for b in range(n_tensor.bit_length() - 1):
+        slab = slab + lax.ppermute(
+            slab, ("tz", "tx"), [(i, i ^ (1 << b)) for i in range(n_tensor)]
+        )
+    for b in (0, 2, 3, 1):
+        slab = slab + lax.ppermute(slab, "dp", [(i, i ^ (1 << b)) for i in range(n_dp)])
     grid = slab[:, :seq_len]
     ids_all = slab[:, seq_len:2 * seq_len].astype(jnp.int32)
     plen_all = slab[:, 2 * seq_len]

time: 406 us -> 371 us (0.914)
  blocking collectives: 76.5 us -> 0 us
  waiting for transfers between devices: 177 us -> 200 us
  starting transfers between devices: 24.5 us -> 43.6 us
    psum x1 -> x0, blocking collectives: 76.5 us -> none  [local(): slab = lax.psum(slot[:, None] * row[None, :], ('dp', 'tz', 'tx'))]
    ppermute x0 -> x8, waiting for transfers between devices: none -> 21.5 us  [the longest x4 13.1 us: local(): lax.ppermute(slab, ('tz', 'tx'), [(i, i ^ 1 << b) for i in range(n_tensor)])]
    ppermute x0 -> x8, starting transfers between devices: none -> 16.3 us  [the longest x4 10.3 us: local(): lax.ppermute(slab, 'dp', [(i, i ^ 1 << b) for i in range(n_dp)])]
  transfers between devices with their start and end apart: 16 -> 24, of which waited for: 10 -> 18; matrix products, arithmetic and copies ran while one was open for 18% -> 20% of each run, Pallas kernels for 0% -> 0%
where the time goes in v8:
time: 371 us; the launch traced here: 370 us
  waiting for transfers between devices  200 us (54%)
  other arithmetic  59.2 us (16%)
  starting transfers between devices  43.6 us (12%)
  local copies, waits for them, and re-layouts  31.5 us (8%)
  matrix products  20.7 us (6%)
  between operations  15.4 us (4%)
    ppermute x4, waiting for transfers between devices, local(): got = lax.ppermute(stack, 'dp', [(i, i ^ 1 << b) for i in range(n_dp)])  81.2 us
    ppermute x4, waiting for transfers between devices, local(): lax.ppermute(send.astype(jnp.bfloat16), 'dp', [(i, i ^ 1 << b) for i in r...  28.1 us
    scatter-add x1, other arithmetic, local(): jnp.zeros((slice_len,), jnp.float32).at[idx]  28.1 us
    psum x1, waiting for transfers between devices, local(): part = lax.psum(part, 'tz')  24 us
    all_gather x1, waiting for transfers between devices, local(): hidden = lax.all_gather(part, 'tx', axis=1, tiled=True)  21.1 us
    ppermute x4, waiting for transfers between devices, local(): lax.ppermute(slab, ('tz', 'tx'), [(i, i ^ 1 << b) for i in range(n_tensor)])  13.1 us
    ppermute x4, waiting for transfers between devices, local(): lax.ppermute(grad_out, 'dp', [(i, i ^ 1 << b) for i in range(n_dp)])  12.6 us
    ppermute x4, starting transfers between devices, local(): got = lax.ppermute(stack, 'dp', [(i, i ^ 1 << b) for i in range(n_dp)])  12 us
  transfers between devices with their start and end apart: 24, of which 18 were waited for; matrix products, arithmetic and copies ran while one was open for 20% of the time, Pallas kernels for 0%

profile of v8, /device:TPU:2, one launch (start us, length us, event | category | flops | bytes accessed | tf_op | source)
XLA Modules:
  0.0 370.4 jit_solution(16711267350914129450)
XLA Ops:
  8.3 7.8 %fusion = bf16[256,8192]{1,0:T(8,128)(2,1)} fusion(bf16[256,512]{1,0:T(8,128)(2,1)S(1)} %copy-done.8, bf16[512,8192]{1,0:T(8,128)(2,1)} %param.12, bf16[256,8192]{1,0:T(8,128)(2,1)S(1)} %constant_dynamic-update-slice_fusion.5), kind=kOutput, calls=%fused_computation.7 | convolution fusion | flops 2153775104 | bytes 17039360 | tf_op jit(solution)/shard_map/dot_general | solution.py:49
  16.1 1.0 copy-done.3
  17.1 7.2 %collective-permute-start = (bf16[1,512,512]{2,1,0:T(8,128)(2,1)S(1)}, bf16[1,512,512]{2,1,0:T(8,128)(2,1)S(1)}, u32[]{:S(2)}, u32[]{:S(2)}) collective-permute-start(bf16[1,512,512]{2,1,0:T(8,128)(2,1)S(1)} %bitcast.49), channel_id=1, source_target_pairs={{0,32},{16,48},{32,0},{48,16},{64,96},{80,112},{96,64},{112,80},{1... | collective-permute-start | bytes 1572872 | tf_op jit(solution)/shard_map/ppermute | solution.py:38
  24.3 14.2 %collective-permute-done = bf16[1,512,512]{2,1,0:T(8,128)(2,1)S(1)} collective-permute-done((bf16[1,512,512]{2,1,0:T(8,128)(2,1)S(1)}, bf16[1,512,512]{2,1,0:T(8,128)(2,1)S(1)}, u32[]{:S(2)}, u32[]{:S(2)}) %collective-permute-start) | collective-permute-done | bytes 524320 | tf_op jit(solution)/shard_map/ppermute | solution.py:38
  38.6 1.7 collective-permute-start.1
  40.2 22.6 %collective-permute-done.1 = bf16[2,512,512]{2,1,0:T(8,128)(2,1)S(1)} collective-permute-done((bf16[2,512,512]{2,1,0:T(8,128)(2,1)S(1)}, bf16[2,512,512]{2,1,0:T(8,128)(2,1)S(1)}, u32[]{:S(2)}, u32[]{:S(2)}) %collective-permute-start.1) | collective-permute-done | bytes 1048608 | tf_op jit(solution)/shard_map/ppermute | solution.py:38
  62.8 1.6 pad_maximum_fusion.1
  64.4 3.2 collective-permute-start.2
  67.7 44.4 %collective-permute-done.2 = bf16[4,512,512]{2,1,0:T(8,128)(2,1)} collective-permute-done((bf16[4,512,512]{2,1,0:T(8,128)(2,1)}, bf16[4,512,512]{2,1,0:T(8,128)(2,1)}, u32[]{:S(2)}, u32[]{:S(2)}) %collective-permute-start.2) | collective-permute-done | bytes 2097184 | tf_op jit(solution)/shard_map/ppermute | solution.py:38
  112.1 3.5 pad_maximum_fusion
  115.6 24.0 %all-reduce.2.cloned.1.call-done = bf16[256,2048]{1,0:T(8,128)(2,1)} async-done(((bf16[256,2048]{1,0:T(8,128)(2,1)}), bf16[256,2048]{1,0:T(8,128)(2,1)}) %all-reduce.2.cloned.1.call-update) | async-done | bytes 1048592 | tf_op jit(solution)/shard_map/psum | solution.py:52
  141.2 1.7 gather_fusion.1
  142.9 0.9 constant_dynamic-update-slice_fusion.4
  143.8 0.9 constant_dynamic-update-slice_fusion.3
  144.7 1.1 constant_dynamic-update-slice_fusion.2
  145.7 3.1 constant_dynamic-update-slice_fusion.1
  148.8 4.4 %constant_dynamic-update-slice_fusion = bf16[16,512,512]{2,1,0:T(8,128)(2,1)} fusion(bf16[16,512,512]{2,1,0:T(8,128)(2,1)} %constant_dynamic-update-slice_fusion.1, bf16[8,512,512]{2,1,0:T(8,128)(2,1)} %collective-permute-done.3), kind=kLoop, calls=%fused_computation.55 | loop fusion | bytes 8388608 | tf_op jit(solution)/shard_map/concatenate | solution.py:39
  153.2 8.7 %gather_fusion = bf16[16,512,512]{2,1,0:T(8,128)(2,1)} fusion(bf16[16,512,512]{2,1,0:T(8,128)(2,1)} %constant_dynamic-update-slice_fusion, s32[1024]{0:T(1024)S(1)} %pad_clamp_fusion.1), kind=kCustom, calls=%fused_computation | custom fusion | bytes 16777280 | tf_op jit(solution)/shard_map/jit(_take)/gather | solution.py:44
  161.8 7.5 %bitcast_select_fusion = bf16[8192,512]{1,0:T(8,128)(2,1)} fusion(bf16[16,512,512]{2,1,0:T(8,128)(2,1)} %gather_fusion, pred[8192]{0:T(1024)(128)(4,1)S(1)} %bitcast.55), kind=kLoop, calls=%fused_computation.11 | loop fusion | flops 4194304 | bytes 16785408 | tf_op jit(solution)/shard_map/jit(_take)/select_n | solution.py:44
  169.3 21.1 %all-gather.2.cloned.1.call-done = bf16[256,8192]{1,0:T(8,128)(2,1)} async-done(((bf16[256,2048]{1,0:T(8,128)(2,1)}), bf16[256,8192]{1,0:T(8,128)(2,1)}) %all-gather.2.cloned.1.call-update) | async-done | bytes 4194320 | tf_op jit(solution)/shard_map/all_gather | solution.py:53
  190.4 3.3 fusion.1
  193.8 5.8 %fusion.6 = f32[256,512]{1,0:T(8,128)S(1)} fusion(bf16[8192,512]{1,0:T(8,128)(2,1)} %bitcast_select_fusion, bf16[256,8192]{1,0:T(8,128)(2,1)S(1)} %copy-done.4, f32[8192]{0:T(1024)S(1)} %copy-done.9, f32[256]{0:T(256)S(1)} %add_rsqrt_fusion), kind=kOutput, calls=%fused_computation.19 | convolution fusion | flops 2155872256 | bytes 13140992 | tf_op jit(solution)/shard_map/dot_general | solution.py:56
  199.7 0.6 fusion.17
  200.5 1.2 collective-permute-start.4
  201.7 2.8 collective-permute-done.4
  204.6 1.2 collective-permute-start.5
  205.7 4.6 %collective-permute-done.5 = f32[16,514]{1,0:T(8,128)S(1)} collective-permute-done((f32[16,514]{1,0:T(8,128)S(1)}, f32[16,514]{1,0:T(8,128)S(1)}, u32[]{:S(2)}, u32[]{:S(2)}) %collective-permute-start.5) | collective-permute-done | bytes 32928 | tf_op jit(solution)/shard_map/ppermute | solution.py:74
  210.4 1.6 collective-permute-start.6
  212.0 2.9 collective-permute-done.6
  214.9 2.1 collective-permute-start.7
  216.9 2.8 collective-permute-done.7
  219.8 1.2 collective-permute-done.8
  221.0 1.5 collective-permute-start.9
  222.5 2.5 collective-permute-done.9
  225.0 3.0 collective-permute-start.10
  228.0 2.5 collective-permute-done.10
  230.5 5.8 %collective-permute-start.11 = (f32[16,514]{1,0:T(8,128)S(1)}, f32[16,514]{1,0:T(8,128)S(1)}, u32[]{:S(2)}, u32[]{:S(2)}) collective-permute-start(f32[16,514]{1,0:T(8,128)S(1)} %add.172), channel_id=1, source_target_pairs={{0,32},{16,48},{32,0},{48,16},{64,96},{80,112},{96,64},{112,80},{1... | collective-permute-start | bytes 98696 | tf_op jit(solution)/shard_map/ppermute | solution.py:78
  236.3 2.2 collective-permute-done.11
  239.0 4.9 %convolution_convert_fusion = bf16[8192,512]{1,0:T(8,128)(2,1)S(1)} fusion(bf16[256,8192]{1,0:T(8,128)(2,1)} %all-gather.2.cloned.1.call-done, f32[8192]{0:T(1024)S(1)} %copy-done.9, f32[256]{0:T(256)S(1)} %add_rsqrt_fusion, f32[256,512]{1,0:T(8,128)S(1)} %fusion.6, f32[512]{0:T(512)S(1)} %copy-done.10, f32[256]{0:T(256)S(1)} %bitcast.60), kind=kOutput, calls=%fused_computation.3 | convolution fusion | flops 2161377280 | bytes 13144064 | tf_op jit(solution)/shard_map/dot_general | solution.py:115
  243.9 2.3 fusion.32
  246.2 4.1 %convert.1 = f32[2,2,2,2,512,256]{5,4,3,2,1,0:T(8,128)} convert(bf16[2,2,2,2,512,256]{5,4,3,2,1,0:T(8,128)(2,1)S(1)} %bitcast.48) | non-fusion elementwise | flops 2097152 | bytes 12582912 | tf_op jit(solution)/shard_map/reshape | solution.py:121
  250.4 2.4 fusion.4
  252.9 4.3 %collective-permute-done.12 = bf16[2,2,2,512,256]{4,3,2,0,1:T(8,128)(2,1)} collective-permute-done((bf16[2,2,2,512,256]{4,3,2,0,1:T(8,128)(2,1)S(1)}, bf16[2,2,2,512,256]{4,3,2,0,1:T(8,128)(2,1)}, u32[]{:S(2)}, u32[]{:S(2)}) %collective-permute-start.12) | collective-permute-done | bytes 2097184 | tf_op jit(solution)/shard_map/ppermute | solution.py:129
  257.2 3.2 bitcast_add_fusion
  260.4 1.9 copy-done.2
  262.5 1.6 collective-permute-start.13
  264.1 23.8 %collective-permute-done.13 = bf16[2,2,512,256]{3,2,1,0:T(8,128)(2,1)} collective-permute-done((bf16[2,2,512,256]{3,2,1,0:T(8,128)(2,1)S(1)}, bf16[2,2,512,256]{3,2,1,0:T(8,128)(2,1)}, u32[]{:S(2)}, u32[]{:S(2)}) %collective-permute-start.13) | collective-permute-done | bytes 1048608 | tf_op jit(solution)/shard_map/ppermute | solution.py:129
  287.9 2.2 bitcast_add_fusion.1
  290.1 3.1 collective-permute-start.14
  293.2 1.6 fusion.15
  294.8 1.2 collective-permute-done.16
  295.9 0.6 collective-permute-start.17
  296.6 11.5 %collective-permute-done.17 = f32[512]{0:T(512)S(1)} collective-permute-done((f32[512]{0:T(512)S(1)}, f32[512]{0:T(512)S(1)}, u32[]{:S(2)}, u32[]{:S(2)}) %collective-permute-start.17) | collective-permute-done | bytes 2080 | tf_op jit(solution)/shard_map/ppermute | solution.py:99
  308.0 2.7 collective-permute-start.18
  310.8 1.2 bitcast_add_fusion.2
  312.0 1.0 copy-done.5
  312.9 6.9 %collective-permute-start.15 = (bf16[512,256]{1,0:T(8,128)(2,1)S(1)}, bf16[512,256]{1,0:T(8,128)(2,1)S(1)}, u32[]{:S(2)}, u32[]{:S(2)}) collective-permute-start(bf16[512,256]{1,0:T(8,128)(2,1)S(1)} %fusion.11), channel_id=1, source_target_pairs={{0,32},{16,48},{32,0},{48,16},{64,96},{80,112},{96,64},{112,80},{1... | collective-permute-start | bytes 786440 | tf_op jit(solution)/shard_map/ppermute | solution.py:129
  320.0 0.6 constant_dynamic-slice_fusion.3
  320.6 28.1 %scatter_custom_fusion = f32[8016]{0:T(1024)} fusion(s32[4096]{0:T(1024)S(1)} %bitcast.56, f32[4096]{0:T(1024)S(1)} %bitcast.57, f32[]{:T(128)} %constant.95.clone.1), kind=kCustom, calls=%fused_computation.47 | custom fusion | flops 4096 | bytes 32068 | tf_op jit(solution)/shard_map/scatter-add | solution.py:106
  348.7 0.6 add.191
  349.3 1.1 bitcast_add_fusion.3
  350.4 11.3 %reduce-scatter.5.cloned.1.call-done = bf16[512,256]{1,0:T(8,128)(2,1)} async-done(((bf16[8192,256]{1,0:T(8,128)(2,1)}), bf16[512,256]{1,0:T(8,128)(2,1)}) %reduce-scatter.5.cloned.1.call-update) | async-done | bytes 262160 | tf_op jit(solution)/shard_map/reduce_scatter | solution.py:119
  361.7 1.0 convert_element_type.92
  362.7 1.1 pad_maximum_fusion.3
  (80 shorter events, 3.1 us)
Async XLA Ops:
  7.2 134.0 %copy-start = (f32[128256]{0:T(1024)S(1)}, f32[128256]{0:T(1024)}, u32[]{:S(2)}) copy-start(f32[128256]{0:T(1024)} %param.17) | copy-start | bytes 1539076
  7.2 1.0 copy-start.6
  7.2 1.1 copy-start.8
  7.2 60.4 %reduce-scatter.3.cloned.1.call-start = ((), (), s32[]{:S(2)}) async-start(), calls=%async_computation.2 | async-start | bytes 5242880 | tf_op jit(solution)/shard_map/reduce_scatter | solution.py:51
  16.1 1.0 copy-start.3
  16.1 123.5 %all-reduce.2.cloned.1.call-start = ((), (), s32[]{:S(2)}) async-start(), calls=%async_computation.3 | async-start | bytes 2097152 | tf_op jit(solution)/shard_map/psum | solution.py:52
  17.1 21.4 %collective-permute-start = (bf16[1,512,512]{2,1,0:T(8,128)(2,1)S(1)}, bf16[1,512,512]{2,1,0:T(8,128)(2,1)S(1)}, u32[]{:S(2)}, u32[]{:S(2)}) collective-permute-start(bf16[1,512,512]{2,1,0:T(8,128)(2,1)S(1)} %bitcast.49), channel_id=1, source_target_pairs={{0,32},{16,48},{32,0},{48,16},{64,96},{80,112},{96,64},{112,80},{1... | collective-permute-start | bytes 1572872 | tf_op jit(solution)/shard_map/ppermute | solution.py:38
  38.6 24.3 %collective-permute-start.1 = (bf16[2,512,512]{2,1,0:T(8,128)(2,1)S(1)}, bf16[2,512,512]{2,1,0:T(8,128)(2,1)S(1)}, u32[]{:S(2)}, u32[]{:S(2)}) collective-permute-start(bf16[2,512,512]{2,1,0:T(8,128)(2,1)S(1)} %pad_maximum_fusion.2), channel_id=1, source_target_pairs={{0,64},{16,80},{32,96},{48,112},{64,0},{80,16},{96,32},{112,48},{1... | collective-permute-start | bytes 3145736 | tf_op jit(solution)/shard_map/ppermute | solution.py:38
  64.4 47.7 %collective-permute-start.2 = (bf16[4,512,512]{2,1,0:T(8,128)(2,1)}, bf16[4,512,512]{2,1,0:T(8,128)(2,1)}, u32[]{:S(2)}, u32[]{:S(2)}) collective-permute-start(bf16[4,512,512]{2,1,0:T(8,128)(2,1)} %pad_maximum_fusion.1), channel_id=1, source_target_pairs={{0,128},{16,144},{32,160},{48,176},{64,192},{80,208},{96,224},{112... | collective-permute-start | bytes 6291464 | tf_op jit(solution)/shard_map/ppermute | solution.py:38
  67.6 73.5 %copy-start.7 = (s32[256]{0:T(256)S(1)}, s32[256]{0:T(256)}, u32[]{:S(2)}) copy-start(s32[256]{0:T(256)} %param.10) | copy-start | bytes 3076
  67.6 122.8 %all-gather.2.cloned.1.call-start = ((), (), s32[]{:S(2)}) async-start(), calls=%async_computation.4 | async-start | bytes 5242880 | tf_op jit(solution)/shard_map/all_gather | solution.py:53
  115.6 33.2 %collective-permute-start.3 = (bf16[8,512,512]{2,1,0:T(8,128)(2,1)}, bf16[8,512,512]{2,1,0:T(8,128)(2,1)}, u32[]{:S(2)}, u32[]{:S(2)}) collective-permute-start(bf16[8,512,512]{2,1,0:T(8,128)(2,1)} %pad_maximum_fusion), channel_id=1, source_target_pairs={{0,16},{16,0},{32,48},{48,32},{64,80},{80,64},{96,112},{112,96},{1... | collective-permute-start | bytes 12582920 | tf_op jit(solution)/shard_map/ppermute | solution.py:38
  139.6 222.1 %reduce-scatter.5.cloned.1.call-start = ((), (), s32[]{:S(2)}) async-start(), calls=%async_computation.5 | async-start | bytes 4456448 | tf_op jit(solution)/shard_map/reduce_scatter | solution.py:119
  161.8 31.8 %copy-start.9 = (f32[8192]{0:T(1024)S(1)}, f32[8192]{0:T(1024)}, u32[]{:S(2)}) copy-start(f32[8192]{0:T(1024)} %param.14) | copy-start | bytes 98308
  190.4 3.4 copy-start.4
  193.8 5.9 %copy-start.10 = (f32[512]{0:T(512)S(1)}, f32[512]{0:T(512)}, u32[]{:S(2)}) copy-start(f32[512]{0:T(512)} %param.16) | copy-start | bytes 6148
  199.7 44.2 %copy-start.11 = (f32[256,512]{1,0:T(8,128)}, f32[256,512]{1,0:T(8,128)S(1)}, u32[]{:S(2)}) copy-start(f32[256,512]{1,0:T(8,128)S(1)} %fusion.6) | copy-start | bytes 1572868
  200.5 4.0 %collective-permute-start.4 = (f32[16,514]{1,0:T(8,128)S(1)}, f32[16,514]{1,0:T(8,128)S(1)}, u32[]{:S(2)}, u32[]{:S(2)}) collective-permute-start(f32[16,514]{1,0:T(8,128)S(1)} %broadcast_multiply_fusion), channel_id=1, source_target_pairs={{0,1},{1,0},{2,3},{3,2},{4,5},{5,4},{6,7},{7,6},{8,9},{9,8},{10,11... | collective-permute-start | bytes 98696 | tf_op jit(solution)/shard_map/ppermute | solution.py:74
  204.6 5.7 %collective-permute-start.5 = (f32[16,514]{1,0:T(8,128)S(1)}, f32[16,514]{1,0:T(8,128)S(1)}, u32[]{:S(2)}, u32[]{:S(2)}) collective-permute-start(f32[16,514]{1,0:T(8,128)S(1)} %fusion.26), channel_id=1, source_target_pairs={{0,2},{1,3},{2,0},{3,1},{4,6},{5,7},{6,4},{7,5},{8,10},{9,11},{10,... | collective-permute-start | bytes 98696 | tf_op jit(solution)/shard_map/ppermute | solution.py:74
  210.4 4.5 %collective-permute-start.6 = (f32[16,514]{1,0:T(8,128)S(1)}, f32[16,514]{1,0:T(8,128)S(1)}, u32[]{:S(2)}, u32[]{:S(2)}) collective-permute-start(f32[16,514]{1,0:T(8,128)S(1)} %fusion.37), channel_id=1, source_target_pairs={{0,4},{1,5},{2,6},{3,7},{4,0},{5,1},{6,2},{7,3},{8,12},{9,13},{10,... | collective-permute-start | bytes 98696 | tf_op jit(solution)/shard_map/ppermute | solution.py:74
  214.9 4.9 %collective-permute-start.7 = (f32[16,514]{1,0:T(8,128)S(1)}, f32[16,514]{1,0:T(8,128)S(1)}, u32[]{:S(2)}, u32[]{:S(2)}) collective-permute-start(f32[16,514]{1,0:T(8,128)S(1)} %add.168), channel_id=1, source_target_pairs={{0,8},{1,9},{2,10},{3,11},{4,12},{5,13},{6,14},{7,15},{8,0},{9,1},... | collective-permute-start | bytes 98696 | tf_op jit(solution)/shard_map/ppermute | solution.py:74
  219.8 1.2 collective-permute-start.8
  221.0 4.0 %collective-permute-start.9 = (f32[16,514]{1,0:T(8,128)S(1)}, f32[16,514]{1,0:T(8,128)S(1)}, u32[]{:S(2)}, u32[]{:S(2)}) collective-permute-start(f32[16,514]{1,0:T(8,128)S(1)} %add.170), channel_id=1, source_target_pairs={{0,64},{16,80},{32,96},{48,112},{64,0},{80,16},{96,32},{112,48},{1... | collective-permute-start | bytes 98696 | tf_op jit(solution)/shard_map/ppermute | solution.py:78
  225.0 5.5 %collective-permute-start.10 = (f32[16,514]{1,0:T(8,128)S(1)}, f32[16,514]{1,0:T(8,128)S(1)}, u32[]{:S(2)}, u32[]{:S(2)}) collective-permute-start(f32[16,514]{1,0:T(8,128)S(1)} %add.171), channel_id=1, source_target_pairs={{0,128},{16,144},{32,160},{48,176},{64,192},{80,208},{96,224},{112... | collective-permute-start | bytes 98696 | tf_op jit(solution)/shard_map/ppermute | solution.py:78
  230.5 8.0 %collective-permute-start.11 = (f32[16,514]{1,0:T(8,128)S(1)}, f32[16,514]{1,0:T(8,128)S(1)}, u32[]{:S(2)}, u32[]{:S(2)}) collective-permute-start(f32[16,514]{1,0:T(8,128)S(1)} %add.172), channel_id=1, source_target_pairs={{0,32},{16,48},{32,0},{48,16},{64,96},{80,112},{96,64},{112,80},{1... | collective-permute-start | bytes 98696 | tf_op jit(solution)/shard_map/ppermute | solution.py:78
  252.8 4.4 %collective-permute-start.12 = (bf16[2,2,2,512,256]{4,3,2,0,1:T(8,128)(2,1)S(1)}, bf16[2,2,2,512,256]{4,3,2,0,1:T(8,128)(2,1)}, u32[]{:S(2)}, u32[]{:S(2)}) collective-permute-start(bf16[2,2,2,512,256]{4,3,2,0,1:T(8,128)(2,1)S(1)} %fusion.4), channel_id=1, source_target_pairs={{0,16},{16,0},{32,48},{48,32},{64,80},{80,64},{96,112},{112,96},{1... | collective-permute-start | bytes 6291464 | tf_op jit(solution)/shard_map/ppermute | solution.py:129
  260.4 2.0 copy-start.2
  262.5 25.4 %collective-permute-start.13 = (bf16[2,2,512,256]{3,2,1,0:T(8,128)(2,1)S(1)}, bf16[2,2,512,256]{3,2,1,0:T(8,128)(2,1)}, u32[]{:S(2)}, u32[]{:S(2)}) collective-permute-start(bf16[2,2,512,256]{3,2,1,0:T(8,128)(2,1)S(1)} %fusion.8), channel_id=1, source_target_pairs={{0,64},{16,80},{32,96},{48,112},{64,0},{80,16},{96,32},{112,48},{1... | collective-permute-start | bytes 3145736 | tf_op jit(solution)/shard_map/ppermute | solution.py:129
  290.1 20.6 %collective-permute-start.14 = (bf16[2,512,256]{2,1,0:T(8,128)(2,1)S(1)}, bf16[2,512,256]{2,1,0:T(8,128)(2,1)}, u32[]{:S(2)}, u32[]{:S(2)}) collective-permute-start(bf16[2,512,256]{2,1,0:T(8,128)(2,1)S(1)} %fusion.9), channel_id=1, source_target_pairs={{0,128},{16,144},{32,160},{48,176},{64,192},{80,208},{96,224},{112... | collective-permute-start | bytes 1572872 | tf_op jit(solution)/shard_map/ppermute | solution.py:129
  293.2 70.6 %copy-start.1 = (f32[128256]{0:T(1024)S(1)}, f32[128256]{0:T(1024)}, u32[]{:S(2)}) copy-start(f32[128256]{0:T(1024)} %param.17) | copy-start | bytes 1539076
  294.8 1.2 collective-permute-start.16
  295.9 12.1 %collective-permute-start.17 = (f32[512]{0:T(512)S(1)}, f32[512]{0:T(512)S(1)}, u32[]{:S(2)}, u32[]{:S(2)}) collective-permute-start(f32[512]{0:T(512)S(1)} %add.188), channel_id=1, source_target_pairs={{0,64},{16,80},{32,96},{48,112},{64,0},{80,16},{96,32},{112,48},{1... | collective-permute-start | bytes 6152 | tf_op jit(solution)/shard_map/ppermute | solution.py:99
  308.0 11.8 %collective-permute-start.18 = (f32[512]{0:T(512)S(1)}, f32[512]{0:T(512)S(1)}, u32[]{:S(2)}, u32[]{:S(2)}) collective-permute-start(f32[512]{0:T(512)S(1)} %add.189), channel_id=1, source_target_pairs={{0,128},{16,144},{32,160},{48,176},{64,192},{80,208},{96,224},{112... | collective-permute-start | bytes 6152 | tf_op jit(solution)/shard_map/ppermute | solution.py:99
  311.9 1.0 copy-start.5
  312.9 36.3 %collective-permute-start.15 = (bf16[512,256]{1,0:T(8,128)(2,1)S(1)}, bf16[512,256]{1,0:T(8,128)(2,1)S(1)}, u32[]{:S(2)}, u32[]{:S(2)}) collective-permute-start(bf16[512,256]{1,0:T(8,128)(2,1)S(1)} %fusion.11), channel_id=1, source_target_pairs={{0,32},{16,48},{32,0},{48,16},{64,96},{80,112},{96,64},{112,80},{1... | collective-permute-start | bytes 786440 | tf_op jit(solution)/shard_map/ppermute | solution.py:129
  319.9 28.8 %collective-permute-start.19 = (f32[512]{0:T(512)S(1)}, f32[512]{0:T(512)S(1)}, u32[]{:S(2)}, u32[]{:S(2)}) collective-permute-start(f32[512]{0:T(512)S(1)} %add.190), channel_id=1, source_target_pairs={{0,32},{16,48},{32,0},{48,16},{64,96},{80,112},{96,64},{112,80},{1... | collective-permute-start | bytes 6152 | tf_op jit(solution)/shard_map/ppermute | solution.py:99
Sparse Core Ops, SparseCore 0:
  16.2 51.0 reduce-scatter.2
  70.0 69.5 all-reduce.1
  141.4 48.9 all-gather.1
  250.5 111.2 reduce-scatter.4

commit v9 on v8

--- a/solution.py
+++ b/solution.py
@@ -49,7 +49,10 @@
     partial_sum = jnp.dot(attn_heads, out_proj, preferred_element_type=jnp.float32)
     partial_sum = (partial_sum + resid_pad.astype(jnp.float32)).astype(jnp.bfloat16)
     part = lax.psum_scatter(partial_sum, "tx", scatter_dimension=1, tiled=True)
-    part = lax.psum(part, "tz")
+    n_z = lax.axis_size("tz")
+    for b in range(n_z.bit_length() - 1):
+        got = lax.ppermute(part, "tz", [(i, i ^ (1 << b)) for i in range(n_z)])
+        part = (part.astype(jnp.float32) + got.astype(jnp.float32)).astype(jnp.bfloat16)
     hidden = lax.all_gather(part, "tx", axis=1, tiled=True)
     normed = normalize(hidden, norm_gain)
 

time: 371 us -> 373 us (level)
  starting transfers between devices: 43.6 us -> 47.6 us
    ppermute x4, waiting for transfers between devices: 81.2 us -> 36.5 us  [local(): got = lax.ppermute(stack, 'dp', [(i, i ^ 1 << b) for i in range(n_dp)])]
    ppermute x0 -> x2, waiting for transfers between devices: none -> 39.1 us  [local(): got = lax.ppermute(part, 'tz', [(i, i ^ 1 << b) for i in range(n_z)])]
    reduce_scatter x1, waiting for transfers between devices: 0.01 us -> 26.2 us  [local(): part = lax.psum_scatter(partial_sum, 'tx', scatter_dimension=1, tiled=True)]
    psum x1 -> x0, waiting for transfers between devices: 24 us -> none  [local(): part = lax.psum(part, 'tz')]
    ppermute x0 -> x2, starting transfers between devices: none -> 4.18 us  [local(): got = lax.ppermute(part, 'tz', [(i, i ^ 1 << b) for i in range(n_z)])]
    unnamed x32 -> x38, local copies, waits for them, and re-layouts: 10.6 us -> 10.3 us
  transfers between devices with their start and end apart: 24 -> 25, of which waited for: 18 -> 19; matrix products, arithmetic and copies ran while one was open for 20% -> 20% of each run, Pallas kernels for 0% -> 0%
where the time goes in v9:
time: 373 us
  waiting for transfers between devices  199 us (53%)
  other arithmetic  58.9 us (16%)
  starting transfers between devices  47.6 us (13%)
  local copies, waits for them, and re-layouts  31.5 us (8%)
  matrix products  20.6 us (6%)
  between operations  15.4 us (4%)
    ppermute x2, waiting for transfers between devices, local(): got = lax.ppermute(part, 'tz', [(i, i ^ 1 << b) for i in range(n_z)])  39.1 us
    ppermute x4, waiting for transfers between devices, local(): got = lax.ppermute(stack, 'dp', [(i, i ^ 1 << b) for i in range(n_dp)])  36.5 us
    ppermute x4, waiting for transfers between devices, local(): lax.ppermute(send.astype(jnp.bfloat16), 'dp', [(i, i ^ 1 << b) for i in r...  28.1 us
    scatter-add x1, other arithmetic, local(): jnp.zeros((slice_len,), jnp.float32).at[idx]  27.7 us
    reduce_scatter x1, waiting for transfers between devices, local(): part = lax.psum_scatter(partial_sum, 'tx', scatter_dimension=1, tiled=True)  26.2 us
    all_gather x1, waiting for transfers between devices, local(): hidden = lax.all_gather(part, 'tx', axis=1, tiled=True)  22.7 us
    ppermute x4, waiting for transfers between devices, local(): lax.ppermute(slab, ('tz', 'tx'), [(i, i ^ 1 << b) for i in range(n_tensor)])  13 us
    ppermute x4, waiting for transfers between devices, local(): lax.ppermute(grad_out, 'dp', [(i, i ^ 1 << b) for i in range(n_dp)])  12.6 us
  transfers between devices with their start and end apart: 25, of which 19 were waited for; matrix products, arithmetic and copies ran while one was open for 20% of the time, Pallas kernels for 0%

profile of v9, /device:TPU:2, one launch (start us, length us, event | category | flops | bytes accessed | tf_op | source)
XLA Modules:
  0.0 372.7 jit_solution(9658990112749862318)
XLA Ops:
  8.3 7.8 %fusion = bf16[256,8192]{1,0:T(8,128)(2,1)} fusion(bf16[256,512]{1,0:T(8,128)(2,1)S(1)} %copy-done.11, bf16[512,8192]{1,0:T(8,128)(2,1)} %param.12, bf16[256,8192]{1,0:T(8,128)(2,1)S(1)} %constant_dynamic-update-slice_fusion.5), kind=kOutput, calls=%fused_computation.7 | convolution fusion | flops 2153775104 | bytes 17039360 | tf_op jit(solution)/shard_map/dot_general | solution.py:49
  16.1 1.0 copy-done.5
  17.1 7.2 %collective-permute-start.2 = (bf16[1,512,512]{2,1,0:T(8,128)(2,1)S(1)}, bf16[1,512,512]{2,1,0:T(8,128)(2,1)S(1)}, u32[]{:S(2)}, u32[]{:S(2)}) collective-permute-start(bf16[1,512,512]{2,1,0:T(8,128)(2,1)S(1)} %bitcast.49), channel_id=1, source_target_pairs={{0,32},{16,48},{32,0},{48,16},{64,96},{80,112},{96,64},{112,80},{1... | collective-permute-start | bytes 1572872 | tf_op jit(solution)/shard_map/ppermute | solution.py:38
  24.3 14.2 %collective-permute-done.2 = bf16[1,512,512]{2,1,0:T(8,128)(2,1)S(1)} collective-permute-done((bf16[1,512,512]{2,1,0:T(8,128)(2,1)S(1)}, bf16[1,512,512]{2,1,0:T(8,128)(2,1)S(1)}, u32[]{:S(2)}, u32[]{:S(2)}) %collective-permute-start.2) | collective-permute-done | bytes 524320 | tf_op jit(solution)/shard_map/ppermute | solution.py:38
  38.5 1.1 pad_maximum_fusion.2
  39.5 1.6 collective-permute-start.3
  41.1 26.2 %reduce-scatter.3.cloned.1.call-done = bf16[256,2048]{1,0:T(8,128)(2,1)} async-done(((bf16[256,8192]{1,0:T(8,128)(2,1)}), bf16[256,2048]{1,0:T(8,128)(2,1)}) %reduce-scatter.3.cloned.1.call-update) | async-done | bytes 1048592 | tf_op jit(solution)/shard_map/reduce_scatter | solution.py:51
  67.3 1.6 collective-permute-start
  69.1 3.1 collective-permute-start.4
  72.2 20.2 %collective-permute-done = bf16[256,2048]{1,0:T(8,128)(2,1)S(1)} collective-permute-done((bf16[256,2048]{1,0:T(8,128)(2,1)}, bf16[256,2048]{1,0:T(8,128)(2,1)S(1)}, u32[]{:S(2)}, u32[]{:S(2)}) %collective-permute-start) | collective-permute-done | bytes 1048608 | tf_op jit(solution)/shard_map/ppermute | solution.py:54
  92.8 2.6 collective-permute-start.1
  95.4 22.3 %collective-permute-done.4 = bf16[4,512,512]{2,1,0:T(8,128)(2,1)S(1)} collective-permute-done((bf16[4,512,512]{2,1,0:T(8,128)(2,1)S(1)}, bf16[4,512,512]{2,1,0:T(8,128)(2,1)S(1)}, u32[]{:S(2)}, u32[]{:S(2)}) %collective-permute-start.4) | collective-permute-done | bytes 2097184 | tf_op jit(solution)/shard_map/ppermute | solution.py:38
  117.7 1.3 copy-done.3
  119.1 2.2 pad_maximum_fusion
  121.3 18.9 %collective-permute-done.1 = bf16[256,2048]{1,0:T(8,128)(2,1)S(1)} collective-permute-done((bf16[256,2048]{1,0:T(8,128)(2,1)S(1)}, bf16[256,2048]{1,0:T(8,128)(2,1)S(1)}, u32[]{:S(2)}, u32[]{:S(2)}) %collective-permute-start.1) | collective-permute-done | bytes 1048608 | tf_op jit(solution)/shard_map/ppermute | solution.py:54
  140.2 1.4 add_convert_fusion
  143.3 1.7 gather_fusion.1
  145.1 0.9 constant_dynamic-update-slice_fusion.4
  146.8 1.1 constant_dynamic-update-slice_fusion.2
  147.9 1.5 constant_dynamic-update-slice_fusion.1
  149.4 4.4 %constant_dynamic-update-slice_fusion = bf16[16,512,512]{2,1,0:T(8,128)(2,1)} fusion(bf16[16,512,512]{2,1,0:T(8,128)(2,1)} %constant_dynamic-update-slice_fusion.1, bf16[8,512,512]{2,1,0:T(8,128)(2,1)} %collective-permute-done.5), kind=kLoop, calls=%fused_computation.57 | loop fusion | bytes 8388608 | tf_op jit(solution)/shard_map/concatenate | solution.py:39
  153.8 8.9 %gather_fusion = bf16[16,512,512]{2,1,0:T(8,128)(2,1)} fusion(bf16[16,512,512]{2,1,0:T(8,128)(2,1)} %constant_dynamic-update-slice_fusion, s32[1024]{0:T(1024)S(1)} %pad_clamp_fusion.1), kind=kCustom, calls=%fused_computation | custom fusion | bytes 16777280 | tf_op jit(solution)/shard_map/jit(_take)/gather | solution.py:44
  162.7 7.5 %bitcast_select_fusion = bf16[8192,512]{1,0:T(8,128)(2,1)} fusion(bf16[16,512,512]{2,1,0:T(8,128)(2,1)} %gather_fusion, pred[8192]{0:T(1024)(128)(4,1)S(1)} %bitcast.55), kind=kLoop, calls=%fused_computation.11 | loop fusion | flops 4194304 | bytes 16785408 | tf_op jit(solution)/shard_map/jit(_take)/select_n | solution.py:44
  170.1 22.7 %all-gather.2.cloned.1.call-done = bf16[256,8192]{1,0:T(8,128)(2,1)} async-done(((bf16[256,2048]{1,0:T(8,128)(2,1)}), bf16[256,8192]{1,0:T(8,128)(2,1)}) %all-gather.2.cloned.1.call-update) | async-done | bytes 4194320 | tf_op jit(solution)/shard_map/all_gather | solution.py:56
  192.9 3.3 fusion.1
  196.3 5.8 %fusion.6 = f32[256,512]{1,0:T(8,128)S(1)} fusion(bf16[8192,512]{1,0:T(8,128)(2,1)} %bitcast_select_fusion, bf16[256,8192]{1,0:T(8,128)(2,1)S(1)} %copy-done.6, f32[8192]{0:T(1024)S(1)} %copy-done.12, f32[256]{0:T(256)S(1)} %add_rsqrt_fusion), kind=kOutput, calls=%fused_computation.21 | convolution fusion | flops 2155872256 | bytes 13140992 | tf_op jit(solution)/shard_map/dot_general | solution.py:59
  203.0 1.2 collective-permute-start.6
  204.2 2.8 collective-permute-done.6
  207.1 1.0 collective-permute-start.7
  208.0 4.6 %collective-permute-done.7 = f32[16,514]{1,0:T(8,128)S(1)} collective-permute-done((f32[16,514]{1,0:T(8,128)S(1)}, f32[16,514]{1,0:T(8,128)S(1)}, u32[]{:S(2)}, u32[]{:S(2)}) %collective-permute-start.7) | collective-permute-done | bytes 32928 | tf_op jit(solution)/shard_map/ppermute | solution.py:77
  212.7 1.6 collective-permute-start.8
  214.3 2.9 collective-permute-done.8
  217.2 2.1 collective-permute-start.9
  219.3 2.8 collective-permute-done.9
  222.1 1.2 collective-permute-done.10
  223.3 1.5 collective-permute-start.11
  224.8 2.5 collective-permute-done.11
  227.3 3.0 collective-permute-start.12
  230.3 2.5 collective-permute-done.12
  232.8 5.8 %collective-permute-start.13 = (f32[16,514]{1,0:T(8,128)S(1)}, f32[16,514]{1,0:T(8,128)S(1)}, u32[]{:S(2)}, u32[]{:S(2)}) collective-permute-start(f32[16,514]{1,0:T(8,128)S(1)} %add.178), channel_id=1, source_target_pairs={{0,32},{16,48},{32,0},{48,16},{64,96},{80,112},{96,64},{112,80},{1... | collective-permute-start | bytes 98696 | tf_op jit(solution)/shard_map/ppermute | solution.py:81
  238.6 2.2 collective-permute-done.13
  241.3 4.9 %convolution_convert_fusion = bf16[8192,512]{1,0:T(8,128)(2,1)S(1)} fusion(bf16[256,8192]{1,0:T(8,128)(2,1)} %all-gather.2.cloned.1.call-done, f32[8192]{0:T(1024)S(1)} %copy-done.12, f32[256]{0:T(256)S(1)} %add_rsqrt_fusion, f32[256,512]{1,0:T(8,128)S(1)} %fusion.6, f32[512]{0:T(512)S(1)} %copy-done.13, f32[256]{0:T(256)S(1)} %bitcast.60), kind=kOutput, calls=%fused_computation.3 | convolution fusion | flops 2161377280 | bytes 13144064 | tf_op jit(solution)/shard_map/dot_general | solution.py:118
  246.2 2.3 fusion.32
  248.5 4.2 %convert.1 = f32[2,2,2,2,512,256]{5,4,3,2,1,0:T(8,128)} convert(bf16[2,2,2,2,512,256]{5,4,3,2,1,0:T(8,128)(2,1)S(1)} %bitcast.48) | non-fusion elementwise | flops 2097152 | bytes 12582912 | tf_op jit(solution)/shard_map/reshape | solution.py:124
  252.7 2.4 fusion.4
  255.2 4.3 %collective-permute-done.14 = bf16[2,2,2,512,256]{4,3,2,0,1:T(8,128)(2,1)} collective-permute-done((bf16[2,2,2,512,256]{4,3,2,0,1:T(8,128)(2,1)S(1)}, bf16[2,2,2,512,256]{4,3,2,0,1:T(8,128)(2,1)}, u32[]{:S(2)}, u32[]{:S(2)}) %collective-permute-start.14) | collective-permute-done | bytes 2097184 | tf_op jit(solution)/shard_map/ppermute | solution.py:132
  259.5 3.2 bitcast_add_fusion
  262.8 1.9 copy-done.2
  264.8 1.6 collective-permute-start.15
  266.4 23.8 %collective-permute-done.15 = bf16[2,2,512,256]{3,2,1,0:T(8,128)(2,1)} collective-permute-done((bf16[2,2,512,256]{3,2,1,0:T(8,128)(2,1)S(1)}, bf16[2,2,512,256]{3,2,1,0:T(8,128)(2,1)}, u32[]{:S(2)}, u32[]{:S(2)}) %collective-permute-start.15) | collective-permute-done | bytes 1048608 | tf_op jit(solution)/shard_map/ppermute | solution.py:132
  290.2 2.2 bitcast_add_fusion.1
  292.4 3.1 collective-permute-start.16
  295.5 1.6 fusion.15
  297.1 1.2 collective-permute-done.18
  298.9 11.5 %collective-permute-done.19 = f32[512]{0:T(512)S(1)} collective-permute-done((f32[512]{0:T(512)S(1)}, f32[512]{0:T(512)S(1)}, u32[]{:S(2)}, u32[]{:S(2)}) %collective-permute-start.19) | collective-permute-done | bytes 2080 | tf_op jit(solution)/shard_map/ppermute | solution.py:102
  310.4 2.7 collective-permute-start.20
  313.1 1.2 bitcast_add_fusion.2
  314.3 1.0 copy-done.7
  315.3 6.9 %collective-permute-start.17 = (bf16[512,256]{1,0:T(8,128)(2,1)S(1)}, bf16[512,256]{1,0:T(8,128)(2,1)S(1)}, u32[]{:S(2)}, u32[]{:S(2)}) collective-permute-start(bf16[512,256]{1,0:T(8,128)(2,1)S(1)} %fusion.11), channel_id=1, source_target_pairs={{0,32},{16,48},{32,0},{48,16},{64,96},{80,112},{96,64},{112,80},{1... | collective-permute-start | bytes 786440 | tf_op jit(solution)/shard_map/ppermute | solution.py:132
  322.9 27.7 %scatter_custom_fusion = f32[8016]{0:T(1024)} fusion(s32[4096]{0:T(1024)S(1)} %bitcast.56, f32[4096]{0:T(1024)S(1)} %bitcast.57, f32[]{:T(128)} %constant.95.clone.1), kind=kCustom, calls=%fused_computation.49 | custom fusion | flops 4096 | bytes 32068 | tf_op jit(solution)/shard_map/scatter-add | solution.py:109
  351.2 1.1 bitcast_add_fusion.3
  352.3 11.8 %reduce-scatter.5.cloned.1.call-done = bf16[512,256]{1,0:T(8,128)(2,1)} async-done(((bf16[8192,256]{1,0:T(8,128)(2,1)}), bf16[512,256]{1,0:T(8,128)(2,1)}) %reduce-scatter.5.cloned.1.call-update) | async-done | bytes 262160 | tf_op jit(solution)/shard_map/reduce_scatter | solution.py:122
  364.1 1.0 convert_element_type.116
  365.1 1.1 pad_maximum_fusion.3
  (89 shorter events, 6.9 us)
Async XLA Ops:
  7.2 136.2 %copy-start = (f32[128256]{0:T(1024)S(1)}, f32[128256]{0:T(1024)}, u32[]{:S(2)}) copy-start(f32[128256]{0:T(1024)} %param.17) | copy-start | bytes 1539076
  7.2 1.0 copy-start.9
  7.2 1.1 copy-start.11
  7.2 60.1 %reduce-scatter.3.cloned.1.call-start = ((), (), s32[]{:S(2)}) async-start(), calls=%async_computation.2 | async-start | bytes 5242880 | tf_op jit(solution)/shard_map/reduce_scatter | solution.py:51
  16.1 1.0 copy-start.5
  16.1 176.8 %all-gather.2.cloned.1.call-start = ((), (), s32[]{:S(2)}) async-start(), calls=%async_computation.3 | async-start | bytes 5242880 | tf_op jit(solution)/shard_map/all_gather | solution.py:56
  17.1 21.4 %collective-permute-start.2 = (bf16[1,512,512]{2,1,0:T(8,128)(2,1)S(1)}, bf16[1,512,512]{2,1,0:T(8,128)(2,1)S(1)}, u32[]{:S(2)}, u32[]{:S(2)}) collective-permute-start(bf16[1,512,512]{2,1,0:T(8,128)(2,1)S(1)} %bitcast.49), channel_id=1, source_target_pairs={{0,32},{16,48},{32,0},{48,16},{64,96},{80,112},{96,64},{112,80},{1... | collective-permute-start | bytes 1572872 | tf_op jit(solution)/shard_map/ppermute | solution.py:38
  39.5 29.4 %collective-permute-start.3 = (bf16[2,512,512]{2,1,0:T(8,128)(2,1)}, bf16[2,512,512]{2,1,0:T(8,128)(2,1)S(1)}, u32[]{:S(2)}, u32[]{:S(2)}) collective-permute-start(bf16[2,512,512]{2,1,0:T(8,128)(2,1)} %pad_maximum_fusion.2), channel_id=1, source_target_pairs={{0,64},{16,80},{32,96},{48,112},{64,0},{80,16},{96,32},{112,48},{1... | collective-permute-start | bytes 3145736 | tf_op jit(solution)/shard_map/ppermute | solution.py:38
  67.3 25.1 %copy-start.8 = (bf16[256,2048]{1,0:T(8,128)(2,1)S(1)}, bf16[256,2048]{1,0:T(8,128)(2,1)}, u32[]{:S(2)}) copy-start(bf16[256,2048]{1,0:T(8,128)(2,1)} %reduce-scatter.3.cloned.1.call-done) | copy-start | bytes 3145732
  67.3 25.1 %collective-permute-start = (bf16[256,2048]{1,0:T(8,128)(2,1)}, bf16[256,2048]{1,0:T(8,128)(2,1)S(1)}, u32[]{:S(2)}, u32[]{:S(2)}) collective-permute-start(bf16[256,2048]{1,0:T(8,128)(2,1)} %reduce-scatter.3.cloned.1.call-done), channel_id=1, source_target_pairs={{0,4},{4,0},{8,12},{12,8},{1,5},{5,1},{9,13},{13,9},{2,6},{6,2},{1... | collective-permute-start | bytes 3145736 | tf_op jit(solution)/shard_map/ppermute | solution.py:54
  69.1 48.6 %collective-permute-start.4 = (bf16[4,512,512]{2,1,0:T(8,128)(2,1)S(1)}, bf16[4,512,512]{2,1,0:T(8,128)(2,1)S(1)}, u32[]{:S(2)}, u32[]{:S(2)}) collective-permute-start(bf16[4,512,512]{2,1,0:T(8,128)(2,1)S(1)} %pad_maximum_fusion.1), channel_id=1, source_target_pairs={{0,128},{16,144},{32,160},{48,176},{64,192},{80,208},{96,224},{112... | collective-permute-start | bytes 6291464 | tf_op jit(solution)/shard_map/ppermute | solution.py:38
  92.8 47.4 %collective-permute-start.1 = (bf16[256,2048]{1,0:T(8,128)(2,1)S(1)}, bf16[256,2048]{1,0:T(8,128)(2,1)S(1)}, u32[]{:S(2)}, u32[]{:S(2)}) collective-permute-start(bf16[256,2048]{1,0:T(8,128)(2,1)S(1)} %add_convert_fusion.1), channel_id=1, source_target_pairs={{0,8},{4,12},{8,0},{12,4},{1,9},{5,13},{9,1},{13,5},{2,10},{6,14},... | collective-permute-start | bytes 3145736 | tf_op jit(solution)/shard_map/ppermute | solution.py:54
  117.7 1.3 copy-start.3
  121.3 22.0 %copy-start.10 = (s32[256]{0:T(256)S(1)}, s32[256]{0:T(256)}, u32[]{:S(2)}) copy-start(s32[256]{0:T(256)} %param.10) | copy-start | bytes 3076
  121.3 28.1 %collective-permute-start.5 = (bf16[8,512,512]{2,1,0:T(8,128)(2,1)}, bf16[8,512,512]{2,1,0:T(8,128)(2,1)}, u32[]{:S(2)}, u32[]{:S(2)}) collective-permute-start(bf16[8,512,512]{2,1,0:T(8,128)(2,1)} %pad_maximum_fusion), channel_id=1, source_target_pairs={{0,16},{16,0},{32,48},{48,32},{64,80},{80,64},{96,112},{112,96},{1... | collective-permute-start | bytes 12582920 | tf_op jit(solution)/shard_map/ppermute | solution.py:38
  141.6 222.4 %reduce-scatter.5.cloned.1.call-start = ((), (), s32[]{:S(2)}) async-start(), calls=%async_computation.4 | async-start | bytes 4456448 | tf_op jit(solution)/shard_map/reduce_scatter | solution.py:122
  145.1 2.8 copy-start.4
  162.7 33.5 %copy-start.12 = (f32[8192]{0:T(1024)S(1)}, f32[8192]{0:T(1024)}, u32[]{:S(2)}) copy-start(f32[8192]{0:T(1024)} %param.14) | copy-start | bytes 98308
  192.9 3.4 copy-start.6
  196.3 5.9 %copy-start.13 = (f32[512]{0:T(512)S(1)}, f32[512]{0:T(512)}, u32[]{:S(2)}) copy-start(f32[512]{0:T(512)} %param.16) | copy-start | bytes 6148
  202.2 44.0 %copy-start.14 = (f32[256,512]{1,0:T(8,128)}, f32[256,512]{1,0:T(8,128)S(1)}, u32[]{:S(2)}) copy-start(f32[256,512]{1,0:T(8,128)S(1)} %fusion.6) | copy-start | bytes 1572868
  203.0 4.0 %collective-permute-start.6 = (f32[16,514]{1,0:T(8,128)S(1)}, f32[16,514]{1,0:T(8,128)S(1)}, u32[]{:S(2)}, u32[]{:S(2)}) collective-permute-start(f32[16,514]{1,0:T(8,128)S(1)} %broadcast_multiply_fusion), channel_id=1, source_target_pairs={{0,1},{1,0},{2,3},{3,2},{4,5},{5,4},{6,7},{7,6},{8,9},{9,8},{10,11... | collective-permute-start | bytes 98696 | tf_op jit(solution)/shard_map/ppermute | solution.py:77
  207.1 5.5 %collective-permute-start.7 = (f32[16,514]{1,0:T(8,128)S(1)}, f32[16,514]{1,0:T(8,128)S(1)}, u32[]{:S(2)}, u32[]{:S(2)}) collective-permute-start(f32[16,514]{1,0:T(8,128)S(1)} %fusion.26), channel_id=1, source_target_pairs={{0,2},{1,3},{2,0},{3,1},{4,6},{5,7},{6,4},{7,5},{8,10},{9,11},{10,... | collective-permute-start | bytes 98696 | tf_op jit(solution)/shard_map/ppermute | solution.py:77
  212.7 4.5 %collective-permute-start.8 = (f32[16,514]{1,0:T(8,128)S(1)}, f32[16,514]{1,0:T(8,128)S(1)}, u32[]{:S(2)}, u32[]{:S(2)}) collective-permute-start(f32[16,514]{1,0:T(8,128)S(1)} %fusion.37), channel_id=1, source_target_pairs={{0,4},{1,5},{2,6},{3,7},{4,0},{5,1},{6,2},{7,3},{8,12},{9,13},{10,... | collective-permute-start | bytes 98696 | tf_op jit(solution)/shard_map/ppermute | solution.py:77
  217.2 4.9 %collective-permute-start.9 = (f32[16,514]{1,0:T(8,128)S(1)}, f32[16,514]{1,0:T(8,128)S(1)}, u32[]{:S(2)}, u32[]{:S(2)}) collective-permute-start(f32[16,514]{1,0:T(8,128)S(1)} %add.174), channel_id=1, source_target_pairs={{0,8},{1,9},{2,10},{3,11},{4,12},{5,13},{6,14},{7,15},{8,0},{9,1},... | collective-permute-start | bytes 98696 | tf_op jit(solution)/shard_map/ppermute | solution.py:77
  222.1 1.2 collective-permute-start.10
  223.3 4.0 %collective-permute-start.11 = (f32[16,514]{1,0:T(8,128)S(1)}, f32[16,514]{1,0:T(8,128)S(1)}, u32[]{:S(2)}, u32[]{:S(2)}) collective-permute-start(f32[16,514]{1,0:T(8,128)S(1)} %add.176), channel_id=1, source_target_pairs={{0,64},{16,80},{32,96},{48,112},{64,0},{80,16},{96,32},{112,48},{1... | collective-permute-start | bytes 98696 | tf_op jit(solution)/shard_map/ppermute | solution.py:81
  227.3 5.5 %collective-permute-start.12 = (f32[16,514]{1,0:T(8,128)S(1)}, f32[16,514]{1,0:T(8,128)S(1)}, u32[]{:S(2)}, u32[]{:S(2)}) collective-permute-start(f32[16,514]{1,0:T(8,128)S(1)} %add.177), channel_id=1, source_target_pairs={{0,128},{16,144},{32,160},{48,176},{64,192},{80,208},{96,224},{112... | collective-permute-start | bytes 98696 | tf_op jit(solution)/shard_map/ppermute | solution.py:81
  232.8 8.0 %collective-permute-start.13 = (f32[16,514]{1,0:T(8,128)S(1)}, f32[16,514]{1,0:T(8,128)S(1)}, u32[]{:S(2)}, u32[]{:S(2)}) collective-permute-start(f32[16,514]{1,0:T(8,128)S(1)} %add.178), channel_id=1, source_target_pairs={{0,32},{16,48},{32,0},{48,16},{64,96},{80,112},{96,64},{112,80},{1... | collective-permute-start | bytes 98696 | tf_op jit(solution)/shard_map/ppermute | solution.py:81
  255.1 4.4 %collective-permute-start.14 = (bf16[2,2,2,512,256]{4,3,2,0,1:T(8,128)(2,1)S(1)}, bf16[2,2,2,512,256]{4,3,2,0,1:T(8,128)(2,1)}, u32[]{:S(2)}, u32[]{:S(2)}) collective-permute-start(bf16[2,2,2,512,256]{4,3,2,0,1:T(8,128)(2,1)S(1)} %fusion.4), channel_id=1, source_target_pairs={{0,16},{16,0},{32,48},{48,32},{64,80},{80,64},{96,112},{112,96},{1... | collective-permute-start | bytes 6291464 | tf_op jit(solution)/shard_map/ppermute | solution.py:132
  262.7 1.9 copy-start.2
  264.8 25.4 %collective-permute-start.15 = (bf16[2,2,512,256]{3,2,1,0:T(8,128)(2,1)S(1)}, bf16[2,2,512,256]{3,2,1,0:T(8,128)(2,1)}, u32[]{:S(2)}, u32[]{:S(2)}) collective-permute-start(bf16[2,2,512,256]{3,2,1,0:T(8,128)(2,1)S(1)} %fusion.8), channel_id=1, source_target_pairs={{0,64},{16,80},{32,96},{48,112},{64,0},{80,16},{96,32},{112,48},{1... | collective-permute-start | bytes 3145736 | tf_op jit(solution)/shard_map/ppermute | solution.py:132
  292.4 20.6 %collective-permute-start.16 = (bf16[2,512,256]{2,1,0:T(8,128)(2,1)S(1)}, bf16[2,512,256]{2,1,0:T(8,128)(2,1)}, u32[]{:S(2)}, u32[]{:S(2)}) collective-permute-start(bf16[2,512,256]{2,1,0:T(8,128)(2,1)S(1)} %fusion.9), channel_id=1, source_target_pairs={{0,128},{16,144},{32,160},{48,176},{64,192},{80,208},{96,224},{112... | collective-permute-start | bytes 1572872 | tf_op jit(solution)/shard_map/ppermute | solution.py:132
  295.5 70.6 %copy-start.1 = (f32[128256]{0:T(1024)S(1)}, f32[128256]{0:T(1024)}, u32[]{:S(2)}) copy-start(f32[128256]{0:T(1024)} %param.17) | copy-start | bytes 1539076
  297.1 1.2 collective-permute-start.18
  298.3 12.1 %collective-permute-start.19 = (f32[512]{0:T(512)S(1)}, f32[512]{0:T(512)S(1)}, u32[]{:S(2)}, u32[]{:S(2)}) collective-permute-start(f32[512]{0:T(512)S(1)} %add.194), channel_id=1, source_target_pairs={{0,64},{16,80},{32,96},{48,112},{64,0},{80,16},{96,32},{112,48},{1... | collective-permute-start | bytes 6152 | tf_op jit(solution)/shard_map/ppermute | solution.py:102
  310.4 11.8 %collective-permute-start.20 = (f32[512]{0:T(512)S(1)}, f32[512]{0:T(512)S(1)}, u32[]{:S(2)}, u32[]{:S(2)}) collective-permute-start(f32[512]{0:T(512)S(1)} %add.195), channel_id=1, source_target_pairs={{0,128},{16,144},{32,160},{48,176},{64,192},{80,208},{96,224},{112... | collective-permute-start | bytes 6152 | tf_op jit(solution)/shard_map/ppermute | solution.py:102
  314.3 1.0 copy-start.7
  315.3 35.9 %collective-permute-start.17 = (bf16[512,256]{1,0:T(8,128)(2,1)S(1)}, bf16[512,256]{1,0:T(8,128)(2,1)S(1)}, u32[]{:S(2)}, u32[]{:S(2)}) collective-permute-start(bf16[512,256]{1,0:T(8,128)(2,1)S(1)} %fusion.11), channel_id=1, source_target_pairs={{0,32},{16,48},{32,0},{48,16},{64,96},{80,112},{96,64},{112,80},{1... | collective-permute-start | bytes 786440 | tf_op jit(solution)/shard_map/ppermute | solution.py:132
  322.2 28.4 %collective-permute-start.21 = (f32[512]{0:T(512)S(1)}, f32[512]{0:T(512)S(1)}, u32[]{:S(2)}, u32[]{:S(2)}) collective-permute-start(f32[512]{0:T(512)S(1)} %add.196), channel_id=1, source_target_pairs={{0,32},{16,48},{32,0},{48,16},{64,96},{80,112},{96,64},{112,80},{1... | collective-permute-start | bytes 6152 | tf_op jit(solution)/shard_map/ppermute | solution.py:102
Sparse Core Ops, SparseCore 0:
  16.2 51.0 reduce-scatter.2
  141.7 51.0 all-gather.1
  252.8 111.2 reduce-scatter.4

commit v10 on v8

--- a/solution.py
+++ b/solution.py
@@ -115,10 +115,10 @@
     grad_part = lax.dot_general(
         normed, d_pre, contract, preferred_element_type=jnp.float32
     ).astype(jnp.bfloat16)
-    cols = grad_part.shape[1] // 2
+    cols = grad_part.shape[1] * 3 // 8
     native = lax.psum_scatter(grad_part[:, :cols], "dp", scatter_dimension=0, tiled=True)
     n_bits = n_dp.bit_length() - 1
-    acc = grad_part[:, cols:].astype(jnp.float32).reshape((2,) * n_bits + (-1, cols))
+    acc = grad_part[:, cols:].astype(jnp.float32).reshape((2,) * n_bits + (-1, grad_part.shape[1] - cols))
     left = list(range(n_bits - 1, -1, -1))
     for b in (0, 2, 3, 1):
         axis = left.index(b)

time: 371 us -> 406 us (1.094)
  local copies, waits for them, and re-layouts: 31.5 us -> 67.9 us
    dynamic_slice x0 -> x2, local copies, waits for them, and re-layouts: none -> 14.8 us  [the longest x1 7.41 us: local(): keep = lax.dynamic_index_in_dim(acc, mine, axis=axis, keepdims=False)]
    reshape x0 -> x1, local copies, waits for them, and re-layouts: none -> 14.3 us  [local(): grad_part[:, cols:].astype(jnp.float32)]
    reduce_scatter x1, waiting for transfers between devices: 11.3 us -> 0.01 us  [local(): lax.psum_scatter(grad_part[:, :cols], 'dp', scatter_dimension=0, tiled=True)]
    unnamed x32 -> x30, local copies, waits for them, and re-layouts: 10.6 us -> 16.7 us
  transfers between devices with their start and end apart: 24 -> 24, of which waited for: 18 -> 17; matrix products, arithmetic and copies ran while one was open for 20% -> 21% of each run, Pallas kernels for 0% -> 0%
where the time goes in v10:
time: 406 us; the launch traced here: 405 us
  waiting for transfers between devices  196 us (48%)
  local copies, waits for them, and re-layouts  67.9 us (17%)
  other arithmetic  61.5 us (15%)
  starting transfers between devices  42.5 us (10%)
  matrix products  22 us (5%)
  between operations  15.5 us (4%)
    ppermute x4, waiting for transfers between devices, local(): got = lax.ppermute(stack, 'dp', [(i, i ^ 1 << b) for i in range(n_dp)])  80.6 us
    ppermute x4, waiting for transfers between devices, local(): lax.ppermute(send.astype(jnp.bfloat16), 'dp', [(i, i ^ 1 << b) for i in r...  31.9 us
    scatter-add x1, other arithmetic, local(): jnp.zeros((slice_len,), jnp.float32).at[idx]  28.3 us
    psum x1, waiting for transfers between devices, local(): part = lax.psum(part, 'tz')  24.1 us
    all_gather x1, waiting for transfers between devices, local(): hidden = lax.all_gather(part, 'tx', axis=1, tiled=True)  21.1 us
    unnamed x30, local copies, waits for them, and re-layouts  16.7 us
    ppermute x4, waiting for transfers between devices, local(): lax.ppermute(grad_out, 'dp', [(i, i ^ 1 << b) for i in range(n_dp)])  16.2 us
    reshape x1, local copies, waits for them, and re-layouts, local(): grad_part[:, cols:].astype(jnp.float32)  14.3 us
  transfers between devices with their start and end apart: 24, of which 17 were waited for; matrix products, arithmetic and copies ran while one was open for 21% of the time, Pallas kernels for 0%

profile of v10, /device:TPU:2, one launch (start us, length us, event | category | flops | bytes accessed | tf_op | source)
XLA Modules:
  0.0 405.3 jit_solution(10106437432283336955)
XLA Ops:
  7.7 1.0 constant_dynamic-update-slice_fusion.5
  8.7 8.0 %fusion = bf16[256,8192]{1,0:T(8,128)(2,1)} fusion(bf16[256,512]{1,0:T(8,128)(2,1)} %param.11, bf16[512,8192]{1,0:T(8,128)(2,1)} %param.12, bf16[256,8192]{1,0:T(8,128)(2,1)S(1)} %constant_dynamic-update-slice_fusion.5), kind=kOutput, calls=%fused_computation.7 | convolution fusion | flops 2153775104 | bytes 17039360 | tf_op jit(solution)/shard_map/dot_general | solution.py:49
  16.7 7.3 %collective-permute-start = (bf16[1,512,512]{2,1,0:T(8,128)(2,1)S(1)}, bf16[1,512,512]{2,1,0:T(8,128)(2,1)S(1)}, u32[]{:S(2)}, u32[]{:S(2)}) collective-permute-start(bf16[1,512,512]{2,1,0:T(8,128)(2,1)S(1)} %bitcast.49), channel_id=1, source_target_pairs={{0,32},{16,48},{32,0},{48,16},{64,96},{80,112},{96,64},{112,80},{1... | collective-permute-start | bytes 1572872 | tf_op jit(solution)/shard_map/ppermute | solution.py:38
  24.0 14.2 %collective-permute-done = bf16[1,512,512]{2,1,0:T(8,128)(2,1)S(1)} collective-permute-done((bf16[1,512,512]{2,1,0:T(8,128)(2,1)S(1)}, bf16[1,512,512]{2,1,0:T(8,128)(2,1)S(1)}, u32[]{:S(2)}, u32[]{:S(2)}) %collective-permute-start) | collective-permute-done | bytes 524320 | tf_op jit(solution)/shard_map/ppermute | solution.py:38
  38.3 1.7 collective-permute-start.1
  40.0 22.6 %collective-permute-done.1 = bf16[2,512,512]{2,1,0:T(8,128)(2,1)S(1)} collective-permute-done((bf16[2,512,512]{2,1,0:T(8,128)(2,1)S(1)}, bf16[2,512,512]{2,1,0:T(8,128)(2,1)S(1)}, u32[]{:S(2)}, u32[]{:S(2)}) %collective-permute-start.1) | collective-permute-done | bytes 1048608 | tf_op jit(solution)/shard_map/ppermute | solution.py:38
  62.6 1.6 pad_maximum_fusion.1
  64.1 3.2 collective-permute-start.2
  68.0 43.8 %collective-permute-done.2 = bf16[4,512,512]{2,1,0:T(8,128)(2,1)} collective-permute-done((bf16[4,512,512]{2,1,0:T(8,128)(2,1)}, bf16[4,512,512]{2,1,0:T(8,128)(2,1)}, u32[]{:S(2)}, u32[]{:S(2)}) %collective-permute-start.2) | collective-permute-done | bytes 2097184 | tf_op jit(solution)/shard_map/ppermute | solution.py:38
  111.8 3.4 pad_maximum_fusion
  115.3 24.1 %all-reduce.2.cloned.1.call-done = bf16[256,2048]{1,0:T(8,128)(2,1)} async-done(((bf16[256,2048]{1,0:T(8,128)(2,1)}), bf16[256,2048]{1,0:T(8,128)(2,1)}) %all-reduce.2.cloned.1.call-update) | async-done | bytes 1048592 | tf_op jit(solution)/shard_map/psum | solution.py:52
  140.9 1.7 gather_fusion.1
  142.7 0.9 constant_dynamic-update-slice_fusion.4
  143.5 0.9 constant_dynamic-update-slice_fusion.3
  144.4 1.0 constant_dynamic-update-slice_fusion.2
  145.4 3.1 constant_dynamic-update-slice_fusion.1
  148.5 4.4 %constant_dynamic-update-slice_fusion = bf16[16,512,512]{2,1,0:T(8,128)(2,1)} fusion(bf16[16,512,512]{2,1,0:T(8,128)(2,1)} %constant_dynamic-update-slice_fusion.1, bf16[8,512,512]{2,1,0:T(8,128)(2,1)} %collective-permute-done.3), kind=kLoop, calls=%fused_computation.56 | loop fusion | bytes 8388608 | tf_op jit(solution)/shard_map/concatenate | solution.py:39
  152.9 8.7 %gather_fusion = bf16[16,512,512]{2,1,0:T(8,128)(2,1)} fusion(bf16[16,512,512]{2,1,0:T(8,128)(2,1)} %constant_dynamic-update-slice_fusion, s32[1024]{0:T(1024)S(1)} %pad_clamp_fusion.1), kind=kCustom, calls=%fused_computation | custom fusion | bytes 16777280 | tf_op jit(solution)/shard_map/jit(_take)/gather | solution.py:44
  161.6 7.5 %bitcast_select_fusion = bf16[8192,512]{1,0:T(8,128)(2,1)} fusion(bf16[16,512,512]{2,1,0:T(8,128)(2,1)} %gather_fusion, pred[8192]{0:T(1024)(128)(4,1)S(1)} %bitcast.56), kind=kLoop, calls=%fused_computation.11 | loop fusion | flops 4194304 | bytes 16785408 | tf_op jit(solution)/shard_map/jit(_take)/select_n | solution.py:44
  169.0 21.1 %all-gather.2.cloned.1.call-done = bf16[256,8192]{1,0:T(8,128)(2,1)} async-done(((bf16[256,2048]{1,0:T(8,128)(2,1)}), bf16[256,8192]{1,0:T(8,128)(2,1)}) %all-gather.2.cloned.1.call-update) | async-done | bytes 4194320 | tf_op jit(solution)/shard_map/all_gather | solution.py:53
  190.1 3.1 fusion.1
  193.3 7.0 %fusion.7 = f32[256,512]{1,0:T(8,128)S(1)} fusion(bf16[8192,512]{1,0:T(8,128)(2,1)} %bitcast_select_fusion, bf16[256,8192]{1,0:T(8,128)(2,1)} %all-gather.2.cloned.1.call-done, f32[8192]{0:T(1024)S(1)} %copy-done.7, f32[256]{0:T(256)S(1)} %add_rsqrt_fusion), kind=kOutput, calls=%fused_computation.23 | convolution fusion | flops 2155872256 | bytes 13140992 | tf_op jit(solution)/shard_map/dot_general | solution.py:56
  201.1 1.2 collective-permute-start.4
  202.3 2.8 collective-permute-done.4
  205.2 1.2 collective-permute-start.5
  206.3 4.6 %collective-permute-done.5 = f32[16,514]{1,0:T(8,128)S(1)} collective-permute-done((f32[16,514]{1,0:T(8,128)S(1)}, f32[16,514]{1,0:T(8,128)S(1)}, u32[]{:S(2)}, u32[]{:S(2)}) %collective-permute-start.5) | collective-permute-done | bytes 32928 | tf_op jit(solution)/shard_map/ppermute | solution.py:74
  211.0 1.6 collective-permute-start.6
  212.6 2.9 collective-permute-done.6
  215.5 2.1 collective-permute-start.7
  217.6 2.8 collective-permute-done.7
  220.4 1.2 collective-permute-done.8
  221.6 1.5 collective-permute-start.9
  223.1 2.5 collective-permute-done.9
  225.6 3.0 collective-permute-start.10
  228.6 2.5 collective-permute-done.10
  231.1 5.8 %collective-permute-start.11 = (f32[16,514]{1,0:T(8,128)S(1)}, f32[16,514]{1,0:T(8,128)S(1)}, u32[]{:S(2)}, u32[]{:S(2)}) collective-permute-start(f32[16,514]{1,0:T(8,128)S(1)} %add.172), channel_id=1, source_target_pairs={{0,32},{16,48},{32,0},{48,16},{64,96},{80,112},{96,64},{112,80},{1... | collective-permute-start | bytes 98696 | tf_op jit(solution)/shard_map/ppermute | solution.py:78
  237.0 2.2 collective-permute-done.11
  239.6 4.9 %convolution_convert_fusion = bf16[8192,512]{0,1:T(8,128)(2,1)S(1)} fusion(bf16[256,8192]{1,0:T(8,128)(2,1)} %all-gather.2.cloned.1.call-done, f32[8192]{0:T(1024)S(1)} %copy-done.7, f32[256]{0:T(256)S(1)} %add_rsqrt_fusion, f32[256,512]{1,0:T(8,128)S(1)} %fusion.7, f32[512]{0:T(512)S(1)} %copy-done.8, f32[256]{0:T(256)S(1)} %bitcast.61), kind=kOutput, calls=%fused_computation.3 | convolution fusion | flops 2161377280 | bytes 13144064 | tf_op jit(solution)/shard_map/dot_general | solution.py:115
  244.5 3.3 copy-done.3
  247.8 5.1 %slice_convert_fusion = f32[8192,320]{0,1:T(8,128)} fusion(bf16[8192,512]{0,1:T(8,128)(2,1)S(1)} %convolution_convert_fusion), kind=kLoop, calls=%fused_computation.12 | loop fusion | flops 2621440 | bytes 15728640 | tf_op jit(solution)/shard_map/reshape | solution.py:121
  252.9 14.3 %reshape.153 = f32[2,2,2,2,512,320]{4,3,2,1,0,5:T(2,128)} reshape(f32[8192,320]{0,1:T(8,128)} %slice_convert_fusion) | data formatting | bytes 20971520 | tf_op jit(solution)/shard_map/reshape | solution.py:121
  267.2 7.4 %constant_dynamic-slice_fusion = bf16[2,2,2,1,512,320]{4,3,2,1,0,5:T(2,128)(2,1)S(1)} fusion(f32[2,2,2,2,512,320]{4,3,2,1,0,5:T(2,128)} %reshape.153, s32[]{:T(128)S(6)} %select_n.101), kind=kLoop, calls=%fused_computation.69 | loop fusion | bytes 5242884 | tf_op jit(solution)/shard_map/jit(dynamic_index_in_dim)/dynamic_slice | solution.py:128
  274.6 2.8 copy.34
  277.7 4.0 slice.31
  281.7 7.4 %constant_dynamic-slice_fusion.1 = f32[2,2,2,1,512,320]{4,3,2,1,0,5:T(1,128)S(1)} fusion(f32[2,2,2,2,512,320]{4,3,2,1,0,5:T(2,128)} %reshape.153, s32[]{:T(128)S(6)} %select_n.100), kind=kLoop, calls=%fused_computation.70 | loop fusion | bytes 10485764 | tf_op jit(solution)/shard_map/jit(dynamic_index_in_dim)/dynamic_slice | solution.py:127
  289.1 4.9 %bitcast_add_fusion = f32[2,2,2,512,320]{3,4,2,1,0:T(8,128)S(1)} fusion(f32[2,2,2,1,512,320]{4,3,2,1,0,5:T(1,128)S(1)} %constant_dynamic-slice_fusion.1, bf16[2,2,2,512,320]{3,4,2,1,0:T(8,128)(2,1)} %collective-permute-done.12), kind=kLoop, calls=%fused_computation.14 | loop fusion | flops 2621440 | bytes 13107200 | tf_op jit(solution)/shard_map/add | solution.py:132
  294.1 2.3 copy-done.2
  296.5 1.6 collective-permute-start.13
  298.1 31.9 %collective-permute-done.13 = bf16[2,2,512,320]{2,3,1,0:T(8,128)(2,1)} collective-permute-done((bf16[2,2,512,320]{2,3,1,0:T(8,128)(2,1)S(1)}, bf16[2,2,512,320]{2,3,1,0:T(8,128)(2,1)}, u32[]{:S(2)}, u32[]{:S(2)}) %collective-permute-start.13) | collective-permute-done | bytes 1310752 | tf_op jit(solution)/shard_map/ppermute | solution.py:129
  330.0 2.7 bitcast_add_fusion.1
  332.7 0.9 fusion.9
  333.6 3.0 collective-permute-start.14
  336.6 1.5 fusion.15
  338.2 1.2 collective-permute-done.16
  339.9 15.1 %collective-permute-done.17 = f32[512]{0:T(512)S(1)} collective-permute-done((f32[512]{0:T(512)S(1)}, f32[512]{0:T(512)S(1)}, u32[]{:S(2)}, u32[]{:S(2)}) %collective-permute-start.17) | collective-permute-done | bytes 2080 | tf_op jit(solution)/shard_map/ppermute | solution.py:99
  355.0 2.2 collective-permute-start.18
  357.2 1.3 bitcast_add_fusion.2
  358.5 1.1 copy-done.5
  359.6 5.0 %collective-permute-start.15 = (bf16[512,320]{0,1:T(8,128)(2,1)S(1)}, bf16[512,320]{0,1:T(8,128)(2,1)S(1)}, u32[]{:S(2)}, u32[]{:S(2)}) collective-permute-start(bf16[512,320]{0,1:T(8,128)(2,1)S(1)} %fusion.11), channel_id=1, source_target_pairs={{0,32},{16,48},{32,0},{48,16},{64,96},{80,112},{96,64},{112,80},{1... | collective-permute-start | bytes 983048 | tf_op jit(solution)/shard_map/ppermute | solution.py:129
  364.6 1.1 collective-permute-start.19
  366.4 28.3 %scatter_custom_fusion = f32[8016]{0:T(1024)} fusion(s32[4096]{0:T(1024)S(1)} %bitcast.57, f32[4096]{0:T(1024)S(1)} %bitcast.58, f32[]{:T(128)} %constant.95.clone.1), kind=kCustom, calls=%fused_computation.48 | custom fusion | flops 4096 | bytes 32068 | tf_op jit(solution)/shard_map/scatter-add | solution.py:106
  395.2 1.0 convert_element_type.92
  396.2 1.2 bitcast_add_fusion.3
  397.5 1.3 copy.25
  (80 shorter events, 5.5 us)
Async XLA Ops:
  7.2 133.7 %copy-start = (f32[128256]{0:T(1024)S(1)}, f32[128256]{0:T(1024)}, u32[]{:S(2)}) copy-start(f32[128256]{0:T(1024)} %param.17) | copy-start | bytes 1539076
  7.2 60.8 %reduce-scatter.3.cloned.1.call-start = ((), (), s32[]{:S(2)}) async-start(), calls=%async_computation.2 | async-start | bytes 5242880 | tf_op jit(solution)/shard_map/reduce_scatter | solution.py:51
  8.7 8.1 %copy-start.4 = (bf16[512,512]{1,0:T(8,128)(2,1)S(1)}, bf16[512,512]{1,0:T(8,128)(2,1)}, u32[]{:S(2)}) copy-start(bf16[512,512]{1,0:T(8,128)(2,1)} %param.15) | copy-start | bytes 1572868
  16.7 122.7 %all-reduce.2.cloned.1.call-start = ((), (), s32[]{:S(2)}) async-start(), calls=%async_computation.3 | async-start | bytes 2097152 | tf_op jit(solution)/shard_map/psum | solution.py:52
  16.7 21.5 %collective-permute-start = (bf16[1,512,512]{2,1,0:T(8,128)(2,1)S(1)}, bf16[1,512,512]{2,1,0:T(8,128)(2,1)S(1)}, u32[]{:S(2)}, u32[]{:S(2)}) collective-permute-start(bf16[1,512,512]{2,1,0:T(8,128)(2,1)S(1)} %bitcast.49), channel_id=1, source_target_pairs={{0,32},{16,48},{32,0},{48,16},{64,96},{80,112},{96,64},{112,80},{1... | collective-permute-start | bytes 1572872 | tf_op jit(solution)/shard_map/ppermute | solution.py:38
  38.3 24.3 %collective-permute-start.1 = (bf16[2,512,512]{2,1,0:T(8,128)(2,1)S(1)}, bf16[2,512,512]{2,1,0:T(8,128)(2,1)S(1)}, u32[]{:S(2)}, u32[]{:S(2)}) collective-permute-start(bf16[2,512,512]{2,1,0:T(8,128)(2,1)S(1)} %pad_maximum_fusion.2), channel_id=1, source_target_pairs={{0,64},{16,80},{32,96},{48,112},{64,0},{80,16},{96,32},{112,48},{1... | collective-permute-start | bytes 3145736 | tf_op jit(solution)/shard_map/ppermute | solution.py:38
  64.1 47.7 %collective-permute-start.2 = (bf16[4,512,512]{2,1,0:T(8,128)(2,1)}, bf16[4,512,512]{2,1,0:T(8,128)(2,1)}, u32[]{:S(2)}, u32[]{:S(2)}) collective-permute-start(bf16[4,512,512]{2,1,0:T(8,128)(2,1)} %pad_maximum_fusion.1), channel_id=1, source_target_pairs={{0,128},{16,144},{32,160},{48,176},{64,192},{80,208},{96,224},{112... | collective-permute-start | bytes 6291464 | tf_op jit(solution)/shard_map/ppermute | solution.py:38
  67.9 72.9 %copy-start.6 = (s32[256]{0:T(256)S(1)}, s32[256]{0:T(256)}, u32[]{:S(2)}) copy-start(s32[256]{0:T(256)} %param.10) | copy-start | bytes 3076
  68.0 122.2 %all-gather.2.cloned.1.call-start = ((), (), s32[]{:S(2)}) async-start(), calls=%async_computation.4 | async-start | bytes 5242880 | tf_op jit(solution)/shard_map/all_gather | solution.py:53
  115.3 33.2 %collective-permute-start.3 = (bf16[8,512,512]{2,1,0:T(8,128)(2,1)}, bf16[8,512,512]{2,1,0:T(8,128)(2,1)}, u32[]{:S(2)}, u32[]{:S(2)}) collective-permute-start(bf16[8,512,512]{2,1,0:T(8,128)(2,1)} %pad_maximum_fusion), channel_id=1, source_target_pairs={{0,16},{16,0},{32,48},{48,32},{64,80},{80,64},{96,112},{112,96},{1... | collective-permute-start | bytes 12582920 | tf_op jit(solution)/shard_map/ppermute | solution.py:38
  139.4 255.8 %reduce-scatter.5.cloned.1.call-start = ((), (), s32[]{:S(2)}) async-start(), calls=%async_computation.5 | async-start | bytes 3342336 | tf_op jit(solution)/shard_map/reduce_scatter | solution.py:119
  161.6 31.7 %copy-start.7 = (f32[8192]{0:T(1024)S(1)}, f32[8192]{0:T(1024)}, u32[]{:S(2)}) copy-start(f32[8192]{0:T(1024)} %param.14) | copy-start | bytes 98308
  193.2 7.1 %copy-start.8 = (f32[512]{0:T(512)S(1)}, f32[512]{0:T(512)}, u32[]{:S(2)}) copy-start(f32[512]{0:T(512)} %param.16) | copy-start | bytes 6148
  200.3 44.2 %copy-start.9 = (f32[256,512]{1,0:T(8,128)}, f32[256,512]{1,0:T(8,128)S(1)}, u32[]{:S(2)}) copy-start(f32[256,512]{1,0:T(8,128)S(1)} %fusion.7) | copy-start | bytes 1572868
  201.1 4.0 collective-permute-start.4
  205.2 5.7 %collective-permute-start.5 = (f32[16,514]{1,0:T(8,128)S(1)}, f32[16,514]{1,0:T(8,128)S(1)}, u32[]{:S(2)}, u32[]{:S(2)}) collective-permute-start(f32[16,514]{1,0:T(8,128)S(1)} %fusion.26), channel_id=1, source_target_pairs={{0,2},{1,3},{2,0},{3,1},{4,6},{5,7},{6,4},{7,5},{8,10},{9,11},{10,... | collective-permute-start | bytes 98696 | tf_op jit(solution)/shard_map/ppermute | solution.py:74
  211.0 4.5 %collective-permute-start.6 = (f32[16,514]{1,0:T(8,128)S(1)}, f32[16,514]{1,0:T(8,128)S(1)}, u32[]{:S(2)}, u32[]{:S(2)}) collective-permute-start(f32[16,514]{1,0:T(8,128)S(1)} %fusion.36), channel_id=1, source_target_pairs={{0,4},{1,5},{2,6},{3,7},{4,0},{5,1},{6,2},{7,3},{8,12},{9,13},{10,... | collective-permute-start | bytes 98696 | tf_op jit(solution)/shard_map/ppermute | solution.py:74
  215.5 4.9 %collective-permute-start.7 = (f32[16,514]{1,0:T(8,128)S(1)}, f32[16,514]{1,0:T(8,128)S(1)}, u32[]{:S(2)}, u32[]{:S(2)}) collective-permute-start(f32[16,514]{1,0:T(8,128)S(1)} %add.168), channel_id=1, source_target_pairs={{0,8},{1,9},{2,10},{3,11},{4,12},{5,13},{6,14},{7,15},{8,0},{9,1},... | collective-permute-start | bytes 98696 | tf_op jit(solution)/shard_map/ppermute | solution.py:74
  220.4 1.2 collective-permute-start.8
  221.6 4.0 collective-permute-start.9
  225.6 5.5 %collective-permute-start.10 = (f32[16,514]{1,0:T(8,128)S(1)}, f32[16,514]{1,0:T(8,128)S(1)}, u32[]{:S(2)}, u32[]{:S(2)}) collective-permute-start(f32[16,514]{1,0:T(8,128)S(1)} %add.171), channel_id=1, source_target_pairs={{0,128},{16,144},{32,160},{48,176},{64,192},{80,208},{96,224},{112... | collective-permute-start | bytes 98696 | tf_op jit(solution)/shard_map/ppermute | solution.py:78
  231.1 8.0 %collective-permute-start.11 = (f32[16,514]{1,0:T(8,128)S(1)}, f32[16,514]{1,0:T(8,128)S(1)}, u32[]{:S(2)}, u32[]{:S(2)}) collective-permute-start(f32[16,514]{1,0:T(8,128)S(1)} %add.172), channel_id=1, source_target_pairs={{0,32},{16,48},{32,0},{48,16},{64,96},{80,112},{96,64},{112,80},{1... | collective-permute-start | bytes 98696 | tf_op jit(solution)/shard_map/ppermute | solution.py:78
  244.5 3.3 copy-start.3
  277.4 11.7 %collective-permute-start.12 = (bf16[2,2,2,512,320]{3,4,2,1,0:T(8,128)(2,1)S(1)}, bf16[2,2,2,512,320]{3,4,2,1,0:T(8,128)(2,1)}, u32[]{:S(2)}, u32[]{:S(2)}) collective-permute-start(bf16[2,2,2,512,320]{3,4,2,1,0:T(8,128)(2,1)S(1)} %bitcast.53), channel_id=1, source_target_pairs={{0,16},{16,0},{32,48},{48,32},{64,80},{80,64},{96,112},{112,96},{1... | collective-permute-start | bytes 7864328 | tf_op jit(solution)/shard_map/ppermute | solution.py:129
  294.0 2.3 copy-start.2
  296.5 33.5 %collective-permute-start.13 = (bf16[2,2,512,320]{2,3,1,0:T(8,128)(2,1)S(1)}, bf16[2,2,512,320]{2,3,1,0:T(8,128)(2,1)}, u32[]{:S(2)}, u32[]{:S(2)}) collective-permute-start(bf16[2,2,512,320]{2,3,1,0:T(8,128)(2,1)S(1)} %fusion.5), channel_id=1, source_target_pairs={{0,64},{16,80},{32,96},{48,112},{64,0},{80,16},{96,32},{112,48},{1... | collective-permute-start | bytes 3932168 | tf_op jit(solution)/shard_map/ppermute | solution.py:129
  333.6 23.6 %collective-permute-start.14 = (bf16[2,512,320]{1,2,0:T(8,128)(2,1)}, bf16[2,512,320]{1,2,0:T(8,128)(2,1)}, u32[]{:S(2)}, u32[]{:S(2)}) collective-permute-start(bf16[2,512,320]{1,2,0:T(8,128)(2,1)} %fusion.9), channel_id=1, source_target_pairs={{0,128},{16,144},{32,160},{48,176},{64,192},{80,208},{96,224},{112... | collective-permute-start | bytes 1966088 | tf_op jit(solution)/shard_map/ppermute | solution.py:129
  338.2 1.2 collective-permute-start.16
  339.3 15.7 %collective-permute-start.17 = (f32[512]{0:T(512)S(1)}, f32[512]{0:T(512)S(1)}, u32[]{:S(2)}, u32[]{:S(2)}) collective-permute-start(f32[512]{0:T(512)S(1)} %add.188), channel_id=1, source_target_pairs={{0,64},{16,80},{32,96},{48,112},{64,0},{80,16},{96,32},{112,48},{1... | collective-permute-start | bytes 6152 | tf_op jit(solution)/shard_map/ppermute | solution.py:99
  355.0 43.8 %copy-start.1 = (f32[128256]{0:T(1024)S(1)}, f32[128256]{0:T(1024)}, u32[]{:S(2)}) copy-start(f32[128256]{0:T(1024)} %param.17) | copy-start | bytes 1539076
  355.0 9.6 %collective-permute-start.18 = (f32[512]{0:T(512)S(1)}, f32[512]{0:T(512)S(1)}, u32[]{:S(2)}, u32[]{:S(2)}) collective-permute-start(f32[512]{0:T(512)S(1)} %add.189), channel_id=1, source_target_pairs={{0,128},{16,144},{32,160},{48,176},{64,192},{80,208},{96,224},{112... | collective-permute-start | bytes 6152 | tf_op jit(solution)/shard_map/ppermute | solution.py:99
  358.5 1.1 copy-start.5
  359.6 36.6 %collective-permute-start.15 = (bf16[512,320]{0,1:T(8,128)(2,1)S(1)}, bf16[512,320]{0,1:T(8,128)(2,1)S(1)}, u32[]{:S(2)}, u32[]{:S(2)}) collective-permute-start(bf16[512,320]{0,1:T(8,128)(2,1)S(1)} %fusion.11), channel_id=1, source_target_pairs={{0,32},{16,48},{32,0},{48,16},{64,96},{80,112},{96,64},{112,80},{1... | collective-permute-start | bytes 983048 | tf_op jit(solution)/shard_map/ppermute | solution.py:129
  364.6 30.0 %collective-permute-start.19 = (f32[512]{0:T(512)S(1)}, f32[512]{0:T(512)S(1)}, u32[]{:S(2)}, u32[]{:S(2)}) collective-permute-start(f32[512]{0:T(512)S(1)} %add.190), channel_id=1, source_target_pairs={{0,32},{16,48},{32,0},{48,16},{64,96},{80,112},{96,64},{112,80},{1... | collective-permute-start | bytes 6152 | tf_op jit(solution)/shard_map/ppermute | solution.py:99
Sparse Core Ops, SparseCore 0:
  16.8 51.0 reduce-scatter.2
  70.6 68.7 all-reduce.1
  141.2 48.9 all-gather.1
  281.8 104.2 reduce-scatter.4
